TPU v7x, 256 devices: a whole 4x4x8 slice. The times are simulated.
256 devices in a mesh: run: 2 (over core), ctx: 32 (over x, z), head: 4 (over y).
Axes of the slice: x: 4, y: 4, z: 8, core: 2. Of those that a mesh axis runs over, the one named last changes fastest.
Arguments:
- inner_tokens: bfloat16 [131072, 5120], P(('run', 'ctx', 'head')), parts along dimension 0, may hold values from -6 to 6
- state_inputs: bfloat16 [131072, 256], P(('run', 'ctx', 'head')), parts along dimension 0, may hold values from -6 to 6
- step_raw: bfloat16 [131072, 80], P(('run', 'ctx', 'head')), parts along dimension 0, may hold values from -3 to 24
- conv_inner: float32 [5, 5120], P(None, 'head'), may hold values from -3 to 3
- conv_state: float32 [5, 256], replicated, may hold values from -3 to 3
- head_rates: float32 [4, 80], P('run', 'head'), parts along dimension 0, may hold values from -15 to 4
- skip_gain: float32 [80], P('head'), may hold values from 0.5 to 1.5
Outputs:
- mixed: bfloat16 [131072, 5120], P(('run', 'ctx', 'head')), parts along dimension 0
There are 2 independent parts, one for each index of `run`. A program takes and returns all parts, laid end to end along the dimension named above; an argument that names none is the same for every part. Nothing has to cross between parts.
All inputs are finite; a program needn't handle non-finite values.
Results may differ from a plain program's by a relative error of at most 0.009.
Values may be sent and summed in bfloat16 or wider, within the bound.
No kernel may reach another device: no remote copies, remote signals or barrier semaphores. Data moves between devices by JAX's collectives and lax.ppermute only.
A program may use at most 192 MiB of HBM per device.

v0:
```python
import jax
import jax.numpy as jnp
from jax import lax
from jax.sharding import PartitionSpec as P

KERNEL = 4
SPAN = 256


def from_behind(value, axis, by):
    length = lax.axis_size(axis)
    pairs = [(i, i + by) for i in range(length) if 0 <= i + by < length]
    return lax.ppermute(value, axis, pairs)


def silu_conv(signal, previous_rows, kernel_taps):
    length = signal.shape[0]
    channels = signal.shape[1]
    padded = jnp.concatenate(
        [previous_rows.astype(jnp.float32), signal.astype(jnp.float32)], axis=0
    )
    summed = jnp.zeros((length, channels), jnp.float32) + kernel_taps[KERNEL][None, :]
    for offset in range(KERNEL):
        summed = summed + kernel_taps[offset][None, :] * padded[offset : offset + length]
    return jax.nn.silu(summed).astype(jnp.bfloat16)


def block_terms(carry_state, pieces):
    c_block, b_block, u_block, decay_block = pieces
    cumulative = jnp.cumsum(decay_block, axis=0)
    across = cumulative.T
    inner_scores = jnp.dot(c_block, b_block.T, preferred_element_type=jnp.float32)
    spread = across[:, :, None] - across[:, None, :]
    places = jnp.arange(c_block.shape[0])
    causal = places[:, None] >= places[None, :]
    mixing = (inner_scores[None] * jnp.exp(jnp.where(causal[None], spread, -jnp.inf))).astype(
        jnp.bfloat16
    )
    local_terms = jnp.einsum("hts,shp->thp", mixing, u_block, preferred_element_type=jnp.float32)
    carried = jnp.exp(cumulative)[:, :, None] * jnp.einsum(
        "tn,hpn->thp", c_block.astype(jnp.float32), carry_state, precision=lax.Precision.HIGHEST
    )
    ending = cumulative[-1]
    weights = jnp.exp(ending[None, :] - cumulative)
    scaled = weights[:, :, None] * u_block.astype(jnp.float32)
    new_state = jnp.exp(ending)[:, None, None] * carry_state + jnp.einsum(
        "shp,sn->hpn", scaled, b_block.astype(jnp.float32), precision=lax.Precision.HIGHEST
    )
    return (new_state, local_terms + carried)


def per_device(inner_tokens, state_inputs, step_raw, conv_inner, conv_state, head_rates, skip_gain):
    x_local, step_local = (
        lax.all_to_all(inner_tokens, "head", split_axis=1, concat_axis=0, tiled=True),
        lax.all_to_all(step_raw, "head", split_axis=1, concat_axis=0, tiled=True),
    )
    context = x_local.shape[0]
    channels = x_local.shape[1]
    heads_local = head_rates.shape[1]
    head_width = channels // heads_local
    margin_rows = KERNEL - 1
    state_whole = lax.all_gather(state_inputs, "head", axis=0, tiled=True)
    edge_rows = jnp.concatenate(
        [x_local[context - margin_rows :], state_whole[context - margin_rows :]], axis=1
    )
    previous_rows = from_behind(edge_rows, "ctx", 1)
    x_previous = previous_rows[:, :channels]
    state_conv = silu_conv(state_whole, previous_rows[:, channels:], conv_state)
    inner_conv = silu_conv(x_local, x_previous, conv_inner)
    state_width = state_conv.shape[1] // 2
    b_rows = state_conv[:, :state_width]
    c_rows = state_conv[:, state_width:]
    step_size = jax.nn.softplus(step_local.astype(jnp.float32) + head_rates[0][None, :])
    log_decay = -step_size * jnp.exp(head_rates[1])[None, :]
    x_heads = inner_conv.reshape(context, heads_local, head_width)
    inputs = (x_heads.astype(jnp.float32) * step_size[:, :, None]).astype(jnp.bfloat16)
    block_count = context // SPAN
    start_state = jnp.zeros((heads_local, head_width, state_width), jnp.float32)
    final_state, outputs = lax.scan(
        block_terms,
        start_state,
        (
            c_rows.reshape(block_count, SPAN, state_width),
            b_rows.reshape(block_count, SPAN, state_width),
            inputs.reshape(block_count, SPAN, heads_local, head_width),
            log_decay.reshape(block_count, SPAN, heads_local),
        ),
    )
    running = jnp.cumsum(log_decay, axis=0)
    device_decay = jnp.exp(running[-1])

    def relay(position, arriving):
        return from_behind(device_decay[:, None, None] * arriving + final_state, "ctx", 1)

    incoming = lax.fori_loop(0, lax.axis_size("ctx") - 1, relay, jnp.zeros_like(final_state))
    carried = jnp.exp(running)[:, :, None] * jnp.einsum(
        "tn,hpn->thp", c_rows.astype(jnp.float32), incoming, precision=lax.Precision.HIGHEST
    )
    summed = (
        outputs.reshape(context, heads_local, head_width)
        + carried
        + skip_gain[None, :, None] * x_heads.astype(jnp.float32)
    )
    regrouped = summed.astype(jnp.bfloat16).reshape(context, channels)
    return lax.all_to_all(regrouped, "head", split_axis=0, concat_axis=1, tiled=True)


def solution(mesh):
    return jax.shard_map(
        per_device,
        mesh=mesh,
        in_specs=(
            P(("run", "ctx", "head"), None),
            P(("run", "ctx", "head"), None),
            P(("run", "ctx", "head"), None),
            P(None, "head"),
            P(),
            P("run", "head"),
            P("head"),
        ),
        out_specs=P(("run", "ctx", "head"), None),
        check_vma=False,
    )
```

profile of v0, /device:TPU:6, one launch (start us, length us, event | category | flops | bytes accessed | tf_op | source)
XLA Modules:
  0.0 1098.5 jit_solution(2019038271376231881)
XLA Ops:
  8.1 4.5 all-to-all-start
  12.5 5.2 copy.109
  18.3 5.2 all-to-all-start.1
  25.1 5.7 reduce-window.16
  31.9 30.6 %all-gather.2.cloned.1.call-done = bf16[2048,256]{1,0:T(8,128)(2,1)} async-done(((bf16[512,256]{1,0:T(8,128)(2,1)}), bf16[2048,256]{1,0:T(8,128)(2,1)}) %all-gather.2.cloned.1.call-update) | async-done | bytes 1048592 | tf_op jit(solution)/shard_map/all_gather | solution.py:62
  64.6 26.9 %all-to-all-done.1 = bf16[512,4,1280]{2,0,1:T(8,128)(2,1)} async-done(((bf16[512,4,1280]{2,0,1:T(8,128)(2,1)}), bf16[512,4,1280]{2,0,1:T(8,128)(2,1)}, u32[]{:S(2)}, u32[]{:S(2)}) %all-to-all-start.1) | async-done | bytes 5242912 | tf_op jit(solution)/shard_map/all_to_all | solution.py:54
  92.2 4.0 collective-permute-start.1
  96.2 3.3 bitcast_convert_fusion
  101.9 8.2 fusion.47
  110.1 11.4 %copy.83 = f32[2048,1280]{0,1:T(8,128)} copy(f32[2048,1280]{1,0:T(8,128)} %fusion.47) | data formatting | bytes 20971520 | tf_op jit(solution)/shard_map/convert_element_type | solution.py:76
  121.5 9.2 copy.101
  130.7 3.6 multiply_convert_fusion.4
  134.3 6.1 copy.85
  142.9 307.2 %while.24 = (s32[]{:T(128)}, f32[20,64,128]{2,1,0:T(8,128)S(1)}, f32[8,256,20,64]{1,0,3,2:T(8,128)}, f32[8,256,20]{1,0,2:T(8,128)S(1)}, bf16[8,256,20,64]{1,3,2,...) while((s32[]{:T(128)}, f32[20,64,128]{2,1,0:T(8,128)S(1)}, ...), condition=%wide.region_3.4_spmd.clone, body=%wide.region_0.3_spmd.clone.sunk | while | flops 1199117312 | bytes 13914835 | solution.py:79
  151.5 30.0 %dynamic_update_slice.6 = f32[8,256,20,64]{1,0,3,2:T(8,128)} dynamic-update-slice(f32[8,256,20,64]{1,0,3,2:T(8,128)} %get-tuple-element.251, f32[1,256,20,64]{1,0,3,2:T(1,128)S(1)} %copy.120, s32[]{:T(128)S(6)} %copy.125, s32[]{:T(128)} %constant.36.clone.1..sunk, s32[]{:T(128)} %constant.36.clone.1..sunk, s32[]{:T(128)} %constant.36.clone.1..sunk) | dynamic-update-slice | bytes 2621444 | tf_op jit(solution)/shard_map/while/body/jit(dynamic_update_index_in_dim)/dynamic_update_slice | solution.py:79
  182.7 2.6 fusion.86
  189.9 30.0 %dynamic_update_slice.6 = f32[8,256,20,64]{1,0,3,2:T(8,128)} dynamic-update-slice(f32[8,256,20,64]{1,0,3,2:T(8,128)} %get-tuple-element.251, f32[1,256,20,64]{1,0,3,2:T(1,128)S(1)} %copy.120, s32[]{:T(128)S(6)} %copy.125, s32[]{:T(128)} %constant.36.clone.1..sunk, s32[]{:T(128)} %constant.36.clone.1..sunk, s32[]{:T(128)} %constant.36.clone.1..sunk) | dynamic-update-slice | bytes 2621444 | tf_op jit(solution)/shard_map/while/body/jit(dynamic_update_index_in_dim)/dynamic_update_slice | solution.py:79
  228.2 30.0 %dynamic_update_slice.6 = f32[8,256,20,64]{1,0,3,2:T(8,128)} dynamic-update-slice(f32[8,256,20,64]{1,0,3,2:T(8,128)} %get-tuple-element.251, f32[1,256,20,64]{1,0,3,2:T(1,128)S(1)} %copy.120, s32[]{:T(128)S(6)} %copy.125, s32[]{:T(128)} %constant.36.clone.1..sunk, s32[]{:T(128)} %constant.36.clone.1..sunk, s32[]{:T(128)} %constant.36.clone.1..sunk) | dynamic-update-slice | bytes 2621444 | tf_op jit(solution)/shard_map/while/body/jit(dynamic_update_index_in_dim)/dynamic_update_slice | solution.py:79
  266.6 30.0 %dynamic_update_slice.6 = f32[8,256,20,64]{1,0,3,2:T(8,128)} dynamic-update-slice(f32[8,256,20,64]{1,0,3,2:T(8,128)} %get-tuple-element.251, f32[1,256,20,64]{1,0,3,2:T(1,128)S(1)} %copy.120, s32[]{:T(128)S(6)} %copy.125, s32[]{:T(128)} %constant.36.clone.1..sunk, s32[]{:T(128)} %constant.36.clone.1..sunk, s32[]{:T(128)} %constant.36.clone.1..sunk) | dynamic-update-slice | bytes 2621444 | tf_op jit(solution)/shard_map/while/body/jit(dynamic_update_index_in_dim)/dynamic_update_slice | solution.py:79
  297.8 2.6 fusion.86
  305.0 30.0 %dynamic_update_slice.6 = f32[8,256,20,64]{1,0,3,2:T(8,128)} dynamic-update-slice(f32[8,256,20,64]{1,0,3,2:T(8,128)} %get-tuple-element.251, f32[1,256,20,64]{1,0,3,2:T(1,128)S(1)} %copy.120, s32[]{:T(128)S(6)} %copy.125, s32[]{:T(128)} %constant.36.clone.1..sunk, s32[]{:T(128)} %constant.36.clone.1..sunk, s32[]{:T(128)} %constant.36.clone.1..sunk) | dynamic-update-slice | bytes 2621444 | tf_op jit(solution)/shard_map/while/body/jit(dynamic_update_index_in_dim)/dynamic_update_slice | solution.py:79
  343.3 30.0 %dynamic_update_slice.6 = f32[8,256,20,64]{1,0,3,2:T(8,128)} dynamic-update-slice(f32[8,256,20,64]{1,0,3,2:T(8,128)} %get-tuple-element.251, f32[1,256,20,64]{1,0,3,2:T(1,128)S(1)} %copy.120, s32[]{:T(128)S(6)} %copy.125, s32[]{:T(128)} %constant.36.clone.1..sunk, s32[]{:T(128)} %constant.36.clone.1..sunk, s32[]{:T(128)} %constant.36.clone.1..sunk) | dynamic-update-slice | bytes 2621444 | tf_op jit(solution)/shard_map/while/body/jit(dynamic_update_index_in_dim)/dynamic_update_slice | solution.py:79
  381.7 30.0 %dynamic_update_slice.6 = f32[8,256,20,64]{1,0,3,2:T(8,128)} dynamic-update-slice(f32[8,256,20,64]{1,0,3,2:T(8,128)} %get-tuple-element.251, f32[1,256,20,64]{1,0,3,2:T(1,128)S(1)} %copy.120, s32[]{:T(128)S(6)} %copy.125, s32[]{:T(128)} %constant.36.clone.1..sunk, s32[]{:T(128)} %constant.36.clone.1..sunk, s32[]{:T(128)} %constant.36.clone.1..sunk) | dynamic-update-slice | bytes 2621444 | tf_op jit(solution)/shard_map/while/body/jit(dynamic_update_index_in_dim)/dynamic_update_slice | solution.py:79
  413.0 2.6 fusion.86
  420.1 30.0 %dynamic_update_slice.6 = f32[8,256,20,64]{1,0,3,2:T(8,128)} dynamic-update-slice(f32[8,256,20,64]{1,0,3,2:T(8,128)} %get-tuple-element.251, f32[1,256,20,64]{1,0,3,2:T(1,128)S(1)} %copy.120, s32[]{:T(128)S(6)} %copy.125, s32[]{:T(128)} %constant.36.clone.1..sunk, s32[]{:T(128)} %constant.36.clone.1..sunk, s32[]{:T(128)} %constant.36.clone.1..sunk) | dynamic-update-slice | bytes 2621444 | tf_op jit(solution)/shard_map/while/body/jit(dynamic_update_index_in_dim)/dynamic_update_slice | solution.py:79
  450.1 11.4 %reshape.140 = f32[2048,20,64]{0,2,1:T(8,128)} reshape(f32[8,256,20,64]{1,0,3,2:T(8,128)} %get-tuple-element.65) | data formatting | bytes 20971520 | tf_op jit(solution)/shard_map/reshape | solution.py:100
  461.6 559.1 %while.23 = (s32[]{:T(128)}, f32[20,64,128]{2,1,0:T(8,128)S(1)}, f32[20]{0:T(128)S(1)}, f32[20,64,128]{2,1,0:T(8,128)S(1)}, s32[]{:T(128)}) while((s32[]{:T(128)}, f32[20,64,128]{2,1,0:T(8,128)S(1)}, f32[20]{0:T(128)S(1)}, f32[20,64,128]{2,1,0:T(8,128)S(1)}, s32[]{:T(128)}) %tuple.57), condition=%wide.region_7.8_spmd, body=%wide.region_6.7_spmd.sunk | while | flops 327682 | bytes 4587701 | solution.py:95
  463.8 16.0 %collective-permute-done = f32[20,64,128]{2,1,0:T(8,128)S(1)} collective-permute-done((f32[20,64,128]{2,1,0:T(8,128)S(1)}, f32[20,64,128]{2,1,0:T(8,128)S(1)}, u32[]{:S(2)}, u32[]{:S(2)}) %collective-permute-start) | collective-permute-done | bytes 655392 | tf_op jit(solution)/shard_map/while/body/eval_jaxpr/ppermute | solution.py:13
  481.8 15.1 %collective-permute-done = f32[20,64,128]{2,1,0:T(8,128)S(1)} collective-permute-done((f32[20,64,128]{2,1,0:T(8,128)S(1)}, f32[20,64,128]{2,1,0:T(8,128)S(1)}, u32[]{:S(2)}, u32[]{:S(2)}) %collective-permute-start) | collective-permute-done | bytes 655392 | tf_op jit(solution)/shard_map/while/body/eval_jaxpr/ppermute | solution.py:13
  499.0 14.2 %collective-permute-done = f32[20,64,128]{2,1,0:T(8,128)S(1)} collective-permute-done((f32[20,64,128]{2,1,0:T(8,128)S(1)}, f32[20,64,128]{2,1,0:T(8,128)S(1)}, u32[]{:S(2)}, u32[]{:S(2)}) %collective-permute-start) | collective-permute-done | bytes 655392 | tf_op jit(solution)/shard_map/while/body/eval_jaxpr/ppermute | solution.py:13
  515.3 13.4 %collective-permute-done = f32[20,64,128]{2,1,0:T(8,128)S(1)} collective-permute-done((f32[20,64,128]{2,1,0:T(8,128)S(1)}, f32[20,64,128]{2,1,0:T(8,128)S(1)}, u32[]{:S(2)}, u32[]{:S(2)}) %collective-permute-start) | collective-permute-done | bytes 655392 | tf_op jit(solution)/shard_map/while/body/eval_jaxpr/ppermute | solution.py:13
  530.7 13.3 %collective-permute-done = f32[20,64,128]{2,1,0:T(8,128)S(1)} collective-permute-done((f32[20,64,128]{2,1,0:T(8,128)S(1)}, f32[20,64,128]{2,1,0:T(8,128)S(1)}, u32[]{:S(2)}, u32[]{:S(2)}) %collective-permute-start) | collective-permute-done | bytes 655392 | tf_op jit(solution)/shard_map/while/body/eval_jaxpr/ppermute | solution.py:13
  546.1 14.4 %collective-permute-done = f32[20,64,128]{2,1,0:T(8,128)S(1)} collective-permute-done((f32[20,64,128]{2,1,0:T(8,128)S(1)}, f32[20,64,128]{2,1,0:T(8,128)S(1)}, u32[]{:S(2)}, u32[]{:S(2)}) %collective-permute-start) | collective-permute-done | bytes 655392 | tf_op jit(solution)/shard_map/while/body/eval_jaxpr/ppermute | solution.py:13
  562.5 15.5 %collective-permute-done = f32[20,64,128]{2,1,0:T(8,128)S(1)} collective-permute-done((f32[20,64,128]{2,1,0:T(8,128)S(1)}, f32[20,64,128]{2,1,0:T(8,128)S(1)}, u32[]{:S(2)}, u32[]{:S(2)}) %collective-permute-start) | collective-permute-done | bytes 655392 | tf_op jit(solution)/shard_map/while/body/eval_jaxpr/ppermute | solution.py:13
  580.1 16.7 %collective-permute-done = f32[20,64,128]{2,1,0:T(8,128)S(1)} collective-permute-done((f32[20,64,128]{2,1,0:T(8,128)S(1)}, f32[20,64,128]{2,1,0:T(8,128)S(1)}, u32[]{:S(2)}, u32[]{:S(2)}) %collective-permute-start) | collective-permute-done | bytes 655392 | tf_op jit(solution)/shard_map/while/body/eval_jaxpr/ppermute | solution.py:13
  598.9 17.8 %collective-permute-done = f32[20,64,128]{2,1,0:T(8,128)S(1)} collective-permute-done((f32[20,64,128]{2,1,0:T(8,128)S(1)}, f32[20,64,128]{2,1,0:T(8,128)S(1)}, u32[]{:S(2)}, u32[]{:S(2)}) %collective-permute-start) | collective-permute-done | bytes 655392 | tf_op jit(solution)/shard_map/while/body/eval_jaxpr/ppermute | solution.py:13
  618.8 19.0 %collective-permute-done = f32[20,64,128]{2,1,0:T(8,128)S(1)} collective-permute-done((f32[20,64,128]{2,1,0:T(8,128)S(1)}, f32[20,64,128]{2,1,0:T(8,128)S(1)}, u32[]{:S(2)}, u32[]{:S(2)}) %collective-permute-start) | collective-permute-done | bytes 655392 | tf_op jit(solution)/shard_map/while/body/eval_jaxpr/ppermute | solution.py:13
  639.9 19.2 %collective-permute-done = f32[20,64,128]{2,1,0:T(8,128)S(1)} collective-permute-done((f32[20,64,128]{2,1,0:T(8,128)S(1)}, f32[20,64,128]{2,1,0:T(8,128)S(1)}, u32[]{:S(2)}, u32[]{:S(2)}) %collective-permute-start) | collective-permute-done | bytes 655392 | tf_op jit(solution)/shard_map/while/body/eval_jaxpr/ppermute | solution.py:13
  661.1 18.4 %collective-permute-done = f32[20,64,128]{2,1,0:T(8,128)S(1)} collective-permute-done((f32[20,64,128]{2,1,0:T(8,128)S(1)}, f32[20,64,128]{2,1,0:T(8,128)S(1)}, u32[]{:S(2)}, u32[]{:S(2)}) %collective-permute-start) | collective-permute-done | bytes 655392 | tf_op jit(solution)/shard_map/while/body/eval_jaxpr/ppermute | solution.py:13
  681.6 17.5 %collective-permute-done = f32[20,64,128]{2,1,0:T(8,128)S(1)} collective-permute-done((f32[20,64,128]{2,1,0:T(8,128)S(1)}, f32[20,64,128]{2,1,0:T(8,128)S(1)}, u32[]{:S(2)}, u32[]{:S(2)}) %collective-permute-start) | collective-permute-done | bytes 655392 | tf_op jit(solution)/shard_map/while/body/eval_jaxpr/ppermute | solution.py:13
  701.1 16.7 %collective-permute-done = f32[20,64,128]{2,1,0:T(8,128)S(1)} collective-permute-done((f32[20,64,128]{2,1,0:T(8,128)S(1)}, f32[20,64,128]{2,1,0:T(8,128)S(1)}, u32[]{:S(2)}, u32[]{:S(2)}) %collective-permute-start) | collective-permute-done | bytes 655392 | tf_op jit(solution)/shard_map/while/body/eval_jaxpr/ppermute | solution.py:13
  719.9 15.8 %collective-permute-done = f32[20,64,128]{2,1,0:T(8,128)S(1)} collective-permute-done((f32[20,64,128]{2,1,0:T(8,128)S(1)}, f32[20,64,128]{2,1,0:T(8,128)S(1)}, u32[]{:S(2)}, u32[]{:S(2)}) %collective-permute-start) | collective-permute-done | bytes 655392 | tf_op jit(solution)/shard_map/while/body/eval_jaxpr/ppermute | solution.py:13
  737.7 14.9 %collective-permute-done = f32[20,64,128]{2,1,0:T(8,128)S(1)} collective-permute-done((f32[20,64,128]{2,1,0:T(8,128)S(1)}, f32[20,64,128]{2,1,0:T(8,128)S(1)}, u32[]{:S(2)}, u32[]{:S(2)}) %collective-permute-start) | collective-permute-done | bytes 655392 | tf_op jit(solution)/shard_map/while/body/eval_jaxpr/ppermute | solution.py:13
  754.7 14.1 %collective-permute-done = f32[20,64,128]{2,1,0:T(8,128)S(1)} collective-permute-done((f32[20,64,128]{2,1,0:T(8,128)S(1)}, f32[20,64,128]{2,1,0:T(8,128)S(1)}, u32[]{:S(2)}, u32[]{:S(2)}) %collective-permute-start) | collective-permute-done | bytes 655392 | tf_op jit(solution)/shard_map/while/body/eval_jaxpr/ppermute | solution.py:13
  770.9 13.2 %collective-permute-done = f32[20,64,128]{2,1,0:T(8,128)S(1)} collective-permute-done((f32[20,64,128]{2,1,0:T(8,128)S(1)}, f32[20,64,128]{2,1,0:T(8,128)S(1)}, u32[]{:S(2)}, u32[]{:S(2)}) %collective-permute-start) | collective-permute-done | bytes 655392 | tf_op jit(solution)/shard_map/while/body/eval_jaxpr/ppermute | solution.py:13
  786.2 13.4 %collective-permute-done = f32[20,64,128]{2,1,0:T(8,128)S(1)} collective-permute-done((f32[20,64,128]{2,1,0:T(8,128)S(1)}, f32[20,64,128]{2,1,0:T(8,128)S(1)}, u32[]{:S(2)}, u32[]{:S(2)}) %collective-permute-start) | collective-permute-done | bytes 655392 | tf_op jit(solution)/shard_map/while/body/eval_jaxpr/ppermute | solution.py:13
  801.7 14.6 %collective-permute-done = f32[20,64,128]{2,1,0:T(8,128)S(1)} collective-permute-done((f32[20,64,128]{2,1,0:T(8,128)S(1)}, f32[20,64,128]{2,1,0:T(8,128)S(1)}, u32[]{:S(2)}, u32[]{:S(2)}) %collective-permute-start) | collective-permute-done | bytes 655392 | tf_op jit(solution)/shard_map/while/body/eval_jaxpr/ppermute | solution.py:13
  818.3 15.7 %collective-permute-done = f32[20,64,128]{2,1,0:T(8,128)S(1)} collective-permute-done((f32[20,64,128]{2,1,0:T(8,128)S(1)}, f32[20,64,128]{2,1,0:T(8,128)S(1)}, u32[]{:S(2)}, u32[]{:S(2)}) %collective-permute-start) | collective-permute-done | bytes 655392 | tf_op jit(solution)/shard_map/while/body/eval_jaxpr/ppermute | solution.py:13
  836.0 16.8 %collective-permute-done = f32[20,64,128]{2,1,0:T(8,128)S(1)} collective-permute-done((f32[20,64,128]{2,1,0:T(8,128)S(1)}, f32[20,64,128]{2,1,0:T(8,128)S(1)}, u32[]{:S(2)}, u32[]{:S(2)}) %collective-permute-start) | collective-permute-done | bytes 655392 | tf_op jit(solution)/shard_map/while/body/eval_jaxpr/ppermute | solution.py:13
  855.0 18.0 %collective-permute-done = f32[20,64,128]{2,1,0:T(8,128)S(1)} collective-permute-done((f32[20,64,128]{2,1,0:T(8,128)S(1)}, f32[20,64,128]{2,1,0:T(8,128)S(1)}, u32[]{:S(2)}, u32[]{:S(2)}) %collective-permute-start) | collective-permute-done | bytes 655392 | tf_op jit(solution)/shard_map/while/body/eval_jaxpr/ppermute | solution.py:13
  875.0 19.1 %collective-permute-done = f32[20,64,128]{2,1,0:T(8,128)S(1)} collective-permute-done((f32[20,64,128]{2,1,0:T(8,128)S(1)}, f32[20,64,128]{2,1,0:T(8,128)S(1)}, u32[]{:S(2)}, u32[]{:S(2)}) %collective-permute-start) | collective-permute-done | bytes 655392 | tf_op jit(solution)/shard_map/while/body/eval_jaxpr/ppermute | solution.py:13
  896.2 19.1 %collective-permute-done = f32[20,64,128]{2,1,0:T(8,128)S(1)} collective-permute-done((f32[20,64,128]{2,1,0:T(8,128)S(1)}, f32[20,64,128]{2,1,0:T(8,128)S(1)}, u32[]{:S(2)}, u32[]{:S(2)}) %collective-permute-start) | collective-permute-done | bytes 655392 | tf_op jit(solution)/shard_map/while/body/eval_jaxpr/ppermute | solution.py:13
  917.4 18.2 %collective-permute-done = f32[20,64,128]{2,1,0:T(8,128)S(1)} collective-permute-done((f32[20,64,128]{2,1,0:T(8,128)S(1)}, f32[20,64,128]{2,1,0:T(8,128)S(1)}, u32[]{:S(2)}, u32[]{:S(2)}) %collective-permute-start) | collective-permute-done | bytes 655392 | tf_op jit(solution)/shard_map/while/body/eval_jaxpr/ppermute | solution.py:13
  937.6 17.4 %collective-permute-done = f32[20,64,128]{2,1,0:T(8,128)S(1)} collective-permute-done((f32[20,64,128]{2,1,0:T(8,128)S(1)}, f32[20,64,128]{2,1,0:T(8,128)S(1)}, u32[]{:S(2)}, u32[]{:S(2)}) %collective-permute-start) | collective-permute-done | bytes 655392 | tf_op jit(solution)/shard_map/while/body/eval_jaxpr/ppermute | solution.py:13
  957.0 16.5 %collective-permute-done = f32[20,64,128]{2,1,0:T(8,128)S(1)} collective-permute-done((f32[20,64,128]{2,1,0:T(8,128)S(1)}, f32[20,64,128]{2,1,0:T(8,128)S(1)}, u32[]{:S(2)}, u32[]{:S(2)}) %collective-permute-start) | collective-permute-done | bytes 655392 | tf_op jit(solution)/shard_map/while/body/eval_jaxpr/ppermute | solution.py:13
  975.6 15.6 %collective-permute-done = f32[20,64,128]{2,1,0:T(8,128)S(1)} collective-permute-done((f32[20,64,128]{2,1,0:T(8,128)S(1)}, f32[20,64,128]{2,1,0:T(8,128)S(1)}, u32[]{:S(2)}, u32[]{:S(2)}) %collective-permute-start) | collective-permute-done | bytes 655392 | tf_op jit(solution)/shard_map/while/body/eval_jaxpr/ppermute | solution.py:13
  993.3 12.7 %collective-permute-done = f32[20,64,128]{2,1,0:T(8,128)S(1)} collective-permute-done((f32[20,64,128]{2,1,0:T(8,128)S(1)}, f32[20,64,128]{2,1,0:T(8,128)S(1)}, u32[]{:S(2)}, u32[]{:S(2)}) %collective-permute-start) | collective-permute-done | bytes 655392 | tf_op jit(solution)/shard_map/while/body/eval_jaxpr/ppermute | solution.py:13
  1008.0 12.7 %collective-permute-done = f32[20,64,128]{2,1,0:T(8,128)S(1)} collective-permute-done((f32[20,64,128]{2,1,0:T(8,128)S(1)}, f32[20,64,128]{2,1,0:T(8,128)S(1)}, u32[]{:S(2)}, u32[]{:S(2)}) %collective-permute-start) | collective-permute-done | bytes 655392 | tf_op jit(solution)/shard_map/while/body/eval_jaxpr/ppermute | solution.py:13
  1020.7 4.2 fusion.57
  1025.0 8.9 add_convert_fusion
  1033.9 9.5 all_to_all.44
  1043.4 3.5 copy.91
  1046.9 36.9 %all_to_all.51 = bf16[4,512,1280]{1,2,0:T(8,128)(2,1)} all-to-all(bf16[4,512,1280]{1,2,0:T(8,128)(2,1)S(1)} %copy.91), channel_id=1, replica_groups=mesh['run'=2,'ctx'=32,'head'=4] {'head'}, dimensions={0} | all-to-all | bytes 10485760 | tf_op jit(solution)/shard_map/all_to_all | solution.py:105
  1083.8 7.9 copy.92
  (278 shorter events, 134.2 us)
Async XLA Ops:
  8.1 10.3 all-to-all-start
  18.3 5.9 copy-start.3
  18.3 6.0 copy-start.5
  18.3 6.1 copy-start.4
  18.3 73.1 %all-to-all-start.1 = ((bf16[512,4,1280]{2,0,1:T(8,128)(2,1)}), bf16[512,4,1280]{2,0,1:T(8,128)(2,1)}, u32[]{:S(2)}, u32[]{:S(2)}) async-start(bf16[512,4,1280]{2,0,1:T(8,128)(2,1)} %bitcast.129), calls=%async_computation.1 | async-start | bytes 10485760 | tf_op jit(solution)/shard_map/all_to_all | solution.py:54
  23.5 39.0 %all-gather.2.cloned.1.call-start = ((), (), s32[]{:S(2)}) async-start(), calls=%async_computation.3 | async-start | bytes 1310720 | tf_op jit(solution)/shard_map/all_gather | solution.py:62
  92.2 9.7 collective-permute-start.1
  141.9 1.0 copy-start.1
  461.5 559.2 %copy-start.2 = (bf16[2048,256]{1,0:T(8,128)(2,1)S(1)}, bf16[2048,256]{1,0:T(8,128)(2,1)}, u32[]{:S(2)}) copy-start(bf16[2048,256]{1,0:T(8,128)(2,1)} %copy-done.1) | copy-start | bytes 3145732
  461.7 18.0 %collective-permute-start = (f32[20,64,128]{2,1,0:T(8,128)S(1)}, f32[20,64,128]{2,1,0:T(8,128)S(1)}, u32[]{:S(2)}, u32[]{:S(2)}) collective-permute-start(f32[20,64,128]{2,1,0:T(8,128)S(1)} %multiply_add_fusion.2), channel_id=1, source_target_pairs={{0,4},{4,8},{8,12},{12,16},{16,20},{20,24},{24,28},{28,32},{32,36}... | collective-permute-start | bytes 1966088 | tf_op jit(solution)/shard_map/while/body/eval_jaxpr/ppermute | solution.py:13
  479.9 17.0 %collective-permute-start = (f32[20,64,128]{2,1,0:T(8,128)S(1)}, f32[20,64,128]{2,1,0:T(8,128)S(1)}, u32[]{:S(2)}, u32[]{:S(2)}) collective-permute-start(f32[20,64,128]{2,1,0:T(8,128)S(1)} %multiply_add_fusion.2), channel_id=1, source_target_pairs={{0,4},{4,8},{8,12},{12,16},{16,20},{20,24},{24,28},{28,32},{32,36}... | collective-permute-start | bytes 1966088 | tf_op jit(solution)/shard_map/while/body/eval_jaxpr/ppermute | solution.py:13
  497.1 16.2 %collective-permute-start = (f32[20,64,128]{2,1,0:T(8,128)S(1)}, f32[20,64,128]{2,1,0:T(8,128)S(1)}, u32[]{:S(2)}, u32[]{:S(2)}) collective-permute-start(f32[20,64,128]{2,1,0:T(8,128)S(1)} %multiply_add_fusion.2), channel_id=1, source_target_pairs={{0,4},{4,8},{8,12},{12,16},{16,20},{20,24},{24,28},{28,32},{32,36}... | collective-permute-start | bytes 1966088 | tf_op jit(solution)/shard_map/while/body/eval_jaxpr/ppermute | solution.py:13
  513.4 15.3 %collective-permute-start = (f32[20,64,128]{2,1,0:T(8,128)S(1)}, f32[20,64,128]{2,1,0:T(8,128)S(1)}, u32[]{:S(2)}, u32[]{:S(2)}) collective-permute-start(f32[20,64,128]{2,1,0:T(8,128)S(1)} %multiply_add_fusion.2), channel_id=1, source_target_pairs={{0,4},{4,8},{8,12},{12,16},{16,20},{20,24},{24,28},{28,32},{32,36}... | collective-permute-start | bytes 1966088 | tf_op jit(solution)/shard_map/while/body/eval_jaxpr/ppermute | solution.py:13
  528.8 15.2 %collective-permute-start = (f32[20,64,128]{2,1,0:T(8,128)S(1)}, f32[20,64,128]{2,1,0:T(8,128)S(1)}, u32[]{:S(2)}, u32[]{:S(2)}) collective-permute-start(f32[20,64,128]{2,1,0:T(8,128)S(1)} %multiply_add_fusion.2), channel_id=1, source_target_pairs={{0,4},{4,8},{8,12},{12,16},{16,20},{20,24},{24,28},{28,32},{32,36}... | collective-permute-start | bytes 1966088 | tf_op jit(solution)/shard_map/while/body/eval_jaxpr/ppermute | solution.py:13
  544.1 16.3 %collective-permute-start = (f32[20,64,128]{2,1,0:T(8,128)S(1)}, f32[20,64,128]{2,1,0:T(8,128)S(1)}, u32[]{:S(2)}, u32[]{:S(2)}) collective-permute-start(f32[20,64,128]{2,1,0:T(8,128)S(1)} %multiply_add_fusion.2), channel_id=1, source_target_pairs={{0,4},{4,8},{8,12},{12,16},{16,20},{20,24},{24,28},{28,32},{32,36}... | collective-permute-start | bytes 1966088 | tf_op jit(solution)/shard_map/while/body/eval_jaxpr/ppermute | solution.py:13
  560.6 17.5 %collective-permute-start = (f32[20,64,128]{2,1,0:T(8,128)S(1)}, f32[20,64,128]{2,1,0:T(8,128)S(1)}, u32[]{:S(2)}, u32[]{:S(2)}) collective-permute-start(f32[20,64,128]{2,1,0:T(8,128)S(1)} %multiply_add_fusion.2), channel_id=1, source_target_pairs={{0,4},{4,8},{8,12},{12,16},{16,20},{20,24},{24,28},{28,32},{32,36}... | collective-permute-start | bytes 1966088 | tf_op jit(solution)/shard_map/while/body/eval_jaxpr/ppermute | solution.py:13
  578.2 18.6 %collective-permute-start = (f32[20,64,128]{2,1,0:T(8,128)S(1)}, f32[20,64,128]{2,1,0:T(8,128)S(1)}, u32[]{:S(2)}, u32[]{:S(2)}) collective-permute-start(f32[20,64,128]{2,1,0:T(8,128)S(1)} %multiply_add_fusion.2), channel_id=1, source_target_pairs={{0,4},{4,8},{8,12},{12,16},{16,20},{20,24},{24,28},{28,32},{32,36}... | collective-permute-start | bytes 1966088 | tf_op jit(solution)/shard_map/while/body/eval_jaxpr/ppermute | solution.py:13
  597.0 19.8 %collective-permute-start = (f32[20,64,128]{2,1,0:T(8,128)S(1)}, f32[20,64,128]{2,1,0:T(8,128)S(1)}, u32[]{:S(2)}, u32[]{:S(2)}) collective-permute-start(f32[20,64,128]{2,1,0:T(8,128)S(1)} %multiply_add_fusion.2), channel_id=1, source_target_pairs={{0,4},{4,8},{8,12},{12,16},{16,20},{20,24},{24,28},{28,32},{32,36}... | collective-permute-start | bytes 1966088 | tf_op jit(solution)/shard_map/while/body/eval_jaxpr/ppermute | solution.py:13
  616.9 20.9 %collective-permute-start = (f32[20,64,128]{2,1,0:T(8,128)S(1)}, f32[20,64,128]{2,1,0:T(8,128)S(1)}, u32[]{:S(2)}, u32[]{:S(2)}) collective-permute-start(f32[20,64,128]{2,1,0:T(8,128)S(1)} %multiply_add_fusion.2), channel_id=1, source_target_pairs={{0,4},{4,8},{8,12},{12,16},{16,20},{20,24},{24,28},{28,32},{32,36}... | collective-permute-start | bytes 1966088 | tf_op jit(solution)/shard_map/while/body/eval_jaxpr/ppermute | solution.py:13
  637.9 21.2 %collective-permute-start = (f32[20,64,128]{2,1,0:T(8,128)S(1)}, f32[20,64,128]{2,1,0:T(8,128)S(1)}, u32[]{:S(2)}, u32[]{:S(2)}) collective-permute-start(f32[20,64,128]{2,1,0:T(8,128)S(1)} %multiply_add_fusion.2), channel_id=1, source_target_pairs={{0,4},{4,8},{8,12},{12,16},{16,20},{20,24},{24,28},{28,32},{32,36}... | collective-permute-start | bytes 1966088 | tf_op jit(solution)/shard_map/while/body/eval_jaxpr/ppermute | solution.py:13
  659.2 20.3 %collective-permute-start = (f32[20,64,128]{2,1,0:T(8,128)S(1)}, f32[20,64,128]{2,1,0:T(8,128)S(1)}, u32[]{:S(2)}, u32[]{:S(2)}) collective-permute-start(f32[20,64,128]{2,1,0:T(8,128)S(1)} %multiply_add_fusion.2), channel_id=1, source_target_pairs={{0,4},{4,8},{8,12},{12,16},{16,20},{20,24},{24,28},{28,32},{32,36}... | collective-permute-start | bytes 1966088 | tf_op jit(solution)/shard_map/while/body/eval_jaxpr/ppermute | solution.py:13
  679.6 19.4 %collective-permute-start = (f32[20,64,128]{2,1,0:T(8,128)S(1)}, f32[20,64,128]{2,1,0:T(8,128)S(1)}, u32[]{:S(2)}, u32[]{:S(2)}) collective-permute-start(f32[20,64,128]{2,1,0:T(8,128)S(1)} %multiply_add_fusion.2), channel_id=1, source_target_pairs={{0,4},{4,8},{8,12},{12,16},{16,20},{20,24},{24,28},{28,32},{32,36}... | collective-permute-start | bytes 1966088 | tf_op jit(solution)/shard_map/while/body/eval_jaxpr/ppermute | solution.py:13
  699.2 18.6 %collective-permute-start = (f32[20,64,128]{2,1,0:T(8,128)S(1)}, f32[20,64,128]{2,1,0:T(8,128)S(1)}, u32[]{:S(2)}, u32[]{:S(2)}) collective-permute-start(f32[20,64,128]{2,1,0:T(8,128)S(1)} %multiply_add_fusion.2), channel_id=1, source_target_pairs={{0,4},{4,8},{8,12},{12,16},{16,20},{20,24},{24,28},{28,32},{32,36}... | collective-permute-start | bytes 1966088 | tf_op jit(solution)/shard_map/while/body/eval_jaxpr/ppermute | solution.py:13
  717.9 17.7 %collective-permute-start = (f32[20,64,128]{2,1,0:T(8,128)S(1)}, f32[20,64,128]{2,1,0:T(8,128)S(1)}, u32[]{:S(2)}, u32[]{:S(2)}) collective-permute-start(f32[20,64,128]{2,1,0:T(8,128)S(1)} %multiply_add_fusion.2), channel_id=1, source_target_pairs={{0,4},{4,8},{8,12},{12,16},{16,20},{20,24},{24,28},{28,32},{32,36}... | collective-permute-start | bytes 1966088 | tf_op jit(solution)/shard_map/while/body/eval_jaxpr/ppermute | solution.py:13
  735.8 16.9 %collective-permute-start = (f32[20,64,128]{2,1,0:T(8,128)S(1)}, f32[20,64,128]{2,1,0:T(8,128)S(1)}, u32[]{:S(2)}, u32[]{:S(2)}) collective-permute-start(f32[20,64,128]{2,1,0:T(8,128)S(1)} %multiply_add_fusion.2), channel_id=1, source_target_pairs={{0,4},{4,8},{8,12},{12,16},{16,20},{20,24},{24,28},{28,32},{32,36}... | collective-permute-start | bytes 1966088 | tf_op jit(solution)/shard_map/while/body/eval_jaxpr/ppermute | solution.py:13
  752.8 16.0 %collective-permute-start = (f32[20,64,128]{2,1,0:T(8,128)S(1)}, f32[20,64,128]{2,1,0:T(8,128)S(1)}, u32[]{:S(2)}, u32[]{:S(2)}) collective-permute-start(f32[20,64,128]{2,1,0:T(8,128)S(1)} %multiply_add_fusion.2), channel_id=1, source_target_pairs={{0,4},{4,8},{8,12},{12,16},{16,20},{20,24},{24,28},{28,32},{32,36}... | collective-permute-start | bytes 1966088 | tf_op jit(solution)/shard_map/while/body/eval_jaxpr/ppermute | solution.py:13
  769.0 15.2 %collective-permute-start = (f32[20,64,128]{2,1,0:T(8,128)S(1)}, f32[20,64,128]{2,1,0:T(8,128)S(1)}, u32[]{:S(2)}, u32[]{:S(2)}) collective-permute-start(f32[20,64,128]{2,1,0:T(8,128)S(1)} %multiply_add_fusion.2), channel_id=1, source_target_pairs={{0,4},{4,8},{8,12},{12,16},{16,20},{20,24},{24,28},{28,32},{32,36}... | collective-permute-start | bytes 1966088 | tf_op jit(solution)/shard_map/while/body/eval_jaxpr/ppermute | solution.py:13
  784.2 15.3 %collective-permute-start = (f32[20,64,128]{2,1,0:T(8,128)S(1)}, f32[20,64,128]{2,1,0:T(8,128)S(1)}, u32[]{:S(2)}, u32[]{:S(2)}) collective-permute-start(f32[20,64,128]{2,1,0:T(8,128)S(1)} %multiply_add_fusion.2), channel_id=1, source_target_pairs={{0,4},{4,8},{8,12},{12,16},{16,20},{20,24},{24,28},{28,32},{32,36}... | collective-permute-start | bytes 1966088 | tf_op jit(solution)/shard_map/while/body/eval_jaxpr/ppermute | solution.py:13
  799.7 16.5 %collective-permute-start = (f32[20,64,128]{2,1,0:T(8,128)S(1)}, f32[20,64,128]{2,1,0:T(8,128)S(1)}, u32[]{:S(2)}, u32[]{:S(2)}) collective-permute-start(f32[20,64,128]{2,1,0:T(8,128)S(1)} %multiply_add_fusion.2), channel_id=1, source_target_pairs={{0,4},{4,8},{8,12},{12,16},{16,20},{20,24},{24,28},{28,32},{32,36}... | collective-permute-start | bytes 1966088 | tf_op jit(solution)/shard_map/while/body/eval_jaxpr/ppermute | solution.py:13
  816.3 17.6 %collective-permute-start = (f32[20,64,128]{2,1,0:T(8,128)S(1)}, f32[20,64,128]{2,1,0:T(8,128)S(1)}, u32[]{:S(2)}, u32[]{:S(2)}) collective-permute-start(f32[20,64,128]{2,1,0:T(8,128)S(1)} %multiply_add_fusion.2), channel_id=1, source_target_pairs={{0,4},{4,8},{8,12},{12,16},{16,20},{20,24},{24,28},{28,32},{32,36}... | collective-permute-start | bytes 1966088 | tf_op jit(solution)/shard_map/while/body/eval_jaxpr/ppermute | solution.py:13
  834.1 18.8 %collective-permute-start = (f32[20,64,128]{2,1,0:T(8,128)S(1)}, f32[20,64,128]{2,1,0:T(8,128)S(1)}, u32[]{:S(2)}, u32[]{:S(2)}) collective-permute-start(f32[20,64,128]{2,1,0:T(8,128)S(1)} %multiply_add_fusion.2), channel_id=1, source_target_pairs={{0,4},{4,8},{8,12},{12,16},{16,20},{20,24},{24,28},{28,32},{32,36}... | collective-permute-start | bytes 1966088 | tf_op jit(solution)/shard_map/while/body/eval_jaxpr/ppermute | solution.py:13
  853.0 19.9 %collective-permute-start = (f32[20,64,128]{2,1,0:T(8,128)S(1)}, f32[20,64,128]{2,1,0:T(8,128)S(1)}, u32[]{:S(2)}, u32[]{:S(2)}) collective-permute-start(f32[20,64,128]{2,1,0:T(8,128)S(1)} %multiply_add_fusion.2), channel_id=1, source_target_pairs={{0,4},{4,8},{8,12},{12,16},{16,20},{20,24},{24,28},{28,32},{32,36}... | collective-permute-start | bytes 1966088 | tf_op jit(solution)/shard_map/while/body/eval_jaxpr/ppermute | solution.py:13
  873.1 21.1 %collective-permute-start = (f32[20,64,128]{2,1,0:T(8,128)S(1)}, f32[20,64,128]{2,1,0:T(8,128)S(1)}, u32[]{:S(2)}, u32[]{:S(2)}) collective-permute-start(f32[20,64,128]{2,1,0:T(8,128)S(1)} %multiply_add_fusion.2), channel_id=1, source_target_pairs={{0,4},{4,8},{8,12},{12,16},{16,20},{20,24},{24,28},{28,32},{32,36}... | collective-permute-start | bytes 1966088 | tf_op jit(solution)/shard_map/while/body/eval_jaxpr/ppermute | solution.py:13
  894.3 21.0 %collective-permute-start = (f32[20,64,128]{2,1,0:T(8,128)S(1)}, f32[20,64,128]{2,1,0:T(8,128)S(1)}, u32[]{:S(2)}, u32[]{:S(2)}) collective-permute-start(f32[20,64,128]{2,1,0:T(8,128)S(1)} %multiply_add_fusion.2), channel_id=1, source_target_pairs={{0,4},{4,8},{8,12},{12,16},{16,20},{20,24},{24,28},{28,32},{32,36}... | collective-permute-start | bytes 1966088 | tf_op jit(solution)/shard_map/while/body/eval_jaxpr/ppermute | solution.py:13
  915.4 20.1 %collective-permute-start = (f32[20,64,128]{2,1,0:T(8,128)S(1)}, f32[20,64,128]{2,1,0:T(8,128)S(1)}, u32[]{:S(2)}, u32[]{:S(2)}) collective-permute-start(f32[20,64,128]{2,1,0:T(8,128)S(1)} %multiply_add_fusion.2), channel_id=1, source_target_pairs={{0,4},{4,8},{8,12},{12,16},{16,20},{20,24},{24,28},{28,32},{32,36}... | collective-permute-start | bytes 1966088 | tf_op jit(solution)/shard_map/while/body/eval_jaxpr/ppermute | solution.py:13
  935.7 19.3 %collective-permute-start = (f32[20,64,128]{2,1,0:T(8,128)S(1)}, f32[20,64,128]{2,1,0:T(8,128)S(1)}, u32[]{:S(2)}, u32[]{:S(2)}) collective-permute-start(f32[20,64,128]{2,1,0:T(8,128)S(1)} %multiply_add_fusion.2), channel_id=1, source_target_pairs={{0,4},{4,8},{8,12},{12,16},{16,20},{20,24},{24,28},{28,32},{32,36}... | collective-permute-start | bytes 1966088 | tf_op jit(solution)/shard_map/while/body/eval_jaxpr/ppermute | solution.py:13
  955.1 18.4 %collective-permute-start = (f32[20,64,128]{2,1,0:T(8,128)S(1)}, f32[20,64,128]{2,1,0:T(8,128)S(1)}, u32[]{:S(2)}, u32[]{:S(2)}) collective-permute-start(f32[20,64,128]{2,1,0:T(8,128)S(1)} %multiply_add_fusion.2), channel_id=1, source_target_pairs={{0,4},{4,8},{8,12},{12,16},{16,20},{20,24},{24,28},{28,32},{32,36}... | collective-permute-start | bytes 1966088 | tf_op jit(solution)/shard_map/while/body/eval_jaxpr/ppermute | solution.py:13
  973.7 17.6 %collective-permute-start = (f32[20,64,128]{2,1,0:T(8,128)S(1)}, f32[20,64,128]{2,1,0:T(8,128)S(1)}, u32[]{:S(2)}, u32[]{:S(2)}) collective-permute-start(f32[20,64,128]{2,1,0:T(8,128)S(1)} %multiply_add_fusion.2), channel_id=1, source_target_pairs={{0,4},{4,8},{8,12},{12,16},{16,20},{20,24},{24,28},{28,32},{32,36}... | collective-permute-start | bytes 1966088 | tf_op jit(solution)/shard_map/while/body/eval_jaxpr/ppermute | solution.py:13
  991.4 14.6 %collective-permute-start = (f32[20,64,128]{2,1,0:T(8,128)S(1)}, f32[20,64,128]{2,1,0:T(8,128)S(1)}, u32[]{:S(2)}, u32[]{:S(2)}) collective-permute-start(f32[20,64,128]{2,1,0:T(8,128)S(1)} %multiply_add_fusion.2), channel_id=1, source_target_pairs={{0,4},{4,8},{8,12},{12,16},{16,20},{20,24},{24,28},{28,32},{32,36}... | collective-permute-start | bytes 1966088 | tf_op jit(solution)/shard_map/while/body/eval_jaxpr/ppermute | solution.py:13
  1006.1 14.6 %collective-permute-start = (f32[20,64,128]{2,1,0:T(8,128)S(1)}, f32[20,64,128]{2,1,0:T(8,128)S(1)}, u32[]{:S(2)}, u32[]{:S(2)}) collective-permute-start(f32[20,64,128]{2,1,0:T(8,128)S(1)} %multiply_add_fusion.2), channel_id=1, source_target_pairs={{0,4},{4,8},{8,12},{12,16},{16,20},{20,24},{24,28},{28,32},{32,36}... | collective-permute-start | bytes 1966088 | tf_op jit(solution)/shard_map/while/body/eval_jaxpr/ppermute | solution.py:13
  1020.7 4.2 copy-start
  1020.7 4.3 copy-start.6
Sparse Core Ops, SparseCore 0:
  26.1 36.3 all-gather.1
where the time goes:
time: 1110 us; the launch traced here: 1100 us
  waiting for transfers between devices  556 us (50%)
  local copies, waits for them, and re-layouts  324 us (29%)
  starting transfers between devices  73.4 us (7%)
  matrix products  49.4 us (4%)
  other arithmetic  43.6 us (4%)
  blocking collectives  36.9 us (3%)
  between operations  13.7 us (1%)
    ppermute x32, waiting for transfers between devices, from_behind(): return lax.ppermute(value, axis, pairs)  497 us
    dynamic_update_slice x16, local copies, waits for them, and re-layouts, per_device(): lax.scan(block_terms, start_state, (c_rows.reshape(block_count, SPAN, sta...  251 us
    ppermute x32, starting transfers between devices, from_behind(): return lax.ppermute(value, axis, pairs)  63.7 us
    all_to_all x1, blocking collectives, per_device(): lax.all_to_all(regrouped, 'head', split_axis=0, concat_axis=1, tiled=True)  36.9 us
    all_gather x1, waiting for transfers between devices, per_device(): state_whole = lax.all_gather(state_inputs, 'head', axis=0, tiled=True)  30.6 us
    all_to_all x1, waiting for transfers between devices, per_device(): lax.all_to_all(inner_tokens, 'head', split_axis=1, concat_axis=0, tiled=T...  26.9 us
  transfers between devices with their start and end apart: 35, of which 35 were waited for; matrix products, arithmetic and copies ran while one was open for 2% of the time, Pallas kernels for 0%

commit v1 on v0

--- a/solution.py
+++ b/solution.py
@@ -25,28 +25,18 @@
     return jax.nn.silu(summed).astype(jnp.bfloat16)
 
 
-def block_terms(carry_state, pieces):
-    c_block, b_block, u_block, decay_block = pieces
-    cumulative = jnp.cumsum(decay_block, axis=0)
-    across = cumulative.T
-    inner_scores = jnp.dot(c_block, b_block.T, preferred_element_type=jnp.float32)
-    spread = across[:, :, None] - across[:, None, :]
-    places = jnp.arange(c_block.shape[0])
-    causal = places[:, None] >= places[None, :]
-    mixing = (inner_scores[None] * jnp.exp(jnp.where(causal[None], spread, -jnp.inf))).astype(
-        jnp.bfloat16
-    )
-    local_terms = jnp.einsum("hts,shp->thp", mixing, u_block, preferred_element_type=jnp.float32)
-    carried = jnp.exp(cumulative)[:, :, None] * jnp.einsum(
-        "tn,hpn->thp", c_block.astype(jnp.float32), carry_state, precision=lax.Precision.HIGHEST
-    )
-    ending = cumulative[-1]
-    weights = jnp.exp(ending[None, :] - cumulative)
-    scaled = weights[:, :, None] * u_block.astype(jnp.float32)
-    new_state = jnp.exp(ending)[:, None, None] * carry_state + jnp.einsum(
-        "shp,sn->hpn", scaled, b_block.astype(jnp.float32), precision=lax.Precision.HIGHEST
-    )
-    return (new_state, local_terms + carried)
+def relay_states(decay, state, axis):
+    length = lax.axis_size(axis)
+    decay = from_behind(decay, axis, 1)
+    state = from_behind(state, axis, 1)
+    shift = 1
+    while shift < length:
+        decay_in = from_behind(decay, axis, shift)
+        state_in = from_behind(state, axis, shift)
+        state = decay[:, None, None] * state_in + state
+        decay = decay * decay_in
+        shift *= 2
+    return state
 
 
 def per_device(inner_tokens, state_inputs, step_raw, conv_inner, conv_state, head_rates, skip_gain):
@@ -75,30 +65,51 @@
     x_heads = inner_conv.reshape(context, heads_local, head_width)
     inputs = (x_heads.astype(jnp.float32) * step_size[:, :, None]).astype(jnp.bfloat16)
     block_count = context // SPAN
-    start_state = jnp.zeros((heads_local, head_width, state_width), jnp.float32)
-    final_state, outputs = lax.scan(
-        block_terms,
-        start_state,
-        (
-            c_rows.reshape(block_count, SPAN, state_width),
-            b_rows.reshape(block_count, SPAN, state_width),
-            inputs.reshape(block_count, SPAN, heads_local, head_width),
-            log_decay.reshape(block_count, SPAN, heads_local),
-        ),
+
+    c_blocks = c_rows.reshape(block_count, SPAN, state_width)
+    b_blocks = b_rows.reshape(block_count, SPAN, state_width)
+    u_blocks = inputs.reshape(block_count, SPAN, heads_local, head_width)
+    cumulative = jnp.cumsum(log_decay.reshape(block_count, SPAN, heads_local), axis=1)
+    ending = cumulative[:, -1, :]
+
+    weights = jnp.exp(ending[:, None, :] - cumulative)
+    scaled = weights[:, :, :, None] * u_blocks.astype(jnp.float32)
+    block_states = jnp.einsum(
+        "bshp,bsn->bhpn", scaled, b_blocks.astype(jnp.float32), precision=lax.Precision.HIGHEST
     )
-    running = jnp.cumsum(log_decay, axis=0)
-    device_decay = jnp.exp(running[-1])
+    block_decay = jnp.exp(ending)
+    entering = []
+    running = jnp.zeros_like(block_states[0])
+    decay_before = []
+    running_decay = jnp.ones_like(block_decay[0])
+    for k in range(block_count):
+        entering.append(running)
+        decay_before.append(running_decay)
+        running = block_decay[k][:, None, None] * running + block_states[k]
+        running_decay = running_decay * block_decay[k]
+    incoming = relay_states(running_decay, running, "ctx")
 
-    def relay(position, arriving):
-        return from_behind(device_decay[:, None, None] * arriving + final_state, "ctx", 1)
+    inner_scores = jnp.einsum("btn,bsn->bts", c_blocks, b_blocks, preferred_element_type=jnp.float32)
+    across = cumulative.transpose(0, 2, 1)
+    spread = across[:, :, :, None] - across[:, :, None, :]
+    places = jnp.arange(SPAN)
+    causal = places[:, None] >= places[None, :]
+    mixing = (
+        inner_scores[:, None] * jnp.exp(jnp.where(causal[None, None], spread, -jnp.inf))
+    ).astype(jnp.bfloat16)
+    local_terms = jnp.einsum(
+        "bhts,bshp->bthp", mixing, u_blocks, preferred_element_type=jnp.float32
+    )
 
-    incoming = lax.fori_loop(0, lax.axis_size("ctx") - 1, relay, jnp.zeros_like(final_state))
-    carried = jnp.exp(running)[:, :, None] * jnp.einsum(
-        "tn,hpn->thp", c_rows.astype(jnp.float32), incoming, precision=lax.Precision.HIGHEST
+    entering_all = jnp.stack(entering) + jnp.stack(decay_before)[:, :, None, None] * incoming[None]
+    carried = jnp.exp(cumulative)[:, :, :, None] * jnp.einsum(
+        "btn,bhpn->bthp",
+        c_blocks.astype(jnp.float32),
+        entering_all,
+        precision=lax.Precision.HIGHEST,
     )
     summed = (
-        outputs.reshape(context, heads_local, head_width)
-        + carried
+        (local_terms + carried).reshape(context, heads_local, head_width)
         + skip_gain[None, :, None] * x_heads.astype(jnp.float32)
     )
     regrouped = summed.astype(jnp.bfloat16).reshape(context, channels)

time: 1110 us -> 446 us (0.40)
  waiting for transfers between devices: 556 us -> 173 us
  local copies, waits for them, and re-layouts: 324 us -> 68.8 us
  blocking collectives: 36.9 us -> 61.3 us
  starting transfers between devices: 73.4 us -> 49.3 us
  matrix products: 49.4 us -> 33.8 us
    ppermute x32 -> x12, waiting for transfers between devices: 497 us -> 114 us  [from_behind(): return lax.ppermute(value, axis, pairs)]
    dynamic_update_slice x16 -> x0, local copies, waits for them, and re-layouts: 251 us -> none  [per_device(): lax.scan(block_terms, start_state, (c_rows.reshape(block_count, SPAN, sta...]
    all_to_all x1, blocking collectives: 36.9 us -> 61.3 us  [per_device(): lax.all_to_all(regrouped, 'head', split_axis=0, concat_axis=1, tiled=True)]
    ppermute x32 -> x12, starting transfers between devices: 63.7 us -> 39.6 us  [from_behind(): return lax.ppermute(value, axis, pairs)]
    unnamed x21 -> x41, local copies, waits for them, and re-layouts: 16.5 us -> 34.8 us
    add x0 -> x1, local copies, waits for them, and re-layouts: none -> 16.9 us  [per_device(): local_terms + carried]
    dot_general x33 -> x4, matrix products: 49.4 us -> 33.8 us  [the longest x1 12.8 us: per_device(): jnp.einsum('bshp,bsn->bhpn', scaled, b_blocks.astype(jnp.float32), precis...]
    all_to_all x3 -> x2, local copies, waits for them, and re-layouts: 20.9 us -> 8.4 us  [per_device(): lax.all_to_all(regrouped, 'head', split_axis=0, concat_axis=1, tiled=True)]
  transfers between devices with their start and end apart: 35 -> 15, of which waited for: 35 -> 12; matrix products, arithmetic and copies ran while one was open for 2% -> 8% of each run, Pallas kernels for 0% -> 0%
where the time goes in v1:
time: 446 us; the launch traced here: 442 us
  waiting for transfers between devices  173 us (39%)
  local copies, waits for them, and re-layouts  68.8 us (15%)
  blocking collectives  61.3 us (14%)
  starting transfers between devices  49.3 us (11%)
  other arithmetic  40.6 us (9%)
  matrix products  33.8 us (8%)
  between operations  14.4 us (3%)
    ppermute x12, waiting for transfers between devices, from_behind(): return lax.ppermute(value, axis, pairs)  114 us
    all_to_all x1, blocking collectives, per_device(): lax.all_to_all(regrouped, 'head', split_axis=0, concat_axis=1, tiled=True)  61.3 us
    ppermute x12, starting transfers between devices, from_behind(): return lax.ppermute(value, axis, pairs)  39.6 us
    unnamed x41, local copies, waits for them, and re-layouts  34.8 us
    all_gather x1, waiting for transfers between devices, per_device(): state_whole = lax.all_gather(state_inputs, 'head', axis=0, tiled=True)  31.2 us
    all_to_all x1, waiting for transfers between devices, per_device(): lax.all_to_all(inner_tokens, 'head', split_axis=1, concat_axis=0, tiled=T...  28.5 us
    add x1, local copies, waits for them, and re-layouts, per_device(): local_terms + carried  16.9 us
    dot_general x1, matrix products, per_device(): jnp.einsum('bshp,bsn->bhpn', scaled, b_blocks.astype(jnp.float32), precis...  12.8 us
  transfers between devices with their start and end apart: 15, of which 12 were waited for; matrix products, arithmetic and copies ran while one was open for 8% of the time, Pallas kernels for 0%

profile of v1, /device:TPU:6, one launch (start us, length us, event | category | flops | bytes accessed | tf_op | source)
XLA Modules:
  0.0 441.7 jit_solution(12077091317954784458)
XLA Ops:
  6.5 1.5 all_to_all.42
  8.1 4.5 %all-to-all-start.1 = ((bf16[512,4,20]{0,2,1:T(8,128)(2,1)}), bf16[512,4,20]{0,2,1:T(8,128)(2,1)S(1)}, u32[]{:S(2)}, u32[]{:S(2)}) async-start(bf16[512,4,20]{0,2,1:T(8,128)(2,1)} %all_to_all.42), calls=%async_computation.1 | async-start | bytes 196608 | tf_op jit(solution)/shard_map/all_to_all | solution.py:45
  12.5 7.9 %copy.70 = bf16[512,5120]{0,1:T(8,128)(2,1)} copy(bf16[512,5120]{1,0:T(8,128)(2,1)} %param.7) | data formatting | bytes 10485760 | tf_op args[0]
  20.5 5.2 %all-to-all-start = ((bf16[512,4,1280]{0,2,1:T(8,128)(2,1)}), bf16[512,4,1280]{0,2,1:T(8,128)(2,1)}, u32[]{:S(2)}, u32[]{:S(2)}) async-start(bf16[512,4,1280]{0,2,1:T(8,128)(2,1)} %bitcast.164), calls=%async_computation | async-start | bytes 10485760 | tf_op jit(solution)/shard_map/all_to_all | solution.py:44
  25.8 0.9 copy.72
  27.0 0.2 multiply_bitcast_fusion
  27.2 4.6 %reduce-window.6 = f32[8,20,2,128]{3,1,2,0:T(8,128)S(1)} reduce-window(f32[8,20,2,128]{3,1,2,0:T(8,128)S(1)} %copy.76, f32[]{:T(128)} %constant.8.clone.1), window={size=1x1x1x128 pad=0_0x0_0x0_0x127_0}, to_apply=%region_0.1 | reduce-window | flops 5201920 | bytes 327684 | tf_op jit(solution)/shard_map/reduce-window
  32.0 0.2 copy.77
  32.5 0.2 copy.92
  32.7 0.1 copy.84
  32.9 0.6 slice_multiply_fusion
  33.6 31.2 %all-gather.2.cloned.1.call-done = bf16[2048,256]{0,1:T(8,128)(2,1)} async-done(((bf16[512,256]{0,1:T(8,128)(2,1)}), bf16[2048,256]{0,1:T(8,128)(2,1)}) %all-gather.2.cloned.1.call-update) | async-done | bytes 1048592 | tf_op jit(solution)/shard_map/all_gather | solution.py:52
  64.8 0.9 slice.181
  65.7 28.5 %all-to-all-done = bf16[512,4,1280]{0,2,1:T(8,128)(2,1)} async-done(((bf16[512,4,1280]{0,2,1:T(8,128)(2,1)}), bf16[512,4,1280]{0,2,1:T(8,128)(2,1)}, u32[]{:S(2)}, u32[]{:S(2)}) %all-to-all-start) | async-done | bytes 5242912 | tf_op jit(solution)/shard_map/all_to_all | solution.py:44
  94.2 3.4 copy.94
  97.6 0.2 slice.180
  97.9 4.0 collective-permute-start
  101.9 0.2 convert_element_type.69
  102.2 1.4 convert_element_type.60
  103.6 10.3 %collective-permute-done = bf16[3,1536]{0,1:T(8,128)(2,1)S(1)} collective-permute-done((bf16[3,1536]{0,1:T(8,128)(2,1)S(1)}, bf16[3,1536]{0,1:T(8,128)(2,1)S(1)}, u32[]{:S(2)}, u32[]{:S(2)}) %collective-permute-start) | collective-permute-done | bytes 9248 | tf_op jit(solution)/shard_map/ppermute | solution.py:13
  113.9 11.0 %fusion.21 = f32[2048,1280]{0,1:T(8,128)S(1)} fusion(f32[2048,1280]{0,1:T(8,128)S(1)} %convert_element_type.60, f32[1280]{0:T(1024)S(1)} %get-tuple-element.8, f32[3,1280]{0,1:T(8,128)S(1)} %slice_convert_fusion, f32[1280]{0:T(1024)S(1)} %get-tuple-element.9, f32[1280]{0:T(1024)S(1)} %get-tuple-element.6, f32[1280]{0:T(1024)S(1)} %get-tuple-element.7, ...), kind=kLoop, calls=%fused_computation.33 | loop fusion | flops 44564480 | bytes 21012480 | tf_op jit(solution)/shard_map/convert_element_type | solution.py:66
  124.9 9.3 %copy.95 = f32[160,8,8,256]{3,2,1,0:T(8,128)} copy(f32[160,8,8,256]{3,1,2,0:T(8,128)S(1)} %bitcast.154) | data formatting | bytes 20971520
  134.3 2.2 multiply_convert_fusion.4
  136.6 0.3 copy.75
  136.9 11.7 %convert_multiply_fusion = (f32[8,256,20,64]{1,0,3,2:T(8,128)}, bf16[8,256,20,64]{1,0,3,2:T(8,128)(2,1)}) fusion(f32[8,256,20]{1,0,2:T(8,128)S(1)} %subtract_exponential_fusion, f32[8,256,20,64]{1,0,3,2:T(8,128)} %bitcast.159, f32[8,256,20]{1,0,2:T(8,128)S(1)} %get-tuple-element.27), kind=kLoop, calls=%fused_computation.25 | loop fusion | flops 10485760 | bytes 26542080 | tf_op jit(solution)/shard_map/mul | solution.py:76
  148.6 12.8 %fusion.15 = f32[8,20,64,128]{3,2,1,0:T(8,128)S(1)} fusion(bf16[8,256,128,1]{2,1,3,0:T(8,128)(2,1)S(1)} %bitcast.170, f32[8,256,20,64]{1,0,3,2:T(8,128)} %get-tuple-element.22), kind=kOutput, calls=%fused_computation.22 | convolution fusion | flops 4026531840 | bytes 16252928 | tf_op jit(solution)/shard_map/bshp,bsn->bhpn/dot_general | solution.py:77
  161.5 2.3 copy-done.1
  163.7 0.4 fusion.35
  164.2 1.9 collective-permute-start.6
  166.1 16.8 %collective-permute-done.6 = f32[20,64,128]{2,1,0:T(8,128)S(1)} collective-permute-done((f32[20,64,128]{2,1,0:T(8,128)S(1)}, f32[20,64,128]{2,1,0:T(8,128)S(1)}, u32[]{:S(2)}, u32[]{:S(2)}) %collective-permute-start.6) | collective-permute-done | bytes 655392 | tf_op jit(solution)/shard_map/ppermute | solution.py:13
  182.9 1.9 collective-permute-start.7
  184.9 1.9 collective-permute-start.1
  186.8 14.1 %collective-permute-done.1 = f32[20]{0:T(128)S(1)} collective-permute-done((f32[20]{0:T(128)S(1)}, f32[20]{0:T(128)S(1)}, u32[]{:S(2)}, u32[]{:S(2)}) %collective-permute-start.1) | collective-permute-done | bytes 112 | tf_op jit(solution)/shard_map/ppermute | solution.py:13
  201.1 1.9 collective-permute-start.8
  203.2 0.9 broadcast_dynamic-update-slice_fusion
  204.1 1.9 collective-permute-start.2
  206.1 13.9 %collective-permute-done.2 = f32[20]{0:T(128)S(1)} collective-permute-done((f32[20]{0:T(128)S(1)}, f32[20]{0:T(128)S(1)}, u32[]{:S(2)}, u32[]{:S(2)}) %collective-permute-start.2) | collective-permute-done | bytes 112 | tf_op jit(solution)/shard_map/ppermute | solution.py:13
  220.0 10.2 %collective-permute-start.3 = (f32[20]{0:T(128)S(1)}, f32[20]{0:T(128)S(1)}, u32[]{:S(2)}, u32[]{:S(2)}) collective-permute-start(f32[20]{0:T(128)S(1)} %mul.461), channel_id=1, source_target_pairs={{0,8},{4,12},{8,16},{12,20},{16,24},{20,28},{24,32},{28,36},{32,40... | collective-permute-start | bytes 248 | tf_op jit(solution)/shard_map/ppermute | solution.py:13
  230.2 4.0 collective-permute-done.3
  234.3 6.6 %collective-permute-start.4 = (f32[20]{0:T(128)S(1)}, f32[20]{0:T(128)S(1)}, u32[]{:S(2)}, u32[]{:S(2)}) collective-permute-start(f32[20]{0:T(128)S(1)} %mul.462), channel_id=1, source_target_pairs={{0,16},{4,20},{8,24},{12,28},{16,32},{20,36},{24,40},{28,44},{32,4... | collective-permute-start | bytes 248 | tf_op jit(solution)/shard_map/ppermute | solution.py:13
  241.0 3.6 collective-permute-done.4
  244.6 1.3 collective-permute-start.5
  245.8 0.7 stack.5
  246.6 4.1 collective-permute-done.5
  250.6 0.3 copy.74
  250.9 0.4 fusion.55
  251.4 0.9 multiply_add_fusion.3
  252.3 5.3 %collective-permute-start.9 = (f32[20,64,128]{2,1,0:T(8,128)S(1)}, f32[20,64,128]{2,1,0:T(8,128)S(1)}, u32[]{:S(2)}, u32[]{:S(2)}) collective-permute-start(f32[20,64,128]{2,1,0:T(8,128)S(1)} %multiply_add_fusion.3), channel_id=1, source_target_pairs={{0,16},{4,20},{8,24},{12,28},{16,32},{20,36},{24,40},{28,44},{32,4... | collective-permute-start | bytes 1966088 | tf_op jit(solution)/shard_map/ppermute | solution.py:13
  257.7 12.6 %fusion = f32[8,20,64,256]{3,2,1,0:T(8,128)S(1)} fusion(f32[8,20,256]{2,1,0:T(8,128)S(1)} %copy.80, f32[8,256,256]{2,1,0:T(8,128)S(1)} %fusion.55, pred[256,256]{1,0:T(8,128)(4,1)S(1)} %iota_compare_fusion, bf16[8,256,20,64]{1,0,3,2:T(8,128)(2,1)} %get-tuple-element.23), kind=kOutput, calls=%fused_computation.1 | convolution fusion | flops 1384120320 | bytes 18055168 | tf_op jit(solution)/shard_map/bhts,bshp->bthp/dot_general | solution.py:100
  270.5 14.8 %collective-permute-done.9 = f32[20,64,128]{2,1,0:T(8,128)S(1)} collective-permute-done((f32[20,64,128]{2,1,0:T(8,128)S(1)}, f32[20,64,128]{2,1,0:T(8,128)S(1)}, u32[]{:S(2)}, u32[]{:S(2)}) %collective-permute-start.9) | collective-permute-done | bytes 655392 | tf_op jit(solution)/shard_map/ppermute | solution.py:13
  285.4 1.3 collective-permute-start.10
  286.7 0.2 constant_dynamic-update-slice_fusion.2
  287.1 0.2 constant_dynamic-update-slice_fusion.1
  287.3 15.7 %collective-permute-done.10 = f32[20,64,128]{2,1,0:T(8,128)S(1)} collective-permute-done((f32[20,64,128]{2,1,0:T(8,128)S(1)}, f32[20,64,128]{2,1,0:T(8,128)S(1)}, u32[]{:S(2)}, u32[]{:S(2)}) %collective-permute-start.10) | collective-permute-done | bytes 655392 | tf_op jit(solution)/shard_map/ppermute | solution.py:13
  303.1 1.3 collective-permute-start.11
  304.6 0.2 constant_dynamic-update-slice_fusion
  304.9 16.4 %collective-permute-done.11 = f32[20,64,128]{2,1,0:T(8,128)S(1)} collective-permute-done((f32[20,64,128]{2,1,0:T(8,128)S(1)}, f32[20,64,128]{2,1,0:T(8,128)S(1)}, u32[]{:S(2)}, u32[]{:S(2)}) %collective-permute-start.11) | collective-permute-done | bytes 655392 | tf_op jit(solution)/shard_map/ppermute | solution.py:13
  321.4 8.0 %bitcast_add_fusion = f32[8,256,20,64]{1,3,2,0:T(8,128)} fusion(f32[8,20,64,256]{3,2,1,0:T(8,128)S(1)} %fusion, f32[8,256,20]{1,2,0:T(8,128)S(1)} %copy.83, bf16[8,256,128,1]{2,1,3,0:T(8,128)(2,1)S(1)} %bitcast.173, f32[8,20,64,128]{3,2,1,0:T(8,128)S(1)} %add_dynamic-update-slice_fusion, f32[20,64,128]{2,1,0:T(8,128)S(1)} %multiply_add_fusion, ...), kind=kOutput, calls=%fused_computation.21 | convolution fusion | flops 4034396160 | bytes 27558528 | tf_op jit(solution)/shard_map/btn,bhpn->bthp/dot_general | solution.py:105
  329.5 16.9 %copy.87 = f32[8,256,20,64]{1,0,3,2:T(8,128)} copy(f32[8,256,20,64]{1,3,2,0:T(8,128)} %bitcast_add_fusion) | data formatting | bytes 20971520 | tf_op jit(solution)/shard_map/add | solution.py:112
  346.3 13.5 %copy.96 = f32[160,8,8,256]{3,1,2,0:T(8,128)} copy(f32[160,8,8,256]{3,2,1,0:T(8,128)} %bitcast.161) | data formatting | bytes 20971520
  359.8 5.1 %add_convert_fusion = bf16[2048,1280]{0,1:T(8,128)(2,1)S(1)} fusion(f32[2048,1280]{0,1:T(8,128)} %bitcast.160, f32[2048,1280]{0,1:T(8,128)S(1)} %bitcast.156, f32[1280]{0:T(1024)S(1)} %mul.494), kind=kLoop, calls=%fused_computation.24 | loop fusion | flops 7864320 | bytes 26219520 | tf_op jit(solution)/shard_map/convert_element_type | solution.py:115
  364.9 0.5 copy.105
  365.4 61.3 %all_to_all.51 = bf16[4,512,1280]{1,2,0:T(8,128)(2,1)} all-to-all(bf16[4,512,1280]{1,2,0:T(8,128)(2,1)S(1)} %bitcast.165), channel_id=1, replica_groups=mesh['run'=2,'ctx'=32,'head'=4] {'head'}, dimensions={0} | all-to-all | bytes 10485760 | tf_op jit(solution)/shard_map/all_to_all | solution.py:116
  426.7 7.9 %copy.89 = bf16[512,5120]{1,0:T(8,128)(2,1)} copy(bf16[512,5120]{0,1:T(8,128)(2,1)} %bitcast.166) | data formatting | bytes 10485760 | tf_op jit(solution)/shard_map/all_to_all | solution.py:116
  (83 shorter events, 2.7 us)
Async XLA Ops:
  8.1 12.4 %all-to-all-start.1 = ((bf16[512,4,20]{0,2,1:T(8,128)(2,1)}), bf16[512,4,20]{0,2,1:T(8,128)(2,1)S(1)}, u32[]{:S(2)}, u32[]{:S(2)}) async-start(bf16[512,4,20]{0,2,1:T(8,128)(2,1)} %all_to_all.42), calls=%async_computation.1 | async-start | bytes 196608 | tf_op jit(solution)/shard_map/all_to_all | solution.py:45
  20.5 5.3 %copy-start.3 = (bf16[512,256]{1,0:T(8,128)(2,1)S(1)}, bf16[512,256]{1,0:T(8,128)(2,1)}, u32[]{:S(2)}) copy-start(bf16[512,256]{1,0:T(8,128)(2,1)} %param.8) | copy-start | bytes 786436
  20.5 6.2 %copy-start.4 = (f32[5,1280]{1,0:T(8,128)S(1)}, f32[5,1280]{1,0:T(8,128)}, u32[]{:S(2)}) copy-start(f32[5,1280]{1,0:T(8,128)} %param.10) | copy-start | bytes 76804
  20.5 6.3 %copy-start.6 = (f32[2,20]{1,0:T(2,128)S(1)}, f32[2,20]{1,0:T(2,128)}, u32[]{:S(2)}) copy-start(f32[2,20]{1,0:T(2,128)} %param.12) | copy-start | bytes 484
  20.5 6.3 %copy-start.5 = (f32[5,256]{1,0:T(8,128)S(1)}, f32[5,256]{1,0:T(8,128)}, u32[]{:S(2)}) copy-start(f32[5,256]{1,0:T(8,128)} %param.11) | copy-start | bytes 15364
  20.5 73.7 %all-to-all-start = ((bf16[512,4,1280]{0,2,1:T(8,128)(2,1)}), bf16[512,4,1280]{0,2,1:T(8,128)(2,1)}, u32[]{:S(2)}, u32[]{:S(2)}) async-start(bf16[512,4,1280]{0,2,1:T(8,128)(2,1)} %bitcast.164), calls=%async_computation | async-start | bytes 10485760 | tf_op jit(solution)/shard_map/all_to_all | solution.py:44
  25.7 39.1 %all-gather.2.cloned.1.call-start = ((), (), s32[]{:S(2)}) async-start(), calls=%async_computation.3 | async-start | bytes 1310720 | tf_op jit(solution)/shard_map/all_gather | solution.py:52
  94.2 7.7 %copy-start.2 = (bf16[2048,256]{0,1:T(8,128)(2,1)S(1)}, bf16[2048,256]{0,1:T(8,128)(2,1)}, u32[]{:S(2)}) copy-start(bf16[2048,256]{0,1:T(8,128)(2,1)} %all-gather.2.cloned.1.call-done) | copy-start | bytes 3145732
  97.9 16.0 %collective-permute-start = (bf16[3,1536]{0,1:T(8,128)(2,1)S(1)}, bf16[3,1536]{0,1:T(8,128)(2,1)S(1)}, u32[]{:S(2)}, u32[]{:S(2)}) collective-permute-start(bf16[3,1536]{0,1:T(8,128)(2,1)S(1)} %pad_maximum_fusion.2), channel_id=1, source_target_pairs={{0,4},{4,8},{8,12},{12,16},{16,20},{20,24},{24,28},{28,32},{32,36}... | collective-permute-start | bytes 27656 | tf_op jit(solution)/shard_map/ppermute | solution.py:13
  124.9 9.3 %copy-start = (f32[2048,1280]{0,1:T(8,128)}, f32[2048,1280]{0,1:T(8,128)S(1)}, u32[]{:S(2)}) copy-start(f32[2048,1280]{0,1:T(8,128)S(1)} %fusion.21) | copy-start | bytes 31457284
  161.5 2.3 copy-start.1
  161.5 41.5 %copy-start.10 = (f32[20]{0:T(128)S(1)}, f32[20]{0:T(128)}, u32[]{:S(2)}) copy-start(f32[20]{0:T(128)} %param.13) | copy-start | bytes 244
  164.2 18.8 %collective-permute-start.6 = (f32[20,64,128]{2,1,0:T(8,128)S(1)}, f32[20,64,128]{2,1,0:T(8,128)S(1)}, u32[]{:S(2)}, u32[]{:S(2)}) collective-permute-start(f32[20,64,128]{2,1,0:T(8,128)S(1)} %fusion.35), channel_id=1, source_target_pairs={{0,4},{4,8},{8,12},{12,16},{16,20},{20,24},{24,28},{28,32},{32,36}... | collective-permute-start | bytes 1966088 | tf_op jit(solution)/shard_map/ppermute | solution.py:13
  182.9 18.0 %collective-permute-start.7 = (f32[20,64,128]{2,1,0:T(8,128)S(1)}, f32[20,64,128]{2,1,0:T(8,128)S(1)}, u32[]{:S(2)}, u32[]{:S(2)}) collective-permute-start(f32[20,64,128]{2,1,0:T(8,128)S(1)} %collective-permute-done.6), channel_id=1, source_target_pairs={{0,4},{4,8},{8,12},{12,16},{16,20},{20,24},{24,28},{28,32},{32,36}... | collective-permute-start | bytes 1966088 | tf_op jit(solution)/shard_map/ppermute | solution.py:13
  184.9 16.1 %collective-permute-start.1 = (f32[20]{0:T(128)S(1)}, f32[20]{0:T(128)S(1)}, u32[]{:S(2)}, u32[]{:S(2)}) collective-permute-start(f32[20]{0:T(128)S(1)} %get-tuple-element.43), channel_id=1, source_target_pairs={{0,4},{4,8},{8,12},{12,16},{16,20},{20,24},{24,28},{28,32},{32,36}... | collective-permute-start | bytes 248 | tf_op jit(solution)/shard_map/ppermute | solution.py:13
  201.1 50.3 %collective-permute-start.8 = (f32[20,64,128]{2,1,0:T(8,128)S(1)}, f32[20,64,128]{2,1,0:T(8,128)S(1)}, u32[]{:S(2)}, u32[]{:S(2)}) collective-permute-start(f32[20,64,128]{2,1,0:T(8,128)S(1)} %multiply_add_fusion.4), channel_id=1, source_target_pairs={{0,8},{4,12},{8,16},{12,20},{16,24},{20,28},{24,32},{28,36},{32,40... | collective-permute-start | bytes 1966088 | tf_op jit(solution)/shard_map/ppermute | solution.py:13
  204.1 15.9 %collective-permute-start.2 = (f32[20]{0:T(128)S(1)}, f32[20]{0:T(128)S(1)}, u32[]{:S(2)}, u32[]{:S(2)}) collective-permute-start(f32[20]{0:T(128)S(1)} %collective-permute-done.1), channel_id=1, source_target_pairs={{0,4},{4,8},{8,12},{12,16},{16,20},{20,24},{24,28},{28,32},{32,36}... | collective-permute-start | bytes 248 | tf_op jit(solution)/shard_map/ppermute | solution.py:13
  220.0 20.9 %copy-start.9 = (f32[20]{0:T(128)}, f32[20]{0:T(128)S(1)}, u32[]{:S(2)}) copy-start(f32[20]{0:T(128)S(1)} %mul.461) | copy-start | bytes 244
  220.0 14.3 %collective-permute-start.3 = (f32[20]{0:T(128)S(1)}, f32[20]{0:T(128)S(1)}, u32[]{:S(2)}, u32[]{:S(2)}) collective-permute-start(f32[20]{0:T(128)S(1)} %mul.461), channel_id=1, source_target_pairs={{0,8},{4,12},{8,16},{12,20},{16,24},{20,28},{24,32},{28,36},{32,40... | collective-permute-start | bytes 248 | tf_op jit(solution)/shard_map/ppermute | solution.py:13
  234.3 16.3 %copy-start.7 = (f32[20]{0:T(128)}, f32[20]{0:T(128)S(1)}, u32[]{:S(2)}) copy-start(f32[20]{0:T(128)S(1)} %mul.462) | copy-start | bytes 244
  234.3 10.3 %collective-permute-start.4 = (f32[20]{0:T(128)S(1)}, f32[20]{0:T(128)S(1)}, u32[]{:S(2)}, u32[]{:S(2)}) collective-permute-start(f32[20]{0:T(128)S(1)} %mul.462), channel_id=1, source_target_pairs={{0,16},{4,20},{8,24},{12,28},{16,32},{20,36},{24,40},{28,44},{32,4... | collective-permute-start | bytes 248 | tf_op jit(solution)/shard_map/ppermute | solution.py:13
  244.6 6.1 %collective-permute-start.5 = (f32[20]{0:T(128)S(1)}, f32[20]{0:T(128)S(1)}, u32[]{:S(2)}, u32[]{:S(2)}) collective-permute-start(f32[20]{0:T(128)S(1)} %mul.463), channel_id=1, source_target_pairs={{0,32},{4,36},{8,40},{12,44},{16,48},{20,52},{24,56},{28,60},{32,6... | collective-permute-start | bytes 248 | tf_op jit(solution)/shard_map/ppermute | solution.py:13
  251.4 18.9 %slice-start.3 = ((s8[5242880]{0:T(1024)(128)(4,1)}), s8[4194304]{0:T(1024)(128)(4,1)S(1)}, s32[]{:S(2)}) async-start(s8[5242880]{0:T(1024)(128)(4,1)} %bitcast.157), calls=%async_computation.7 | async-start | bytes 8388608
  251.4 18.9 %slice-start.5 = ((s8[5242880]{0:T(1024)(128)(4,1)}), s8[4194304]{0:T(1024)(128)(4,1)S(1)}, s32[]{:S(2)}) async-start(s8[5242880]{0:T(1024)(128)(4,1)} %bitcast.168), calls=%async_computation.9 | async-start | bytes 8388608
  252.3 33.0 %collective-permute-start.9 = (f32[20,64,128]{2,1,0:T(8,128)S(1)}, f32[20,64,128]{2,1,0:T(8,128)S(1)}, u32[]{:S(2)}, u32[]{:S(2)}) collective-permute-start(f32[20,64,128]{2,1,0:T(8,128)S(1)} %multiply_add_fusion.3), channel_id=1, source_target_pairs={{0,16},{4,20},{8,24},{12,28},{16,32},{20,36},{24,40},{28,44},{32,4... | collective-permute-start | bytes 1966088 | tf_op jit(solution)/shard_map/ppermute | solution.py:13
  257.7 12.6 %slice-start.4 = ((s8[5242880]{0:T(1024)(128)(4,1)}), s8[1048576]{0:T(1024)(128)(4,1)S(1)}, s32[]{:S(2)}) async-start(s8[5242880]{0:T(1024)(128)(4,1)} %bitcast.157), calls=%async_computation.8 | async-start | bytes 2097152
  257.7 12.6 %slice-start.6 = ((s8[5242880]{0:T(1024)(128)(4,1)}), s8[1048576]{0:T(1024)(128)(4,1)S(1)}, s32[]{:S(2)}) async-start(s8[5242880]{0:T(1024)(128)(4,1)} %bitcast.168), calls=%async_computation.10 | async-start | bytes 2097152
  257.7 27.6 %copy-start.8 = (f32[20]{0:T(128)S(1)}, f32[20]{0:T(128)}, u32[]{:S(2)}) copy-start(f32[20]{0:T(128)} %copy-done.7) | copy-start | bytes 244
  285.4 17.5 %collective-permute-start.10 = (f32[20,64,128]{2,1,0:T(8,128)S(1)}, f32[20,64,128]{2,1,0:T(8,128)S(1)}, u32[]{:S(2)}, u32[]{:S(2)}) collective-permute-start(f32[20,64,128]{2,1,0:T(8,128)S(1)} %multiply_add_fusion.2), channel_id=1, source_target_pairs={{0,32},{4,36},{8,40},{12,44},{16,48},{20,52},{24,56},{28,60},{32,6... | collective-permute-start | bytes 1966088 | tf_op jit(solution)/shard_map/ppermute | solution.py:13
  303.1 18.2 %collective-permute-start.11 = (f32[20,64,128]{2,1,0:T(8,128)S(1)}, f32[20,64,128]{2,1,0:T(8,128)S(1)}, u32[]{:S(2)}, u32[]{:S(2)}) collective-permute-start(f32[20,64,128]{2,1,0:T(8,128)S(1)} %multiply_add_fusion.1), channel_id=1, source_target_pairs={{0,64},{4,68},{8,72},{12,76},{16,80},{20,84},{24,88},{28,92},{32,9... | collective-permute-start | bytes 1966088 | tf_op jit(solution)/shard_map/ppermute | solution.py:13
  329.4 30.3 %slice-start = ((s8[10485760]{0:T(1024)(128)(4,1)}), s8[4194304]{0:T(1024)(128)(4,1)S(1)}, s32[]{:S(2)}) async-start(s8[10485760]{0:T(1024)(128)(4,1)} %bitcast.155), calls=%async_computation.4 | async-start | bytes 8388608
  329.4 30.3 %slice-start.1 = ((s8[10485760]{0:T(1024)(128)(4,1)}), s8[4194304]{0:T(1024)(128)(4,1)S(1)}, s32[]{:S(2)}) async-start(s8[10485760]{0:T(1024)(128)(4,1)} %bitcast.155), calls=%async_computation.5 | async-start | bytes 8388608
  346.3 13.5 %slice-start.2 = ((s8[10485760]{0:T(1024)(128)(4,1)}), s8[2097152]{0:T(1024)(128)(4,1)S(1)}, s32[]{:S(2)}) async-start(s8[10485760]{0:T(1024)(128)(4,1)} %bitcast.155), calls=%async_computation.6 | async-start | bytes 4194304
Sparse Core Ops, SparseCore 0:
  28.3 36.4 all-gather.1

commit v2 on v1

--- a/solution.py
+++ b/solution.py
@@ -27,16 +27,30 @@
 
 def relay_states(decay, state, axis):
     length = lax.axis_size(axis)
-    decay = from_behind(decay, axis, 1)
-    state = from_behind(state, axis, 1)
-    shift = 1
+    heads = decay.shape[0]
+    size = state.size
+    pad = (-heads) % 128
+
+    def pack(d, s):
+        return jnp.concatenate([s.reshape(-1), jnp.pad(d, (0, pad))])
+
+    def unpack(payload):
+        return payload[size : size + heads], payload[:size].reshape(heads, -1)
+
+    flat_state = state.reshape(heads, -1)
+    arrived = from_behind(pack(decay, flat_state), axis, 1)
+    excl_decay, excl_state = unpack(arrived)
+    incl_state = decay[:, None] * excl_state + flat_state
+    incl_decay = decay * excl_decay
+    shift = 2
     while shift < length:
-        decay_in = from_behind(decay, axis, shift)
-        state_in = from_behind(state, axis, shift)
-        state = decay[:, None, None] * state_in + state
-        decay = decay * decay_in
+        got_decay, got_state = unpack(from_behind(pack(incl_decay, incl_state), axis, shift))
+        excl_state = excl_decay[:, None] * got_state + excl_state
+        incl_state = incl_decay[:, None] * got_state + incl_state
+        excl_decay = excl_decay * got_decay
+        incl_decay = incl_decay * got_decay
         shift *= 2
-    return state
+    return excl_state.reshape(state.shape)
 
 
 def per_device(inner_tokens, state_inputs, step_raw, conv_inner, conv_state, head_rates, skip_gain):
@@ -100,20 +114,29 @@
     local_terms = jnp.einsum(
         "bhts,bshp->bthp", mixing, u_blocks, preferred_element_type=jnp.float32
     )
+    c_float = c_blocks.astype(jnp.float32)
+    entering_intra = jnp.stack(entering).reshape(block_count, channels, state_width)
+    carried_intra = jnp.einsum(
+        "btn,bkn->btk", c_float, entering_intra, precision=lax.Precision.HIGHEST
+    ).reshape(block_count, SPAN, heads_local, head_width)
+    decay_in = jnp.exp(cumulative)
+    known = (
+        local_terms
+        + decay_in[:, :, :, None] * carried_intra
+        + skip_gain[None, None, :, None] * u_x(x_heads, block_count)
+    )
 
-    entering_all = jnp.stack(entering) + jnp.stack(decay_before)[:, :, None, None] * incoming[None]
-    carried = jnp.exp(cumulative)[:, :, :, None] * jnp.einsum(
-        "btn,bhpn->bthp",
-        c_blocks.astype(jnp.float32),
-        entering_all,
-        precision=lax.Precision.HIGHEST,
-    )
-    summed = (
-        (local_terms + carried).reshape(context, heads_local, head_width)
-        + skip_gain[None, :, None] * x_heads.astype(jnp.float32)
-    )
+    carried_in = jnp.einsum(
+        "btn,kn->btk", c_float, incoming.reshape(channels, state_width), precision=lax.Precision.HIGHEST
+    ).reshape(block_count, SPAN, heads_local, head_width)
+    factor = decay_in * jnp.stack(decay_before)[:, None, :]
+    summed = known + factor[:, :, :, None] * carried_in
     regrouped = summed.astype(jnp.bfloat16).reshape(context, channels)
     return lax.all_to_all(regrouped, "head", split_axis=0, concat_axis=1, tiled=True)
+
+
+def u_x(x_heads, block_count):
+    return x_heads.astype(jnp.float32).reshape(block_count, SPAN, *x_heads.shape[1:])
 
 
 def solution(mesh):

time: 446 us -> 455 us (1.020)
  the two profiles are of different devices: /device:TPU:6 before, /device:TPU:102 now
where the time goes in v2:
time: 455 us; the launch traced here: 451 us
  waiting for transfers between devices  137 us (30%)
  local copies, waits for them, and re-layouts  107 us (24%)
  blocking collectives  62.3 us (14%)
  other arithmetic  52.8 us (12%)
  matrix products  52.3 us (11%)
  starting transfers between devices  26.2 us (6%)
  between operations  14.3 us (3%)
    ppermute x6, waiting for transfers between devices, from_behind(): return lax.ppermute(value, axis, pairs)  78 us
    all_to_all x1, blocking collectives, per_device(): lax.all_to_all(regrouped, 'head', split_axis=0, concat_axis=1, tiled=True)  62.3 us
    all_gather x1, waiting for transfers between devices, per_device(): state_whole = lax.all_gather(state_inputs, 'head', axis=0, tiled=True)  29.3 us
    all_to_all x1, waiting for transfers between devices, per_device(): lax.all_to_all(inner_tokens, 'head', split_axis=1, concat_axis=0, tiled=T...  28 us
    mul x24, local copies, waits for them, and re-layouts, per_device(): running = block_decay[k][:, None, None] * running + block_states[k]  26 us
    unnamed x44, local copies, waits for them, and re-layouts  22.8 us
    all_to_all x3, local copies, waits for them, and re-layouts, per_device(): lax.all_to_all(regrouped, 'head', split_axis=0, concat_axis=1, tiled=True)  20.7 us
    ppermute x6, starting transfers between devices, from_behind(): return lax.ppermute(value, axis, pairs)  16.5 us
  transfers between devices with their start and end apart: 9, of which 7 were waited for; matrix products, arithmetic and copies ran while one was open for 19% of the time, Pallas kernels for 0%

profile of v2, /device:TPU:102, one launch (start us, length us, event | category | flops | bytes accessed | tf_op | source)
XLA Modules:
  0.0 451.1 jit_solution(11123096979553055145)
XLA Ops:
  6.5 1.5 all_to_all.42
  8.1 4.5 all-to-all-start.1
  12.5 5.2 %copy.90 = bf16[64,4,8,1280]{3,2,0,1:T(8,128)(2,1)} copy(bf16[64,4,8,1280]{3,2,1,0:T(8,128)(2,1)} %bitcast.176) | data formatting | bytes 10485760 | tf_op jit(solution)/shard_map/all_to_all | solution.py:58
  18.3 5.2 %all-to-all-start = ((bf16[512,4,1280]{2,0,1:T(8,128)(2,1)}), bf16[512,4,1280]{2,0,1:T(8,128)(2,1)}, u32[]{:S(2)}, u32[]{:S(2)}) async-start(bf16[512,4,1280]{2,0,1:T(8,128)(2,1)} %bitcast.151), calls=%async_computation | async-start | bytes 10485760 | tf_op jit(solution)/shard_map/all_to_all | solution.py:58
  24.9 4.6 %reduce-window.6 = f32[8,20,2,128]{3,1,2,0:T(8,128)S(1)} reduce-window(f32[8,20,2,128]{3,1,2,0:T(8,128)S(1)} %copy.55, f32[]{:T(128)} %constant.9.clone.1), window={size=1x1x1x128 pad=0_0x0_0x0_0x127_0}, to_apply=%region_0.1 | reduce-window | flops 5201920 | bytes 327684 | tf_op jit(solution)/shard_map/reduce-window
  32.1 29.3 %all-gather.2.cloned.1.call-done = bf16[2048,256]{1,0:T(8,128)(2,1)} async-done(((bf16[512,256]{1,0:T(8,128)(2,1)}), bf16[2048,256]{1,0:T(8,128)(2,1)}) %all-gather.2.cloned.1.call-update) | async-done | bytes 1048592 | tf_op jit(solution)/shard_map/all_gather | solution.py:66
  62.1 1.4 convert_element_type.72
  63.5 28.0 %all-to-all-done = bf16[512,4,1280]{2,0,1:T(8,128)(2,1)} async-done(((bf16[512,4,1280]{2,0,1:T(8,128)(2,1)}), bf16[512,4,1280]{2,0,1:T(8,128)(2,1)}, u32[]{:S(2)}, u32[]{:S(2)}) %all-to-all-start) | async-done | bytes 5242912 | tf_op jit(solution)/shard_map/all_to_all | solution.py:58
  92.2 5.6 %collective-permute-start = (bf16[3,1536]{1,0:T(4,128)(2,1)S(1)}, bf16[3,1536]{1,0:T(4,128)(2,1)S(1)}, u32[]{:S(2)}, u32[]{:S(2)}) collective-permute-start(bf16[3,1536]{1,0:T(4,128)(2,1)S(1)} %pad_maximum_fusion.2), channel_id=1, source_target_pairs={{0,4},{4,8},{8,12},{12,16},{16,20},{20,24},{24,28},{28,32},{32,36}... | collective-permute-start | bytes 27656 | tf_op jit(solution)/shard_map/ppermute | solution.py:13
  97.8 3.3 bitcast_convert_fusion
  101.1 8.3 %fusion.21 = f32[2048,1280]{1,0:T(8,128)} fusion(f32[2048,1280]{1,0:T(8,128)S(1)} %bitcast_convert_fusion, f32[1280]{0:T(1024)S(1)} %get-tuple-element.8, f32[3,1280]{1,0:T(4,128)S(1)} %slice_convert_fusion, f32[1280]{0:T(1024)S(1)} %get-tuple-element.9, f32[1280]{0:T(1024)S(1)} %get-tuple-element.6, f32[1280]{0:T(1024)S(1)} %get-tuple-element.7, ...), kind=kLoop, calls=%fused_computation.31 | loop fusion | flops 44564480 | bytes 21012480 | tf_op jit(solution)/shard_map/convert_element_type | solution.py:80
  109.4 11.3 %copy.53 = f32[2048,1280]{0,1:T(8,128)} copy(f32[2048,1280]{1,0:T(8,128)} %fusion.21) | data formatting | bytes 20971520 | tf_op jit(solution)/shard_map/convert_element_type | solution.py:80
  120.7 13.2 %copy.78 = f32[160,8,8,256]{3,2,1,0:T(8,128)} copy(f32[160,8,8,256]{3,1,2,0:T(8,128)} %bitcast.150) | data formatting | bytes 20971520
  133.9 1.4 multiply_convert_fusion.4
  135.4 11.8 %convert_multiply_fusion = (f32[8,256,20,64]{1,0,3,2:T(8,128)}, bf16[8,256,20,64]{1,0,3,2:T(8,128)(2,1)}) fusion(f32[8,256,20]{1,0,2:T(8,128)S(1)} %get-tuple-element.46, f32[8,256,20,64]{1,0,3,2:T(8,128)} %bitcast.147, f32[8,256,20]{1,0,2:T(8,128)S(1)} %get-tuple-element.31), kind=kLoop, calls=%fused_computation.26 | loop fusion | flops 10485760 | bytes 26542080 | tf_op jit(solution)/shard_map/mul | solution.py:90
  147.2 12.6 %fusion.18 = f32[8,20,64,128]{3,2,1,0:T(8,128)S(1)} fusion(bf16[8,256,128,1]{2,1,3,0:T(8,128)(2,1)S(1)} %bitcast.172, f32[8,256,20,64]{1,0,3,2:T(8,128)} %get-tuple-element.28), kind=kOutput, calls=%fused_computation.24 | convolution fusion | flops 4026531840 | bytes 16252928 | tf_op jit(solution)/shard_map/bshp,bsn->bhpn/dot_general | solution.py:91
  160.1 2.7 multiply_add_fusion.4
  165.3 2.9 collective-permute-start.1
  169.9 1.0 mul.730
  170.9 2.1 mul.731
  173.0 1.0 mul.732
  174.0 2.2 mul.733
  176.2 1.0 mul.734
  177.2 2.1 mul.735
  179.4 1.0 mul.736
  180.4 2.1 mul.737
  182.5 1.0 mul.738
  183.5 2.2 mul.739
  185.7 1.0 mul.740
  186.7 2.1 mul.741
  188.8 1.0 mul.728
  189.8 2.1 mul.729
  191.9 1.0 mul.725
  193.0 2.1 mul.726
  195.1 1.0 mul.742
  196.1 2.1 mul.743
  199.2 1.7 copy.62
  200.9 1.6 fusion.43
  203.2 4.2 add_add_fusion
  208.4 3.4 collective-permute-start.2
  211.8 12.6 %fusion = f32[8,20,64,256]{3,2,1,0:T(8,128)} fusion(f32[8,20,256]{2,1,0:T(8,128)S(1)} %copy.59, f32[8,256,256]{2,1,0:T(8,128)S(1)} %fusion.43, pred[256,256]{1,0:T(8,128)(4,1)S(1)} %copy-done.11, bf16[8,256,20,64]{1,0,3,2:T(8,128)(2,1)S(1)} %bitcast.175), kind=kOutput, calls=%fused_computation.1 | convolution fusion | flops 1384120320 | bytes 18055168 | tf_op jit(solution)/shard_map/bhts,bshp->bthp/dot_general | solution.py:114
  224.5 1.0 mul.754
  225.5 28.6 %collective-permute-done.2 = f32[163968]{0:T(1024)} collective-permute-done((f32[163968]{0:T(1024)}, f32[163968]{0:T(1024)}, u32[]{:S(2)}, u32[]{:S(2)}) %collective-permute-start.2) | collective-permute-done | bytes 655904 | tf_op jit(solution)/shard_map/ppermute | solution.py:13
  254.8 1.6 multiply_add_fusion.2
  257.3 1.9 collective-permute-start.3
  259.2 2.0 constant_dynamic-update-slice_fusion.6
  263.1 1.0 mul.759
  264.1 30.4 %collective-permute-done.3 = f32[163968]{0:T(1024)} collective-permute-done((f32[163968]{0:T(1024)}, f32[163968]{0:T(1024)}, u32[]{:S(2)}, u32[]{:S(2)}) %collective-permute-start.3) | collective-permute-done | bytes 655904 | tf_op jit(solution)/shard_map/ppermute | solution.py:13
  295.2 1.4 multiply_add_fusion.1
  297.5 1.4 collective-permute-start.4
  298.9 2.0 constant_dynamic-update-slice_fusion.3
  300.9 2.0 constant_dynamic-update-slice_fusion.2
  304.0 12.5 %collective-permute-done.4 = f32[163968]{0:T(1024)} collective-permute-done((f32[163968]{0:T(1024)}, f32[163968]{0:T(1024)}, u32[]{:S(2)}, u32[]{:S(2)}) %collective-permute-start.4) | collective-permute-done | bytes 655904 | tf_op jit(solution)/shard_map/ppermute | solution.py:13
  317.2 1.2 multiply_add_fusion
  318.5 1.3 collective-permute-start.5
  320.7 10.7 %fusion.44 = f32[8,256,1280]{1,2,0:T(8,128)} fusion(bf16[8,256,128]{2,1,0:T(8,128)(2,1)S(1)} %bitcast.154, f32[8,1280,128]{2,1,0:T(8,128)} %constant_dynamic-update-slice_fusion), kind=kOutput, calls=%fused_computation.129 | convolution fusion | flops 4026531840 | bytes 16252928 | tf_op jit(solution)/shard_map/btn,bkn->btk/dot_general | solution.py:119
  331.4 6.4 %collective-permute-done.5 = f32[163968]{0:T(1024)S(1)} collective-permute-done((f32[163968]{0:T(1024)S(1)}, f32[163968]{0:T(1024)S(1)}, u32[]{:S(2)}, u32[]{:S(2)}) %collective-permute-start.5) | collective-permute-done | bytes 655904 | tf_op jit(solution)/shard_map/ppermute | solution.py:13
  338.2 2.0 fusion.31
  340.2 14.8 %fusion.17 = bf16[8,256,20,64]{1,3,2,0:T(8,128)(2,1)S(1)} fusion(f32[8,20,64,256]{3,2,1,0:T(8,128)} %fusion, f32[8,256,20,64]{1,0,3,2:T(8,128)} %bitcast.148, f32[8,256,20,64]{1,3,2,0:T(8,128)} %bitcast.149, f32[8,256,20]{1,2,0:T(8,128)S(1)} %copy.69, f32[20]{0:T(128)S(1)} %copy-done.15, f32[8,256,20]{1,2,0:T(8,128)S(1)} %copy-done.10, ...), kind=kOutput, calls=%fused_computation.22 | convolution fusion | flops 4044881920 | bytes 38207568 | tf_op jit(solution)/shard_map/btn,kn->btk/dot_general | solution.py:129
  355.0 6.1 %copy.70 = bf16[8,256,20,64]{1,0,3,2:T(8,128)(2,1)} copy(bf16[8,256,20,64]{1,3,2,0:T(8,128)(2,1)S(1)} %fusion.17) | data formatting | bytes 10485760 | tf_op jit(solution)/shard_map/convert_element_type | solution.py:134
  361.1 9.2 %all_to_all.44 = bf16[4,512,1280]{1,0,2:T(4,128)(2,1)} reshape(bf16[8,256,20,64]{1,0,3,2:T(8,128)(2,1)} %copy.70) | data formatting | bytes 10485760 | tf_op jit(solution)/shard_map/all_to_all | solution.py:135
  370.3 3.5 copy.71
  373.8 62.3 %all_to_all.51 = bf16[4,512,1280]{1,2,0:T(8,128)(2,1)} all-to-all(bf16[4,512,1280]{1,2,0:T(8,128)(2,1)S(1)} %copy.71), channel_id=1, replica_groups=mesh['run'=2,'ctx'=32,'head'=4] {'head'}, dimensions={0} | all-to-all | bytes 10485760 | tf_op jit(solution)/shard_map/all_to_all | solution.py:135
  436.1 7.9 %copy.72 = bf16[512,5120]{1,0:T(8,128)(2,1)} copy(bf16[512,5120]{0,1:T(8,128)(2,1)} %bitcast.152) | data formatting | bytes 10485760 | tf_op jit(solution)/shard_map/all_to_all | solution.py:135
  (109 shorter events, 21.3 us)
Async XLA Ops:
  8.1 10.3 %all-to-all-start.1 = ((bf16[512,4,20]{0,2,1:T(8,128)(2,1)}), bf16[512,4,20]{0,2,1:T(8,128)(2,1)S(1)}, u32[]{:S(2)}, u32[]{:S(2)}) async-start(bf16[512,4,20]{0,2,1:T(8,128)(2,1)} %all_to_all.42), calls=%async_computation.1 | async-start | bytes 196608 | tf_op jit(solution)/shard_map/all_to_all | solution.py:59
  18.3 5.9 %copy-start.12 = (f32[5,1280]{1,0:T(8,128)S(1)}, f32[5,1280]{1,0:T(8,128)}, u32[]{:S(2)}) copy-start(f32[5,1280]{1,0:T(8,128)} %param.10) | copy-start | bytes 76804
  18.3 6.0 %copy-start.14 = (f32[2,20]{1,0:T(2,128)S(1)}, f32[2,20]{1,0:T(2,128)}, u32[]{:S(2)}) copy-start(f32[2,20]{1,0:T(2,128)} %param.12) | copy-start | bytes 484
  18.3 6.0 %copy-start.13 = (f32[5,256]{1,0:T(8,128)S(1)}, f32[5,256]{1,0:T(8,128)}, u32[]{:S(2)}) copy-start(f32[5,256]{1,0:T(8,128)} %param.11) | copy-start | bytes 15364
  18.3 73.1 %all-to-all-start = ((bf16[512,4,1280]{2,0,1:T(8,128)(2,1)}), bf16[512,4,1280]{2,0,1:T(8,128)(2,1)}, u32[]{:S(2)}, u32[]{:S(2)}) async-start(bf16[512,4,1280]{2,0,1:T(8,128)(2,1)} %bitcast.151), calls=%async_computation | async-start | bytes 10485760 | tf_op jit(solution)/shard_map/all_to_all | solution.py:58
  23.5 37.9 %all-gather.2.cloned.1.call-start = ((), (), s32[]{:S(2)}) async-start(), calls=%async_computation.3 | async-start | bytes 1310720 | tf_op jit(solution)/shard_map/all_gather | solution.py:66
  92.2 8.9 %collective-permute-start = (bf16[3,1536]{1,0:T(4,128)(2,1)S(1)}, bf16[3,1536]{1,0:T(4,128)(2,1)S(1)}, u32[]{:S(2)}, u32[]{:S(2)}) collective-permute-start(bf16[3,1536]{1,0:T(4,128)(2,1)S(1)} %pad_maximum_fusion.2), channel_id=1, source_target_pairs={{0,4},{4,8},{8,12},{12,16},{16,20},{20,24},{24,28},{28,32},{32,36}... | collective-permute-start | bytes 27656 | tf_op jit(solution)/shard_map/ppermute | solution.py:13
  135.4 11.9 %copy-start.5 = (bf16[2048,128]{1,0:T(8,128)(2,1)}, bf16[2048,128]{1,0:T(8,128)(2,1)S(1)}, u32[]{:S(2)}) copy-start(bf16[2048,128]{1,0:T(8,128)(2,1)S(1)} %get-tuple-element.40) | copy-start | bytes 1572868
  160.1 3.7 copy-start.2
  160.1 3.7 copy-start.3
  160.1 3.7 copy-start.4
  162.8 1.6 copy-start
  165.3 37.2 %collective-permute-start.1 = (f32[163968]{0:T(1024)}, f32[163968]{0:T(1024)}, u32[]{:S(2)}, u32[]{:S(2)}) collective-permute-start(f32[163968]{0:T(1024)} %select_maximum_fusion.4), channel_id=1, source_target_pairs={{0,4},{4,8},{8,12},{12,16},{16,20},{20,24},{24,28},{28,32},{32,36}... | collective-permute-start | bytes 1967624 | tf_op jit(solution)/shard_map/ppermute | solution.py:13
  200.9 10.9 %slice-start = ((s8[5242880]{0:T(1024)(128)(4,1)}), s8[4194304]{0:T(1024)(128)(4,1)S(1)}, s32[]{:S(2)}) async-start(s8[5242880]{0:T(1024)(128)(4,1)} %bitcast.174), calls=%async_computation.4 | async-start | bytes 8388608
  203.2 8.6 %slice-start.1 = ((s8[5242880]{0:T(1024)(128)(4,1)}), s8[1048576]{0:T(1024)(128)(4,1)S(1)}, s32[]{:S(2)}) async-start(s8[5242880]{0:T(1024)(128)(4,1)} %bitcast.174), calls=%async_computation.5 | async-start | bytes 2097152
  203.2 8.6 %copy-start.11 = (pred[256,256]{1,0:T(8,128)(4,1)S(1)}, pred[256,256]{1,0:T(8,128)(4,1)}, u32[]{:S(2)}) copy-start(pred[256,256]{1,0:T(8,128)(4,1)} %iota_compare_fusion.1) | copy-start | bytes 196612
  207.4 17.0 %copy-start.1 = (f32[163840]{0:T(1024)}, f32[163840]{0:T(1024)S(1)}, u32[]{:S(2)}) copy-start(f32[163840]{0:T(1024)S(1)} %add_add_fusion) | copy-start | bytes 1966084
  208.4 45.7 %collective-permute-start.2 = (f32[163968]{0:T(1024)}, f32[163968]{0:T(1024)}, u32[]{:S(2)}, u32[]{:S(2)}) collective-permute-start(f32[163968]{0:T(1024)} %select_maximum_fusion.3), channel_id=1, source_target_pairs={{0,8},{4,12},{8,16},{12,20},{16,24},{20,28},{24,32},{28,36},{32,40... | collective-permute-start | bytes 1967624 | tf_op jit(solution)/shard_map/ppermute | solution.py:13
  224.4 36.8 %copy-start.9 = (f32[1,20,64,128]{3,2,1,0:T(8,128)S(1)}, f32[1,20,64,128]{3,2,1,0:T(8,128)}, u32[]{:S(2)}) copy-start(f32[1,20,64,128]{3,2,1,0:T(8,128)} %get-tuple-element.26) | copy-start | bytes 1966084
  224.4 37.7 %copy-start.8 = (f32[1,20,64,128]{3,2,1,0:T(8,128)S(1)}, f32[1,20,64,128]{3,2,1,0:T(8,128)}, u32[]{:S(2)}) copy-start(f32[1,20,64,128]{3,2,1,0:T(8,128)} %get-tuple-element.25) | copy-start | bytes 1966084
  257.3 37.3 %collective-permute-start.3 = (f32[163968]{0:T(1024)}, f32[163968]{0:T(1024)}, u32[]{:S(2)}, u32[]{:S(2)}) collective-permute-start(f32[163968]{0:T(1024)} %select_maximum_fusion.2), channel_id=1, source_target_pairs={{0,16},{4,20},{8,24},{12,28},{16,32},{20,36},{24,40},{28,44},{32,4... | collective-permute-start | bytes 1967624 | tf_op jit(solution)/shard_map/ppermute | solution.py:13
  262.1 40.8 %copy-start.7 = (f32[1,20,64,128]{3,2,1,0:T(8,128)S(1)}, f32[1,20,64,128]{3,2,1,0:T(8,128)}, u32[]{:S(2)}) copy-start(f32[1,20,64,128]{3,2,1,0:T(8,128)} %get-tuple-element.22) | copy-start | bytes 1966084
  297.5 22.3 %copy-start.6 = (f32[1,20,64,128]{3,2,1,0:T(8,128)S(1)}, f32[1,20,64,128]{3,2,1,0:T(8,128)}, u32[]{:S(2)}) copy-start(f32[1,20,64,128]{3,2,1,0:T(8,128)} %get-tuple-element.21) | copy-start | bytes 1966084
  297.5 19.0 %collective-permute-start.4 = (f32[163968]{0:T(1024)}, f32[163968]{0:T(1024)}, u32[]{:S(2)}, u32[]{:S(2)}) collective-permute-start(f32[163968]{0:T(1024)} %select_maximum_fusion.1), channel_id=1, source_target_pairs={{0,32},{4,36},{8,40},{12,44},{16,48},{20,52},{24,56},{28,60},{32,6... | collective-permute-start | bytes 1967624 | tf_op jit(solution)/shard_map/ppermute | solution.py:13
  318.5 19.3 %collective-permute-start.5 = (f32[163968]{0:T(1024)S(1)}, f32[163968]{0:T(1024)S(1)}, u32[]{:S(2)}, u32[]{:S(2)}) collective-permute-start(f32[163968]{0:T(1024)S(1)} %select_maximum_fusion), channel_id=1, source_target_pairs={{0,64},{4,68},{8,72},{12,76},{16,80},{20,84},{24,88},{28,92},{32,9... | collective-permute-start | bytes 1967624 | tf_op jit(solution)/shard_map/ppermute | solution.py:13
  331.4 8.8 %copy-start.10 = (f32[8,256,20]{1,2,0:T(8,128)S(1)}, f32[8,256,20]{1,2,0:T(8,128)}, u32[]{:S(2)}) copy-start(f32[8,256,20]{1,2,0:T(8,128)} %copy.62) | copy-start | bytes 491524
  331.4 8.8 %copy-start.15 = (f32[20]{0:T(128)S(1)}, f32[20]{0:T(128)}, u32[]{:S(2)}) copy-start(f32[20]{0:T(128)} %param.13) | copy-start | bytes 244
Sparse Core Ops, SparseCore 0:
  26.2 35.2 all-gather.1

commit v3 on v2

--- a/solution.py
+++ b/solution.py
@@ -2,6 +2,7 @@
 import jax.numpy as jnp
 from jax import lax
 from jax.sharding import PartitionSpec as P
+
 
 KERNEL = 4
 SPAN = 256
@@ -44,7 +45,8 @@
     incl_decay = decay * excl_decay
     shift = 2
     while shift < length:
-        got_decay, got_state = unpack(from_behind(pack(incl_decay, incl_state), axis, shift))
+        sent = from_behind(pack(incl_decay, incl_state), axis, shift)
+        got_decay, got_state = unpack(sent)
         excl_state = excl_decay[:, None] * got_state + excl_state
         incl_state = incl_decay[:, None] * got_state + incl_state
         excl_decay = excl_decay * got_decay
@@ -94,11 +96,9 @@
     block_decay = jnp.exp(ending)
     entering = []
     running = jnp.zeros_like(block_states[0])
-    decay_before = []
     running_decay = jnp.ones_like(block_decay[0])
     for k in range(block_count):
         entering.append(running)
-        decay_before.append(running_decay)
         running = block_decay[k][:, None, None] * running + block_states[k]
         running_decay = running_decay * block_decay[k]
     incoming = relay_states(running_decay, running, "ctx")
@@ -126,13 +126,38 @@
         + skip_gain[None, None, :, None] * u_x(x_heads, block_count)
     )
 
+    partial = known.astype(jnp.bfloat16).reshape(context, channels)
+    partial_tokens = lax.all_to_all(partial, "head", split_axis=0, concat_axis=1, tiled=True)
+
+    tokens = inner_tokens.shape[0]
+    group = lax.axis_index("head")
+    rates_all = lax.all_gather(head_rates, "head", axis=1, tiled=True)
+    step_tokens = jax.nn.softplus(step_raw.astype(jnp.float32) + rates_all[0][None, :])
+    decay_tokens = -step_tokens * jnp.exp(rates_all[1])[None, :]
+    cumulative_tokens = jnp.cumsum(decay_tokens.reshape(tokens // SPAN, SPAN, -1), axis=1)
+    ends_all = lax.all_gather(cumulative_tokens[:, -1, :], "head", axis=0, tiled=True)
+    exps_all = jnp.exp(ends_all)
+    before_all = []
+    running_decay = jnp.ones_like(exps_all[0])
+    for k in range(exps_all.shape[0]):
+        before_all.append(running_decay)
+        running_decay = running_decay * exps_all[k]
+    before_own = lax.dynamic_slice_in_dim(
+        jnp.stack(before_all), group * (tokens // SPAN), tokens // SPAN, axis=0
+    )
+    factor_tokens = (jnp.exp(cumulative_tokens) * before_own[:, None, :]).reshape(tokens, -1)
+    c_tokens = lax.dynamic_slice_in_dim(c_rows, group * tokens, tokens, axis=0).astype(jnp.float32)
+    incoming_all = lax.all_gather(incoming, "head", axis=0, tiled=True)
     carried_in = jnp.einsum(
-        "btn,kn->btk", c_float, incoming.reshape(channels, state_width), precision=lax.Precision.HIGHEST
-    ).reshape(block_count, SPAN, heads_local, head_width)
-    factor = decay_in * jnp.stack(decay_before)[:, None, :]
-    summed = known + factor[:, :, :, None] * carried_in
-    regrouped = summed.astype(jnp.bfloat16).reshape(context, channels)
-    return lax.all_to_all(regrouped, "head", split_axis=0, concat_axis=1, tiled=True)
+        "tn,kn->tk",
+        c_tokens,
+        incoming_all.reshape(-1, state_width),
+        precision=lax.Precision.HIGHEST,
+    ).reshape(tokens, factor_tokens.shape[1], head_width)
+    summed = partial_tokens.astype(jnp.float32).reshape(carried_in.shape) + (
+        factor_tokens[:, :, None] * carried_in
+    )
+    return summed.astype(jnp.bfloat16).reshape(tokens, -1)
 
 
 def u_x(x_heads, block_count):

time: 455 us -> 518 us (1.14)
  the two profiles are of different devices: /device:TPU:102 before, /device:TPU:98 now
where the time goes in v3:
time: 518 us; the launch traced here: 513 us
  local copies, waits for them, and re-layouts  117 us (23%)
  waiting for transfers between devices  103 us (20%)
  blocking collectives  86.8 us (17%)
  other arithmetic  65.3 us (13%)
  starting transfers between devices  63.4 us (12%)
  matrix products  62.9 us (12%)
  between operations  14.3 us (3%)
    all_gather x1, blocking collectives, per_device(): rates_all = lax.all_gather(head_rates, 'head', axis=1, tiled=True)  78.5 us
    ppermute x6, starting transfers between devices, from_behind(): return lax.ppermute(value, axis, pairs)  48.6 us
    ppermute x6, waiting for transfers between devices, from_behind(): return lax.ppermute(value, axis, pairs)  43.7 us
    all_gather x1, waiting for transfers between devices, per_device(): state_whole = lax.all_gather(state_inputs, 'head', axis=0, tiled=True)  30.1 us
    all_to_all x1, waiting for transfers between devices, per_device(): lax.all_to_all(inner_tokens, 'head', split_axis=1, concat_axis=0, tiled=T...  27.9 us
    mul x25, local copies, waits for them, and re-layouts, per_device(): running = block_decay[k][:, None, None] * running + block_states[k]  26.5 us
    unnamed x73, local copies, waits for them, and re-layouts  23.7 us
    dot_general x1, matrix products, per_device(): jnp.einsum('bhts,bshp->bthp', mixing, u_blocks, preferred_element_type=jn...  20.8 us
  transfers between devices with their start and end apart: 11, of which 6 were waited for; matrix products, arithmetic and copies ran while one was open for 23% of the time, Pallas kernels for 0%

profile of v3, /device:TPU:98, one launch (start us, length us, event | category | flops | bytes accessed | tf_op | source)
XLA Modules:
  0.0 513.2 jit_solution(3245749846790090049)
XLA Ops:
  6.5 1.5 all_to_all.38
  8.1 4.5 all-to-all-start.1
  12.5 5.2 %copy.135 = bf16[64,4,8,1280]{3,2,0,1:T(8,128)(2,1)} copy(bf16[64,4,8,1280]{3,2,1,0:T(8,128)(2,1)} %bitcast.237) | data formatting | bytes 10485760 | tf_op jit(solution)/shard_map/all_to_all | solution.py:60
  18.3 5.2 %all-to-all-start = ((bf16[512,4,1280]{2,0,1:T(8,128)(2,1)}), bf16[512,4,1280]{2,0,1:T(8,128)(2,1)}, u32[]{:S(2)}, u32[]{:S(2)}) async-start(bf16[512,4,1280]{2,0,1:T(8,128)(2,1)} %bitcast.214), calls=%async_computation | async-start | bytes 10485760 | tf_op jit(solution)/shard_map/all_to_all | solution.py:60
  24.9 4.6 reduce-window.14
  31.4 30.1 %all-gather.5.cloned.1.call-done = bf16[2048,256]{1,0:T(8,128)(2,1)} async-done(((bf16[512,256]{1,0:T(8,128)(2,1)}), bf16[2048,256]{1,0:T(8,128)(2,1)}) %all-gather.5.cloned.1.call-update) | async-done | bytes 1048592 | tf_op jit(solution)/shard_map/all_gather | solution.py:68
  62.2 1.4 convert_element_type.89
  63.6 27.9 %all-to-all-done = bf16[512,4,1280]{2,0,1:T(8,128)(2,1)} async-done(((bf16[512,4,1280]{2,0,1:T(8,128)(2,1)}), bf16[512,4,1280]{2,0,1:T(8,128)(2,1)}, u32[]{:S(2)}, u32[]{:S(2)}) %all-to-all-start) | async-done | bytes 5242912 | tf_op jit(solution)/shard_map/all_to_all | solution.py:60
  92.2 5.2 %collective-permute-start = (bf16[3,1536]{1,0:T(4,128)(2,1)S(1)}, bf16[3,1536]{1,0:T(4,128)(2,1)S(1)}, u32[]{:S(2)}, u32[]{:S(2)}) collective-permute-start(bf16[3,1536]{1,0:T(4,128)(2,1)S(1)} %pad_maximum_fusion.2), channel_id=1, source_target_pairs={{0,4},{4,8},{8,12},{12,16},{16,20},{20,24},{24,28},{28,32},{32,36}... | collective-permute-start | bytes 27656 | tf_op jit(solution)/shard_map/ppermute | solution.py:14
  97.4 3.3 bitcast_convert_fusion
  100.7 8.4 %fusion.23 = f32[2048,1280]{1,0:T(8,128)} fusion(f32[2048,1280]{1,0:T(8,128)S(1)} %bitcast_convert_fusion, f32[1280]{0:T(1024)S(1)} %get-tuple-element.8, f32[3,1280]{1,0:T(4,128)S(1)} %slice_convert_fusion, f32[1280]{0:T(1024)S(1)} %get-tuple-element.9, f32[1280]{0:T(1024)S(1)} %get-tuple-element.6, f32[1280]{0:T(1024)S(1)} %get-tuple-element.7, ...), kind=kLoop, calls=%fused_computation.32 | loop fusion | flops 44564480 | bytes 21012480 | tf_op jit(solution)/shard_map/convert_element_type | solution.py:82
  109.1 11.3 %copy.75 = f32[2048,1280]{0,1:T(8,128)} copy(f32[2048,1280]{1,0:T(8,128)} %fusion.23) | data formatting | bytes 20971520 | tf_op jit(solution)/shard_map/convert_element_type | solution.py:82
  120.4 13.2 %copy.110 = f32[160,8,8,256]{3,2,1,0:T(8,128)} copy(f32[160,8,8,256]{3,1,2,0:T(8,128)} %bitcast.212) | data formatting | bytes 20971520
  133.6 1.4 multiply_convert_fusion.6
  135.9 11.7 %convert_multiply_fusion = (f32[8,256,20,64]{1,0,3,2:T(8,128)}, bf16[8,256,20,64]{1,0,3,2:T(8,128)(2,1)}) fusion(f32[8,256,20]{1,0,2:T(8,128)S(1)} %subtract_exponential_fusion, f32[8,256,20,64]{1,0,3,2:T(8,128)} %bitcast.210, f32[8,256,20]{1,0,2:T(8,128)S(1)} %get-tuple-element.31), kind=kLoop, calls=%fused_computation.27 | loop fusion | flops 10485760 | bytes 26542080 | tf_op jit(solution)/shard_map/mul | solution.py:92
  147.6 12.7 %fusion.18 = f32[8,20,64,128]{3,2,1,0:T(8,128)S(1)} fusion(bf16[8,256,128,1]{2,1,3,0:T(8,128)(2,1)S(1)} %bitcast.235, f32[8,256,20,64]{1,0,3,2:T(8,128)} %get-tuple-element.28), kind=kOutput, calls=%fused_computation.25 | convolution fusion | flops 4026531840 | bytes 16252928 | tf_op jit(solution)/shard_map/bshp,bsn->bhpn/dot_general | solution.py:93
  160.5 2.8 multiply_add_fusion.4
  165.9 3.3 collective-permute-start.1
  170.8 1.0 mul.712
  171.8 2.1 mul.713
  173.9 1.7 mul.714
  175.6 2.1 mul.715
  178.7 2.1 mul.717
  181.8 2.1 mul.719
  184.0 1.0 mul.720
  185.0 2.1 mul.721
  187.1 1.0 mul.722
  188.1 2.1 mul.723
  190.2 1.0 mul.710
  191.2 2.1 mul.711
  193.4 1.0 mul.707
  194.4 2.2 mul.708
  196.5 1.0 mul.724
  197.5 2.1 mul.725
  201.3 2.0 constant_dynamic-update-slice_fusion.6
  204.0 4.9 add_add_fusion.1
  210.6 3.2 collective-permute-start.2
  217.6 24.6 %collective-permute-done.2 = f32[163968]{0:T(1024)} collective-permute-done((f32[163968]{0:T(1024)}, f32[163968]{0:T(1024)}, u32[]{:S(2)}, u32[]{:S(2)}) %collective-permute-start.2) | collective-permute-done | bytes 655904 | tf_op jit(solution)/shard_map/ppermute | solution.py:14
  242.8 2.2 multiply_add_fusion.2
  246.0 3.9 collective-permute-start.3
  249.9 2.0 constant_dynamic-update-slice_fusion.2
  251.9 2.0 constant_dynamic-update-slice_fusion.1
  253.8 1.7 fusion.60
  256.7 16.7 %collective-permute-done.3 = f32[163968]{0:T(1024)} collective-permute-done((f32[163968]{0:T(1024)}, f32[163968]{0:T(1024)}, u32[]{:S(2)}, u32[]{:S(2)}) %collective-permute-start.3) | collective-permute-done | bytes 655904 | tf_op jit(solution)/shard_map/ppermute | solution.py:14
  274.1 2.2 multiply_add_fusion.1
  277.2 3.4 collective-permute-start.4
  281.6 10.6 %fusion.61 = f32[8,256,1280]{1,2,0:T(8,128)} fusion(bf16[8,256,128]{2,1,0:T(8,128)(2,1)S(1)} %bitcast.234, f32[8,1280,128]{2,1,0:T(8,128)} %constant_dynamic-update-slice_fusion), kind=kOutput, calls=%fused_computation.150 | convolution fusion | flops 4026531840 | bytes 16252928 | tf_op jit(solution)/shard_map/btn,bkn->btk/dot_general | solution.py:119
  292.4 2.4 collective-permute-done.4
  295.5 2.0 multiply_add_fusion
  298.4 29.6 %collective-permute-start.5 = (f32[163968]{0:T(1024)}, f32[163968]{0:T(1024)}, u32[]{:S(2)}, u32[]{:S(2)}) collective-permute-start(f32[163968]{0:T(1024)} %select_maximum_fusion), channel_id=1, source_target_pairs={{0,64},{4,68},{8,72},{12,76},{16,80},{20,84},{24,88},{28,92},{32,9... | collective-permute-start | bytes 1967624 | tf_op jit(solution)/shard_map/ppermute | solution.py:14
  328.0 20.8 %fusion.16 = bf16[8,256,20,64]{1,3,2,0:T(8,128)(2,1)S(1)} fusion(f32[8,256,20,64]{1,0,3,2:T(8,128)} %bitcast.211, f32[8,256,20,64]{1,3,2,0:T(8,128)} %bitcast.216, f32[8,20,256]{2,1,0:T(8,128)S(1)} %copy.81, f32[8,256,256]{2,1,0:T(8,128)} %fusion.60, pred[256,256]{1,0:T(8,128)(4,1)S(1)} %iota_compare_fusion.1, ...), kind=kOutput, calls=%fused_computation.21 | convolution fusion | flops 1397227520 | bytes 33947728 | tf_op jit(solution)/shard_map/bhts,bshp->bthp/dot_general | solution.py:114
  348.8 6.0 %copy.90 = bf16[8,256,20,64]{1,0,3,2:T(8,128)(2,1)} copy(bf16[8,256,20,64]{1,3,2,0:T(8,128)(2,1)S(1)} %fusion.16) | data formatting | bytes 10485760 | tf_op jit(solution)/shard_map/convert_element_type | solution.py:129
  354.9 9.2 %all_to_all.40 = bf16[4,512,1280]{1,0,2:T(4,128)(2,1)} reshape(bf16[8,256,20,64]{1,0,3,2:T(8,128)(2,1)} %copy.90) | data formatting | bytes 10485760 | tf_op jit(solution)/shard_map/all_to_all | solution.py:130
  364.1 5.9 %copy.91 = bf16[4,512,1280]{1,2,0:T(8,128)(2,1)} copy(bf16[4,512,1280]{1,0,2:T(4,128)(2,1)} %all_to_all.40) | data formatting | bytes 10485760 | tf_op jit(solution)/shard_map/all_to_all | solution.py:130
  370.0 5.2 %all-to-all-start.2 = ((bf16[4,512,1280]{1,2,0:T(8,128)(2,1)}), bf16[4,512,1280]{1,2,0:T(8,128)(2,1)}, u32[]{:S(2)}, u32[]{:S(2)}) async-start(bf16[4,512,1280]{1,2,0:T(8,128)(2,1)} %copy.91), calls=%async_computation.2 | async-start | bytes 10485760 | tf_op jit(solution)/shard_map/all_to_all | solution.py:130
  375.2 1.1 slice.314
  376.4 2.2 add_add_fusion
  378.6 78.5 %all-gather.1 = f32[4,20,2]{1,2,0:T(2,128)S(1)} all-gather(f32[1,20,2]{1,2,0:T(2,128)S(1)} %bitcast.267), channel_id=1, replica_groups=mesh['run'=2,'ctx'=32,'head'=4] {'head'}, dimensions={0}, use_global_device_ids=true | all-gather | bytes 800 | tf_op jit(solution)/shard_map/all_gather | solution.py:134
  457.4 1.3 reduce-window.16
  459.3 8.3 %all-gather = f32[8,1,80]{2,1,0:T(1,128)S(1)} all-gather(f32[2,1,80]{2,1,0:T(1,128)S(1)} %copy.96), channel_id=2, replica_groups=mesh['run'=2,'ctx'=32,'head'=4] {'head'}, dimensions={0}, use_global_device_ids=true | all-gather | bytes 3200 | tf_op jit(solution)/shard_map/all_gather | solution.py:138
  467.8 8.0 %convert_element_type.103 = f32[4,512,1280]{1,2,0:T(8,128)} convert(bf16[4,512,1280]{1,2,0:T(8,128)(2,1)} %all-to-all-done.2) | non-fusion elementwise | flops 2621440 | bytes 15728640 | tf_op jit(solution)/shard_map/convert_element_type | solution.py:157
  475.8 17.1 %fusion.17 = bf16[512,80,64]{0,1,2:T(8,128)(2,1)S(1)} fusion(f32[512,80,64]{0,2,1:T(8,128)} %bitcast.213, f32[512,80]{0,1:T(8,128)S(1)} %bitcast.258, f32[80,64,128]{2,1,0:T(8,128)} %all-gather.7.cloned.1.call-done, bf16[2048,128]{1,0:T(8,128)(2,1)S(1)} %copy-done.5, s32[]{:T(128)S(6)} %select_n.27), kind=kOutput, calls=%fused_computation.23 | convolution fusion | flops 4034396160 | bytes 18644996 | tf_op jit(solution)/shard_map/tn,kn->tk/dot_general | solution.py:151
  493.0 5.3 %copy.100 = bf16[512,80,64]{0,2,1:T(8,128)(2,1)} copy(bf16[512,80,64]{0,1,2:T(8,128)(2,1)S(1)} %fusion.17) | data formatting | bytes 10485760 | tf_op jit(solution)/shard_map/convert_element_type | solution.py:160
  498.3 7.9 %copy.101 = bf16[512,5120]{1,0:T(8,128)(2,1)} copy(bf16[512,5120]{0,1:T(8,128)(2,1)} %bitcast.215) | data formatting | bytes 10485760 | tf_op jit(solution)/shard_map/reshape | solution.py:160
  (157 shorter events, 28.2 us)
Async XLA Ops:
  8.1 10.3 %all-to-all-start.1 = ((bf16[512,4,20]{0,2,1:T(8,128)(2,1)}), bf16[512,4,20]{0,2,1:T(8,128)(2,1)S(1)}, u32[]{:S(2)}, u32[]{:S(2)}) async-start(bf16[512,4,20]{0,2,1:T(8,128)(2,1)} %all_to_all.38), calls=%async_computation.1 | async-start | bytes 196608 | tf_op jit(solution)/shard_map/all_to_all | solution.py:61
  18.3 5.9 %copy-start.18 = (f32[5,1280]{1,0:T(8,128)S(1)}, f32[5,1280]{1,0:T(8,128)}, u32[]{:S(2)}) copy-start(f32[5,1280]{1,0:T(8,128)} %param.10) | copy-start | bytes 76804
  18.3 6.0 %copy-start.28 = (f32[2,20]{1,0:T(2,128)S(1)}, f32[2,20]{1,0:T(2,128)}, u32[]{:S(2)}) copy-start(f32[2,20]{1,0:T(2,128)} %param.12) | copy-start | bytes 484
  18.3 6.0 %copy-start.30 = (f32[5,256]{1,0:T(8,128)S(1)}, f32[5,256]{1,0:T(8,128)}, u32[]{:S(2)}) copy-start(f32[5,256]{1,0:T(8,128)} %param.11) | copy-start | bytes 15364
  18.3 73.1 %all-to-all-start = ((bf16[512,4,1280]{2,0,1:T(8,128)(2,1)}), bf16[512,4,1280]{2,0,1:T(8,128)(2,1)}, u32[]{:S(2)}, u32[]{:S(2)}) async-start(bf16[512,4,1280]{2,0,1:T(8,128)(2,1)} %bitcast.214), calls=%async_computation | async-start | bytes 10485760 | tf_op jit(solution)/shard_map/all_to_all | solution.py:60
  23.5 38.0 %all-gather.5.cloned.1.call-start = ((), (), s32[]{:S(2)}) async-start(), calls=%async_computation.3 | async-start | bytes 1310720 | tf_op jit(solution)/shard_map/all_gather | solution.py:68
  31.2 132.9 %copy-start.22 = (f32[20]{0:T(128)}, f32[20]{0:T(128)S(1)}, u32[]{:S(2)}) copy-start(f32[20]{0:T(128)S(1)} %get-tuple-element.65) | copy-start | bytes 244
  31.2 133.8 %copy-start.24 = (f32[20]{0:T(128)}, f32[20]{0:T(128)S(1)}, u32[]{:S(2)}) copy-start(f32[20]{0:T(128)S(1)} %get-tuple-element.64) | copy-start | bytes 244
  31.2 132.1 %copy-start.20 = (f32[20]{0:T(128)}, f32[20]{0:T(128)S(1)}, u32[]{:S(2)}) copy-start(f32[20]{0:T(128)S(1)} %get-tuple-element.58) | copy-start | bytes 244
  31.2 132.2 %copy-start.19 = (f32[20]{0:T(128)}, f32[20]{0:T(128)S(1)}, u32[]{:S(2)}) copy-start(f32[20]{0:T(128)S(1)} %get-tuple-element.59) | copy-start | bytes 244
  31.3 132.7 %copy-start.26 = (f32[20]{0:T(128)}, f32[20]{0:T(128)S(1)}, u32[]{:S(2)}) copy-start(f32[20]{0:T(128)S(1)} %get-tuple-element.57) | copy-start | bytes 244
  92.2 8.5 %collective-permute-start = (bf16[3,1536]{1,0:T(4,128)(2,1)S(1)}, bf16[3,1536]{1,0:T(4,128)(2,1)S(1)}, u32[]{:S(2)}, u32[]{:S(2)}) collective-permute-start(bf16[3,1536]{1,0:T(4,128)(2,1)S(1)} %pad_maximum_fusion.2), channel_id=1, source_target_pairs={{0,4},{4,8},{8,12},{12,16},{16,20},{20,24},{24,28},{28,32},{32,36}... | collective-permute-start | bytes 27656 | tf_op jit(solution)/shard_map/ppermute | solution.py:14
  135.9 11.7 %copy-start.6 = (bf16[2048,128]{1,0:T(8,128)(2,1)}, bf16[2048,128]{1,0:T(8,128)(2,1)S(1)}, u32[]{:S(2)}) copy-start(bf16[2048,128]{1,0:T(8,128)(2,1)S(1)} %get-tuple-element.40) | copy-start | bytes 1572868
  160.5 3.8 copy-start.2
  160.5 3.8 copy-start.3
  160.5 3.8 copy-start.4
  164.3 6.5 %copy-start.21 = (f32[20]{0:T(128)S(1)}, f32[20]{0:T(128)}, u32[]{:S(2)}) copy-start(f32[20]{0:T(128)} %copy-done.20) | copy-start | bytes 244
  165.9 37.4 %collective-permute-start.1 = (f32[163968]{0:T(1024)}, f32[163968]{0:T(1024)}, u32[]{:S(2)}, u32[]{:S(2)}) collective-permute-start(f32[163968]{0:T(1024)} %select_maximum_fusion.4), channel_id=1, source_target_pairs={{0,4},{4,8},{8,12},{12,16},{16,20},{20,24},{24,28},{28,32},{32,36}... | collective-permute-start | bytes 1967624 | tf_op jit(solution)/shard_map/ppermute | solution.py:14
  175.6 14.6 %copy-start.27 = (f32[20]{0:T(128)S(1)}, f32[20]{0:T(128)}, u32[]{:S(2)}) copy-start(f32[20]{0:T(128)} %copy-done.26) | copy-start | bytes 244
  178.7 14.6 %copy-start.25 = (f32[20]{0:T(128)S(1)}, f32[20]{0:T(128)}, u32[]{:S(2)}) copy-start(f32[20]{0:T(128)} %copy-done.24) | copy-start | bytes 244
  181.8 14.7 %copy-start.23 = (f32[20]{0:T(128)S(1)}, f32[20]{0:T(128)}, u32[]{:S(2)}) copy-start(f32[20]{0:T(128)} %copy-done.22) | copy-start | bytes 244
  185.0 14.7 %copy-start.15 = (f32[8,256,20]{1,0,2:T(8,128)S(1)}, f32[8,256,20]{1,0,2:T(8,128)}, u32[]{:S(2)}) copy-start(f32[8,256,20]{1,0,2:T(8,128)} %get-tuple-element.19) | copy-start | bytes 491524
  204.0 9.8 %copy-start.12 = (f32[1,20,64,128]{3,2,1,0:T(8,128)S(1)}, f32[1,20,64,128]{3,2,1,0:T(8,128)}, u32[]{:S(2)}) copy-start(f32[1,20,64,128]{3,2,1,0:T(8,128)} %get-tuple-element.26) | copy-start | bytes 1966084
  204.0 10.7 %copy-start.11 = (f32[1,20,64,128]{3,2,1,0:T(8,128)S(1)}, f32[1,20,64,128]{3,2,1,0:T(8,128)}, u32[]{:S(2)}) copy-start(f32[1,20,64,128]{3,2,1,0:T(8,128)} %get-tuple-element.25) | copy-start | bytes 1966084
  204.0 11.6 %copy-start.10 = (f32[1,20,64,128]{3,2,1,0:T(8,128)S(1)}, f32[1,20,64,128]{3,2,1,0:T(8,128)}, u32[]{:S(2)}) copy-start(f32[1,20,64,128]{3,2,1,0:T(8,128)} %get-tuple-element.24) | copy-start | bytes 1966084
  208.9 0.8 copy-start
  210.6 32.2 %copy-start.1 = (f32[163840]{0:T(1024)S(1)}, f32[163840]{0:T(1024)}, u32[]{:S(2)}) copy-start(f32[163840]{0:T(1024)} %copy-done) | copy-start | bytes 1966084
  210.6 31.5 %collective-permute-start.2 = (f32[163968]{0:T(1024)}, f32[163968]{0:T(1024)}, u32[]{:S(2)}, u32[]{:S(2)}) collective-permute-start(f32[163968]{0:T(1024)} %select_maximum_fusion.3), channel_id=1, source_target_pairs={{0,8},{4,12},{8,16},{12,20},{16,24},{20,28},{24,32},{28,36},{32,40... | collective-permute-start | bytes 1967624 | tf_op jit(solution)/shard_map/ppermute | solution.py:14
  215.6 38.3 %copy-start.5 = (bf16[2048,128]{1,0:T(8,128)(2,1)S(1)}, bf16[2048,128]{1,0:T(8,128)(2,1)}, u32[]{:S(2)}) copy-start(bf16[2048,128]{1,0:T(8,128)(2,1)} %get-tuple-element.41) | copy-start | bytes 1572868
  215.6 38.3 %copy-start.7 = (bf16[2048,128]{1,0:T(8,128)(2,1)S(1)}, bf16[2048,128]{1,0:T(8,128)(2,1)}, u32[]{:S(2)}) copy-start(bf16[2048,128]{1,0:T(8,128)(2,1)} %copy-done.6) | copy-start | bytes 1572868
  246.0 27.4 %collective-permute-start.3 = (f32[163968]{0:T(1024)}, f32[163968]{0:T(1024)}, u32[]{:S(2)}, u32[]{:S(2)}) collective-permute-start(f32[163968]{0:T(1024)} %select_maximum_fusion.2), channel_id=1, source_target_pairs={{0,16},{4,20},{8,24},{12,28},{16,32},{20,36},{24,40},{28,44},{32,4... | collective-permute-start | bytes 1967624 | tf_op jit(solution)/shard_map/ppermute | solution.py:14
  253.8 26.8 %copy-start.9 = (f32[1,20,64,128]{3,2,1,0:T(8,128)S(1)}, f32[1,20,64,128]{3,2,1,0:T(8,128)}, u32[]{:S(2)}) copy-start(f32[1,20,64,128]{3,2,1,0:T(8,128)} %get-tuple-element.21) | copy-start | bytes 1966084
  277.2 17.6 %collective-permute-start.4 = (f32[163968]{0:T(1024)}, f32[163968]{0:T(1024)}, u32[]{:S(2)}, u32[]{:S(2)}) collective-permute-start(f32[163968]{0:T(1024)} %select_maximum_fusion.1), channel_id=1, source_target_pairs={{0,32},{4,36},{8,40},{12,44},{16,48},{20,52},{24,56},{28,60},{32,6... | collective-permute-start | bytes 1967624 | tf_op jit(solution)/shard_map/ppermute | solution.py:14
  292.1 35.9 %copy-start.17 = (f32[8,256,20]{1,2,0:T(8,128)S(1)}, f32[8,256,20]{1,2,0:T(8,128)}, u32[]{:S(2)}) copy-start(f32[8,256,20]{1,2,0:T(8,128)} %copy.84) | copy-start | bytes 491524
  292.1 35.9 %copy-start.31 = (f32[20]{0:T(128)S(1)}, f32[20]{0:T(128)}, u32[]{:S(2)}) copy-start(f32[20]{0:T(128)} %param.13) | copy-start | bytes 244
  298.4 76.8 %collective-permute-start.5 = (f32[163968]{0:T(1024)}, f32[163968]{0:T(1024)}, u32[]{:S(2)}, u32[]{:S(2)}) collective-permute-start(f32[163968]{0:T(1024)} %select_maximum_fusion), channel_id=1, source_target_pairs={{0,64},{4,68},{8,72},{12,76},{16,80},{20,84},{24,88},{28,92},{32,9... | collective-permute-start | bytes 1967624 | tf_op jit(solution)/shard_map/ppermute | solution.py:14
  370.0 6.4 %copy-start.8 = (f32[163840]{0:T(1024)S(1)}, f32[163840]{0:T(1024)}, u32[]{:S(2)}) copy-start(f32[163840]{0:T(1024)} %get-tuple-element.51) | copy-start | bytes 1966084
  370.0 6.4 %copy-start.13 = (f32[163840]{0:T(1024)S(1)}, f32[163840]{0:T(1024)}, u32[]{:S(2)}) copy-start(f32[163840]{0:T(1024)} %get-tuple-element.49) | copy-start | bytes 1966084
  370.0 6.4 %copy-start.14 = (f32[163840]{0:T(1024)S(1)}, f32[163840]{0:T(1024)}, u32[]{:S(2)}) copy-start(f32[163840]{0:T(1024)} %get-tuple-element.47) | copy-start | bytes 1966084
  370.0 97.9 %all-to-all-start.2 = ((bf16[4,512,1280]{1,2,0:T(8,128)(2,1)}), bf16[4,512,1280]{1,2,0:T(8,128)(2,1)}, u32[]{:S(2)}, u32[]{:S(2)}) async-start(bf16[4,512,1280]{1,2,0:T(8,128)(2,1)} %copy.91), calls=%async_computation.2 | async-start | bytes 10485760 | tf_op jit(solution)/shard_map/all_to_all | solution.py:130
  375.1 3.5 copy-start.29
  375.1 82.1 %copy-start.16 = (bf16[512,80]{0,1:T(8,128)(2,1)S(1)}, bf16[512,80]{0,1:T(8,128)(2,1)}, u32[]{:S(2)}) copy-start(bf16[512,80]{0,1:T(8,128)(2,1)} %param.9) | copy-start | bytes 245764
  375.2 100.7 %all-gather.7.cloned.1.call-start = ((), (), s32[]{:S(2)}) async-start(), calls=%async_computation.4 | async-start | bytes 3276800 | tf_op jit(solution)/shard_map/all_gather | solution.py:150
Sparse Core Ops, SparseCore 0:
  26.1 35.3 all-gather.4
  378.7 56.5 all-gather.6

commit v4 on v3

--- a/solution.py
+++ b/solution.py
@@ -96,9 +96,11 @@
     block_decay = jnp.exp(ending)
     entering = []
     running = jnp.zeros_like(block_states[0])
+    decay_before = []
     running_decay = jnp.ones_like(block_decay[0])
     for k in range(block_count):
         entering.append(running)
+        decay_before.append(running_decay)
         running = block_decay[k][:, None, None] * running + block_states[k]
         running_decay = running_decay * block_decay[k]
     incoming = relay_states(running_decay, running, "ctx")
@@ -127,25 +129,12 @@
     )
 
     partial = known.astype(jnp.bfloat16).reshape(context, channels)
+    factor = (decay_in * jnp.stack(decay_before)[:, None, :]).reshape(context, heads_local)
     partial_tokens = lax.all_to_all(partial, "head", split_axis=0, concat_axis=1, tiled=True)
+    factor_tokens = lax.all_to_all(factor, "head", split_axis=0, concat_axis=1, tiled=True)
 
     tokens = inner_tokens.shape[0]
     group = lax.axis_index("head")
-    rates_all = lax.all_gather(head_rates, "head", axis=1, tiled=True)
-    step_tokens = jax.nn.softplus(step_raw.astype(jnp.float32) + rates_all[0][None, :])
-    decay_tokens = -step_tokens * jnp.exp(rates_all[1])[None, :]
-    cumulative_tokens = jnp.cumsum(decay_tokens.reshape(tokens // SPAN, SPAN, -1), axis=1)
-    ends_all = lax.all_gather(cumulative_tokens[:, -1, :], "head", axis=0, tiled=True)
-    exps_all = jnp.exp(ends_all)
-    before_all = []
-    running_decay = jnp.ones_like(exps_all[0])
-    for k in range(exps_all.shape[0]):
-        before_all.append(running_decay)
-        running_decay = running_decay * exps_all[k]
-    before_own = lax.dynamic_slice_in_dim(
-        jnp.stack(before_all), group * (tokens // SPAN), tokens // SPAN, axis=0
-    )
-    factor_tokens = (jnp.exp(cumulative_tokens) * before_own[:, None, :]).reshape(tokens, -1)
     c_tokens = lax.dynamic_slice_in_dim(c_rows, group * tokens, tokens, axis=0).astype(jnp.float32)
     incoming_all = lax.all_gather(incoming, "head", axis=0, tiled=True)
     carried_in = jnp.einsum(

time: 518 us -> 510 us (0.985)
  blocking collectives: 86.8 us -> 0 us
  waiting for transfers between devices: 103 us -> 180 us
    all_gather x2 -> x0, blocking collectives: 86.8 us -> none  [the longest x1 78.5 us: per_device(): rates_all = lax.all_gather(head_rates, 'head', axis=1, tiled=True)]
    all_to_all x1, waiting for transfers between devices: 0.01 us -> 77.5 us  [per_device(): lax.all_to_all(partial, 'head', split_axis=0, concat_axis=1, tiled=True)]
    mul x25 -> x24, local copies, waits for them, and re-layouts: 26.5 us -> 27 us  [per_device(): running = block_decay[k][:, None, None] * running + block_states[k]]
    unnamed x73 -> x70, local copies, waits for them, and re-layouts: 23.7 us -> 23.5 us
  transfers between devices with their start and end apart: 11 -> 12, of which waited for: 6 -> 7; matrix products, arithmetic and copies ran while one was open for 23% -> 27% of each run, Pallas kernels for 0% -> 0%
where the time goes in v4:
time: 510 us; the launch traced here: 505 us
  waiting for transfers between devices  180 us (35%)
  local copies, waits for them, and re-layouts  119 us (23%)
  starting transfers between devices  66.3 us (13%)
  other arithmetic  63.4 us (12%)
  matrix products  62.9 us (12%)
  between operations  14.3 us (3%)
    all_to_all x1, waiting for transfers between devices, per_device(): lax.all_to_all(partial, 'head', split_axis=0, concat_axis=1, tiled=True)  77.5 us
    ppermute x6, starting transfers between devices, from_behind(): return lax.ppermute(value, axis, pairs)  47.8 us
    ppermute x6, waiting for transfers between devices, from_behind(): return lax.ppermute(value, axis, pairs)  43.7 us
    all_gather x1, waiting for transfers between devices, per_device(): state_whole = lax.all_gather(state_inputs, 'head', axis=0, tiled=True)  29.3 us
    all_to_all x1, waiting for transfers between devices, per_device(): lax.all_to_all(inner_tokens, 'head', split_axis=1, concat_axis=0, tiled=T...  27.9 us
    mul x24, local copies, waits for them, and re-layouts, per_device(): running = block_decay[k][:, None, None] * running + block_states[k]  27 us
    unnamed x70, local copies, waits for them, and re-layouts  23.5 us
    dot_general x1, matrix products, per_device(): jnp.einsum('bhts,bshp->bthp', mixing, u_blocks, preferred_element_type=jn...  20.8 us
  transfers between devices with their start and end apart: 12, of which 7 were waited for; matrix products, arithmetic and copies ran while one was open for 27% of the time, Pallas kernels for 0%

profile of v4, /device:TPU:98, one launch (start us, length us, event | category | flops | bytes accessed | tf_op | source)
XLA Modules:
  0.0 505.3 jit_solution(6043641154321578979)
XLA Ops:
  6.5 1.5 all_to_all.50
  8.1 4.5 all-to-all-start.1
  12.5 5.2 %copy.114 = bf16[64,4,8,1280]{3,2,0,1:T(8,128)(2,1)} copy(bf16[64,4,8,1280]{3,2,1,0:T(8,128)(2,1)} %bitcast.173) | data formatting | bytes 10485760 | tf_op jit(solution)/shard_map/all_to_all | solution.py:60
  18.3 5.2 %all-to-all-start = ((bf16[512,4,1280]{2,0,1:T(8,128)(2,1)}), bf16[512,4,1280]{2,0,1:T(8,128)(2,1)}, u32[]{:S(2)}, u32[]{:S(2)}) async-start(bf16[512,4,1280]{2,0,1:T(8,128)(2,1)} %bitcast.150), calls=%async_computation | async-start | bytes 10485760 | tf_op jit(solution)/shard_map/all_to_all | solution.py:60
  24.9 4.6 reduce-window.6
  32.2 29.3 %all-gather.3.cloned.1.call-done = bf16[2048,256]{1,0:T(8,128)(2,1)} async-done(((bf16[512,256]{1,0:T(8,128)(2,1)}), bf16[2048,256]{1,0:T(8,128)(2,1)}) %all-gather.3.cloned.1.call-update) | async-done | bytes 1048592 | tf_op jit(solution)/shard_map/all_gather | solution.py:68
  62.2 1.4 convert_element_type.86
  63.6 27.9 %all-to-all-done = bf16[512,4,1280]{2,0,1:T(8,128)(2,1)} async-done(((bf16[512,4,1280]{2,0,1:T(8,128)(2,1)}), bf16[512,4,1280]{2,0,1:T(8,128)(2,1)}, u32[]{:S(2)}, u32[]{:S(2)}) %all-to-all-start) | async-done | bytes 5242912 | tf_op jit(solution)/shard_map/all_to_all | solution.py:60
  92.2 5.2 %collective-permute-start = (bf16[3,1536]{1,0:T(4,128)(2,1)S(1)}, bf16[3,1536]{1,0:T(4,128)(2,1)S(1)}, u32[]{:S(2)}, u32[]{:S(2)}) collective-permute-start(bf16[3,1536]{1,0:T(4,128)(2,1)S(1)} %pad_maximum_fusion.2), channel_id=1, source_target_pairs={{0,4},{4,8},{8,12},{12,16},{16,20},{20,24},{24,28},{28,32},{32,36}... | collective-permute-start | bytes 27656 | tf_op jit(solution)/shard_map/ppermute | solution.py:14
  97.5 3.3 bitcast_convert_fusion
  100.8 8.3 %fusion.23 = f32[2048,1280]{1,0:T(8,128)} fusion(f32[2048,1280]{1,0:T(8,128)S(1)} %bitcast_convert_fusion, f32[1280]{0:T(1024)S(1)} %get-tuple-element.8, f32[3,1280]{1,0:T(4,128)S(1)} %slice_convert_fusion, f32[1280]{0:T(1024)S(1)} %get-tuple-element.9, f32[1280]{0:T(1024)S(1)} %get-tuple-element.6, f32[1280]{0:T(1024)S(1)} %get-tuple-element.7, ...), kind=kLoop, calls=%fused_computation.32 | loop fusion | flops 44564480 | bytes 21012480 | tf_op jit(solution)/shard_map/convert_element_type | solution.py:82
  109.1 11.3 %copy.68 = f32[2048,1280]{0,1:T(8,128)} copy(f32[2048,1280]{1,0:T(8,128)} %fusion.23) | data formatting | bytes 20971520 | tf_op jit(solution)/shard_map/convert_element_type | solution.py:82
  120.4 13.2 %copy.95 = f32[160,8,8,256]{3,2,1,0:T(8,128)} copy(f32[160,8,8,256]{3,1,2,0:T(8,128)} %bitcast.148) | data formatting | bytes 20971520
  133.6 1.4 multiply_convert_fusion.6
  135.9 11.7 %convert_multiply_fusion = (f32[8,256,20,64]{1,0,3,2:T(8,128)}, bf16[8,256,20,64]{1,0,3,2:T(8,128)(2,1)}) fusion(f32[8,256,20]{1,0,2:T(8,128)S(1)} %get-tuple-element.53, f32[8,256,20,64]{1,0,3,2:T(8,128)} %bitcast.146, f32[8,256,20]{1,0,2:T(8,128)S(1)} %get-tuple-element.31), kind=kLoop, calls=%fused_computation.27 | loop fusion | flops 10485760 | bytes 26542080 | tf_op jit(solution)/shard_map/mul | solution.py:92
  147.5 12.7 %fusion.18 = f32[8,20,64,128]{3,2,1,0:T(8,128)S(1)} fusion(bf16[8,256,128,1]{2,1,3,0:T(8,128)(2,1)S(1)} %bitcast.171, f32[8,256,20,64]{1,0,3,2:T(8,128)} %get-tuple-element.28), kind=kOutput, calls=%fused_computation.25 | convolution fusion | flops 4026531840 | bytes 16252928 | tf_op jit(solution)/shard_map/bshp,bsn->bhpn/dot_general | solution.py:93
  160.5 2.8 multiply_add_fusion.4
  165.9 3.3 collective-permute-start.1
  170.8 1.0 mul.689
  171.8 2.1 mul.690
  173.9 1.7 mul.691
  175.5 2.2 mul.692
  177.7 1.6 mul.693
  179.3 2.1 mul.694
  181.4 1.0 mul.695
  182.4 2.1 mul.696
  184.5 1.0 mul.697
  185.5 2.1 mul.698
  188.7 2.1 mul.700
  190.8 1.0 mul.687
  191.8 2.1 mul.688
  193.9 1.0 mul.684
  194.9 2.2 mul.685
  198.0 2.1 mul.702
  200.9 1.6 copy.74
  204.2 3.4 all-to-all-start.3
  207.6 2.0 constant_dynamic-update-slice_fusion.6
  210.3 4.9 add_add_fusion.1
  216.9 3.2 collective-permute-start.2
  222.9 1.0 mul.713
  223.8 24.6 %collective-permute-done.2 = f32[163968]{0:T(1024)} collective-permute-done((f32[163968]{0:T(1024)}, f32[163968]{0:T(1024)}, u32[]{:S(2)}, u32[]{:S(2)}) %collective-permute-start.2) | collective-permute-done | bytes 655904 | tf_op jit(solution)/shard_map/ppermute | solution.py:14
  249.1 2.2 multiply_add_fusion.2
  252.2 3.9 collective-permute-start.3
  256.2 2.0 constant_dynamic-update-slice_fusion.2
  258.1 2.0 constant_dynamic-update-slice_fusion.1
  260.1 1.7 fusion.47
  262.9 16.7 %collective-permute-done.3 = f32[163968]{0:T(1024)} collective-permute-done((f32[163968]{0:T(1024)}, f32[163968]{0:T(1024)}, u32[]{:S(2)}, u32[]{:S(2)}) %collective-permute-start.3) | collective-permute-done | bytes 655904 | tf_op jit(solution)/shard_map/ppermute | solution.py:14
  280.4 2.2 multiply_add_fusion.1
  283.5 3.4 collective-permute-start.4
  287.8 10.6 %fusion.48 = f32[8,256,1280]{1,2,0:T(8,128)} fusion(bf16[8,256,128]{2,1,0:T(8,128)(2,1)S(1)} %bitcast.170, f32[8,1280,128]{2,1,0:T(8,128)} %constant_dynamic-update-slice_fusion), kind=kOutput, calls=%fused_computation.132 | convolution fusion | flops 4026531840 | bytes 16252928 | tf_op jit(solution)/shard_map/btn,bkn->btk/dot_general | solution.py:121
  298.6 2.4 collective-permute-done.4
  301.7 2.0 multiply_add_fusion
  303.8 28.8 %collective-permute-start.5 = (f32[163968]{0:T(1024)S(1)}, f32[163968]{0:T(1024)S(1)}, u32[]{:S(2)}, u32[]{:S(2)}) collective-permute-start(f32[163968]{0:T(1024)S(1)} %select_maximum_fusion), channel_id=1, source_target_pairs={{0,64},{4,68},{8,72},{12,76},{16,80},{20,84},{24,88},{28,92},{32,9... | collective-permute-start | bytes 1967624 | tf_op jit(solution)/shard_map/ppermute | solution.py:14
  332.6 20.8 %fusion.16 = bf16[8,256,20,64]{1,3,2,0:T(8,128)(2,1)S(1)} fusion(f32[8,256,20,64]{1,0,3,2:T(8,128)} %bitcast.147, f32[8,256,20,64]{1,3,2,0:T(8,128)} %bitcast.152, f32[8,20,256]{2,1,0:T(8,128)S(1)} %copy-done.17, f32[8,256,256]{2,1,0:T(8,128)} %fusion.47, pred[256,256]{1,0:T(8,128)(4,1)S(1)} %iota_compare_fusion.1, ...), kind=kOutput, calls=%fused_computation.21 | convolution fusion | flops 1397227520 | bytes 33947728 | tf_op jit(solution)/shard_map/bhts,bshp->bthp/dot_general | solution.py:116
  353.5 6.0 %copy.83 = bf16[8,256,20,64]{1,0,3,2:T(8,128)(2,1)} copy(bf16[8,256,20,64]{1,3,2,0:T(8,128)(2,1)S(1)} %fusion.16) | data formatting | bytes 10485760 | tf_op jit(solution)/shard_map/convert_element_type | solution.py:131
  359.5 9.2 %all_to_all.52 = bf16[4,512,1280]{1,0,2:T(4,128)(2,1)} reshape(bf16[8,256,20,64]{1,0,3,2:T(8,128)(2,1)} %copy.83) | data formatting | bytes 10485760 | tf_op jit(solution)/shard_map/all_to_all | solution.py:133
  368.8 5.9 %copy.84 = bf16[4,512,1280]{1,2,0:T(8,128)(2,1)} copy(bf16[4,512,1280]{1,0,2:T(4,128)(2,1)} %all_to_all.52) | data formatting | bytes 10485760 | tf_op jit(solution)/shard_map/all_to_all | solution.py:133
  374.8 5.2 %all-to-all-start.2 = ((bf16[4,512,1280]{1,2,0:T(8,128)(2,1)}), bf16[4,512,1280]{1,2,0:T(8,128)(2,1)}, u32[]{:S(2)}, u32[]{:S(2)}) async-start(bf16[4,512,1280]{1,2,0:T(8,128)(2,1)} %copy.84), calls=%async_computation.2 | async-start | bytes 10485760 | tf_op jit(solution)/shard_map/all_to_all | solution.py:133
  380.2 2.2 add_add_fusion
  382.4 77.5 %all-to-all-done.2 = bf16[4,512,1280]{1,2,0:T(8,128)(2,1)} async-done(((bf16[4,512,1280]{1,2,0:T(8,128)(2,1)}), bf16[4,512,1280]{1,2,0:T(8,128)(2,1)}, u32[]{:S(2)}, u32[]{:S(2)}) %all-to-all-start.2) | async-done | bytes 5242912 | tf_op jit(solution)/shard_map/all_to_all | solution.py:133
  460.0 8.0 %convert_element_type.99 = f32[4,512,1280]{1,2,0:T(8,128)} convert(bf16[4,512,1280]{1,2,0:T(8,128)(2,1)} %all-to-all-done.2) | non-fusion elementwise | flops 2621440 | bytes 15728640 | tf_op jit(solution)/shard_map/convert_element_type | solution.py:146
  467.9 17.1 %fusion.17 = bf16[512,80,64]{0,1,2:T(8,128)(2,1)S(1)} fusion(f32[512,80,64]{0,2,1:T(8,128)} %bitcast.149, f32[512,80]{0,1:T(8,128)S(1)} %mul.650, f32[80,64,128]{2,1,0:T(8,128)} %all-gather.5.cloned.1.call-done, bf16[2048,128]{1,0:T(8,128)(2,1)S(1)} %copy-done.5, s32[]{:T(128)S(6)} %select_n.18), kind=kOutput, calls=%fused_computation.23 | convolution fusion | flops 4034396160 | bytes 18644996 | tf_op jit(solution)/shard_map/tn,kn->tk/dot_general | solution.py:140
  485.1 5.3 %copy.89 = bf16[512,80,64]{0,2,1:T(8,128)(2,1)} copy(bf16[512,80,64]{0,1,2:T(8,128)(2,1)S(1)} %fusion.17) | data formatting | bytes 10485760 | tf_op jit(solution)/shard_map/convert_element_type | solution.py:149
  490.4 7.9 %copy.90 = bf16[512,5120]{1,0:T(8,128)(2,1)} copy(bf16[512,5120]{0,1:T(8,128)(2,1)} %bitcast.151) | data formatting | bytes 10485760 | tf_op jit(solution)/shard_map/reshape | solution.py:149
  (141 shorter events, 27.1 us)
Async XLA Ops:
  8.1 10.3 %all-to-all-start.1 = ((bf16[512,4,20]{0,2,1:T(8,128)(2,1)}), bf16[512,4,20]{0,2,1:T(8,128)(2,1)S(1)}, u32[]{:S(2)}, u32[]{:S(2)}) async-start(bf16[512,4,20]{0,2,1:T(8,128)(2,1)} %all_to_all.50), calls=%async_computation.1 | async-start | bytes 196608 | tf_op jit(solution)/shard_map/all_to_all | solution.py:61
  18.3 6.0 %copy-start.18 = (f32[5,1280]{1,0:T(8,128)S(1)}, f32[5,1280]{1,0:T(8,128)}, u32[]{:S(2)}) copy-start(f32[5,1280]{1,0:T(8,128)} %param.10) | copy-start | bytes 76804
  18.3 6.1 %copy-start.29 = (f32[2,20]{1,0:T(2,128)S(1)}, f32[2,20]{1,0:T(2,128)}, u32[]{:S(2)}) copy-start(f32[2,20]{1,0:T(2,128)} %param.12) | copy-start | bytes 484
  18.3 6.1 %copy-start.28 = (f32[5,256]{1,0:T(8,128)S(1)}, f32[5,256]{1,0:T(8,128)}, u32[]{:S(2)}) copy-start(f32[5,256]{1,0:T(8,128)} %param.11) | copy-start | bytes 15364
  18.3 73.2 %all-to-all-start = ((bf16[512,4,1280]{2,0,1:T(8,128)(2,1)}), bf16[512,4,1280]{2,0,1:T(8,128)(2,1)}, u32[]{:S(2)}, u32[]{:S(2)}) async-start(bf16[512,4,1280]{2,0,1:T(8,128)(2,1)} %bitcast.150), calls=%async_computation | async-start | bytes 10485760 | tf_op jit(solution)/shard_map/all_to_all | solution.py:60
  23.6 37.9 %all-gather.3.cloned.1.call-start = ((), (), s32[]{:S(2)}) async-start(), calls=%async_computation.4 | async-start | bytes 1310720 | tf_op jit(solution)/shard_map/all_gather | solution.py:68
  31.2 132.0 %copy-start.21 = (f32[20]{0:T(128)}, f32[20]{0:T(128)S(1)}, u32[]{:S(2)}) copy-start(f32[20]{0:T(128)S(1)} %get-tuple-element.62) | copy-start | bytes 244
  31.3 132.1 %copy-start.20 = (f32[20]{0:T(128)}, f32[20]{0:T(128)S(1)}, u32[]{:S(2)}) copy-start(f32[20]{0:T(128)S(1)} %get-tuple-element.68) | copy-start | bytes 244
  31.3 132.3 %copy-start.19 = (f32[20]{0:T(128)}, f32[20]{0:T(128)S(1)}, u32[]{:S(2)}) copy-start(f32[20]{0:T(128)S(1)} %get-tuple-element.67) | copy-start | bytes 244
  31.3 132.7 %copy-start.26 = (f32[20]{0:T(128)}, f32[20]{0:T(128)S(1)}, u32[]{:S(2)}) copy-start(f32[20]{0:T(128)S(1)} %get-tuple-element.59) | copy-start | bytes 244
  31.4 133.5 %copy-start.23 = (f32[20]{0:T(128)}, f32[20]{0:T(128)S(1)}, u32[]{:S(2)}) copy-start(f32[20]{0:T(128)S(1)} %get-tuple-element.60) | copy-start | bytes 244
  92.2 8.5 %collective-permute-start = (bf16[3,1536]{1,0:T(4,128)(2,1)S(1)}, bf16[3,1536]{1,0:T(4,128)(2,1)S(1)}, u32[]{:S(2)}, u32[]{:S(2)}) collective-permute-start(bf16[3,1536]{1,0:T(4,128)(2,1)S(1)} %pad_maximum_fusion.2), channel_id=1, source_target_pairs={{0,4},{4,8},{8,12},{12,16},{16,20},{20,24},{24,28},{28,32},{32,36}... | collective-permute-start | bytes 27656 | tf_op jit(solution)/shard_map/ppermute | solution.py:14
  135.9 11.7 %copy-start.6 = (bf16[2048,128]{1,0:T(8,128)(2,1)}, bf16[2048,128]{1,0:T(8,128)(2,1)S(1)}, u32[]{:S(2)}) copy-start(bf16[2048,128]{1,0:T(8,128)(2,1)S(1)} %get-tuple-element.40) | copy-start | bytes 1572868
  160.4 3.8 copy-start.2
  160.4 3.8 copy-start.3
  160.4 3.8 copy-start.4
  164.3 6.5 %copy-start.22 = (f32[20]{0:T(128)S(1)}, f32[20]{0:T(128)}, u32[]{:S(2)}) copy-start(f32[20]{0:T(128)} %copy-done.21) | copy-start | bytes 244
  165.9 43.7 %collective-permute-start.1 = (f32[163968]{0:T(1024)}, f32[163968]{0:T(1024)}, u32[]{:S(2)}, u32[]{:S(2)}) collective-permute-start(f32[163968]{0:T(1024)} %select_maximum_fusion.4), channel_id=1, source_target_pairs={{0,4},{4,8},{8,12},{12,16},{16,20},{20,24},{24,28},{28,32},{32,36}... | collective-permute-start | bytes 1967624 | tf_op jit(solution)/shard_map/ppermute | solution.py:14
  175.5 15.2 %copy-start.27 = (f32[20]{0:T(128)S(1)}, f32[20]{0:T(128)}, u32[]{:S(2)}) copy-start(f32[20]{0:T(128)} %copy-done.26) | copy-start | bytes 244
  179.3 14.6 %copy-start.24 = (f32[20]{0:T(128)S(1)}, f32[20]{0:T(128)}, u32[]{:S(2)}) copy-start(f32[20]{0:T(128)} %copy-done.23) | copy-start | bytes 244
  185.5 14.6 %copy-start.15 = (f32[8,256,20]{1,0,2:T(8,128)S(1)}, f32[8,256,20]{1,0,2:T(8,128)}, u32[]{:S(2)}) copy-start(f32[8,256,20]{1,0,2:T(8,128)} %get-tuple-element.19) | copy-start | bytes 491524
  190.8 18.8 %copy-start.25 = (f32[20]{0:T(128)S(1)}, f32[20]{0:T(128)}, u32[]{:S(2)}) copy-start(f32[20]{0:T(128)} %copy-done.23) | copy-start | bytes 244
  204.2 170.5 %all-to-all-start.3 = ((f32[4,512,20]{1,2,0:T(8,128)}), f32[4,512,20]{1,2,0:T(8,128)S(1)}, u32[]{:S(2)}, u32[]{:S(2)}) async-start(f32[4,512,20]{1,2,0:T(8,128)} %copy.86), calls=%async_computation.3 | async-start | bytes 393216 | tf_op jit(solution)/shard_map/all_to_all | solution.py:134
  210.3 9.8 %copy-start.12 = (f32[1,20,64,128]{3,2,1,0:T(8,128)S(1)}, f32[1,20,64,128]{3,2,1,0:T(8,128)}, u32[]{:S(2)}) copy-start(f32[1,20,64,128]{3,2,1,0:T(8,128)} %get-tuple-element.26) | copy-start | bytes 1966084
  210.3 10.7 %copy-start.11 = (f32[1,20,64,128]{3,2,1,0:T(8,128)S(1)}, f32[1,20,64,128]{3,2,1,0:T(8,128)}, u32[]{:S(2)}) copy-start(f32[1,20,64,128]{3,2,1,0:T(8,128)} %get-tuple-element.25) | copy-start | bytes 1966084
  210.3 11.6 %copy-start.10 = (f32[1,20,64,128]{3,2,1,0:T(8,128)S(1)}, f32[1,20,64,128]{3,2,1,0:T(8,128)}, u32[]{:S(2)}) copy-start(f32[1,20,64,128]{3,2,1,0:T(8,128)} %get-tuple-element.24) | copy-start | bytes 1966084
  215.2 0.8 copy-start
  216.9 32.2 %copy-start.1 = (f32[163840]{0:T(1024)S(1)}, f32[163840]{0:T(1024)}, u32[]{:S(2)}) copy-start(f32[163840]{0:T(1024)} %copy-done) | copy-start | bytes 1966084
  216.9 31.5 %collective-permute-start.2 = (f32[163968]{0:T(1024)}, f32[163968]{0:T(1024)}, u32[]{:S(2)}, u32[]{:S(2)}) collective-permute-start(f32[163968]{0:T(1024)} %select_maximum_fusion.3), channel_id=1, source_target_pairs={{0,8},{4,12},{8,16},{12,20},{16,24},{20,28},{24,32},{28,36},{32,40... | collective-permute-start | bytes 1967624 | tf_op jit(solution)/shard_map/ppermute | solution.py:14
  221.8 38.3 %copy-start.5 = (bf16[2048,128]{1,0:T(8,128)(2,1)S(1)}, bf16[2048,128]{1,0:T(8,128)(2,1)}, u32[]{:S(2)}) copy-start(bf16[2048,128]{1,0:T(8,128)(2,1)} %get-tuple-element.41) | copy-start | bytes 1572868
  221.8 38.3 %copy-start.7 = (bf16[2048,128]{1,0:T(8,128)(2,1)S(1)}, bf16[2048,128]{1,0:T(8,128)(2,1)}, u32[]{:S(2)}) copy-start(bf16[2048,128]{1,0:T(8,128)(2,1)} %copy-done.6) | copy-start | bytes 1572868
  252.2 27.4 %collective-permute-start.3 = (f32[163968]{0:T(1024)}, f32[163968]{0:T(1024)}, u32[]{:S(2)}, u32[]{:S(2)}) collective-permute-start(f32[163968]{0:T(1024)} %select_maximum_fusion.2), channel_id=1, source_target_pairs={{0,16},{4,20},{8,24},{12,28},{16,32},{20,36},{24,40},{28,44},{32,4... | collective-permute-start | bytes 1967624 | tf_op jit(solution)/shard_map/ppermute | solution.py:14
  260.1 26.8 %copy-start.9 = (f32[1,20,64,128]{3,2,1,0:T(8,128)S(1)}, f32[1,20,64,128]{3,2,1,0:T(8,128)}, u32[]{:S(2)}) copy-start(f32[1,20,64,128]{3,2,1,0:T(8,128)} %get-tuple-element.21) | copy-start | bytes 1966084
  283.5 17.6 %collective-permute-start.4 = (f32[163968]{0:T(1024)}, f32[163968]{0:T(1024)}, u32[]{:S(2)}, u32[]{:S(2)}) collective-permute-start(f32[163968]{0:T(1024)} %select_maximum_fusion.1), channel_id=1, source_target_pairs={{0,32},{4,36},{8,40},{12,44},{16,48},{20,52},{24,56},{28,60},{32,6... | collective-permute-start | bytes 1967624 | tf_op jit(solution)/shard_map/ppermute | solution.py:14
  298.4 34.3 %copy-start.16 = (f32[8,256,20]{1,2,0:T(8,128)S(1)}, f32[8,256,20]{1,2,0:T(8,128)}, u32[]{:S(2)}) copy-start(f32[8,256,20]{1,2,0:T(8,128)} %copy.77) | copy-start | bytes 491524
  298.4 34.3 %copy-start.17 = (f32[8,20,256]{2,1,0:T(8,128)S(1)}, f32[8,20,256]{2,1,0:T(8,128)}, u32[]{:S(2)}) copy-start(f32[8,20,256]{2,1,0:T(8,128)} %copy.74) | copy-start | bytes 491524
  298.4 34.3 %copy-start.30 = (f32[20]{0:T(128)S(1)}, f32[20]{0:T(128)}, u32[]{:S(2)}) copy-start(f32[20]{0:T(128)} %param.13) | copy-start | bytes 244
  303.8 70.9 %collective-permute-start.5 = (f32[163968]{0:T(1024)S(1)}, f32[163968]{0:T(1024)S(1)}, u32[]{:S(2)}, u32[]{:S(2)}) collective-permute-start(f32[163968]{0:T(1024)S(1)} %select_maximum_fusion), channel_id=1, source_target_pairs={{0,64},{4,68},{8,72},{12,76},{16,80},{20,84},{24,88},{28,92},{32,9... | collective-permute-start | bytes 1967624 | tf_op jit(solution)/shard_map/ppermute | solution.py:14
  374.7 5.4 %copy-start.8 = (f32[163840]{0:T(1024)S(1)}, f32[163840]{0:T(1024)}, u32[]{:S(2)}) copy-start(f32[163840]{0:T(1024)} %get-tuple-element.51) | copy-start | bytes 1966084
  374.7 5.4 %copy-start.13 = (f32[163840]{0:T(1024)S(1)}, f32[163840]{0:T(1024)}, u32[]{:S(2)}) copy-start(f32[163840]{0:T(1024)} %get-tuple-element.49) | copy-start | bytes 1966084
  374.7 5.4 %copy-start.14 = (f32[163840]{0:T(1024)S(1)}, f32[163840]{0:T(1024)}, u32[]{:S(2)}) copy-start(f32[163840]{0:T(1024)} %get-tuple-element.47) | copy-start | bytes 1966084
  374.8 85.2 %all-to-all-start.2 = ((bf16[4,512,1280]{1,2,0:T(8,128)(2,1)}), bf16[4,512,1280]{1,2,0:T(8,128)(2,1)}, u32[]{:S(2)}, u32[]{:S(2)}) async-start(bf16[4,512,1280]{1,2,0:T(8,128)(2,1)} %copy.84), calls=%async_computation.2 | async-start | bytes 10485760 | tf_op jit(solution)/shard_map/all_to_all | solution.py:133
  379.9 88.0 %all-gather.5.cloned.1.call-start = ((), (), s32[]{:S(2)}) async-start(), calls=%async_computation.5 | async-start | bytes 3276800 | tf_op jit(solution)/shard_map/all_gather | solution.py:139
Sparse Core Ops, SparseCore 0:
  26.2 35.2 all-gather.2
  382.6 56.5 all-gather.4

commit v5 on v4

--- a/solution.py
+++ b/solution.py
@@ -72,7 +72,7 @@
     previous_rows = from_behind(edge_rows, "ctx", 1)
     x_previous = previous_rows[:, :channels]
     state_conv = silu_conv(state_whole, previous_rows[:, channels:], conv_state)
-    inner_conv = silu_conv(x_local, x_previous, conv_inner)
+    inner_conv = lax.optimization_barrier(silu_conv(x_local, x_previous, conv_inner))
     state_width = state_conv.shape[1] // 2
     b_rows = state_conv[:, :state_width]
     c_rows = state_conv[:, state_width:]
@@ -90,8 +90,13 @@
 
     weights = jnp.exp(ending[:, None, :] - cumulative)
     scaled = weights[:, :, :, None] * u_blocks.astype(jnp.float32)
+    scaled_high = scaled.astype(jnp.bfloat16)
+    scaled_low = (scaled - scaled_high.astype(jnp.float32)).astype(jnp.bfloat16)
     block_states = jnp.einsum(
-        "bshp,bsn->bhpn", scaled, b_blocks.astype(jnp.float32), precision=lax.Precision.HIGHEST
+        "bshp,bsn->bhpn",
+        jnp.concatenate([scaled_high, scaled_low], axis=1),
+        jnp.concatenate([b_blocks, b_blocks], axis=1),
+        preferred_element_type=jnp.float32,
     )
     block_decay = jnp.exp(ending)
     entering = []

time: 510 us -> 497 us (0.975)
  local copies, waits for them, and re-layouts: 119 us -> 103 us
  other arithmetic: 63.4 us -> 73.4 us
  matrix products: 62.9 us -> 55.7 us
    mul x24, local copies, waits for them, and re-layouts: 27 us -> 13.8 us  [per_device(): running = block_decay[k][:, None, None] * running + block_states[k]]
    mul x1 -> x0, other arithmetic: 11.7 us -> none  [per_device(): scaled = weights[:, :, :, None] * u_blocks.astype(jnp.float32)]
    convert_element_type x1 -> x2, other arithmetic: 8.33 us -> 19.7 us  [the longest x1 12.7 us: per_device(): scaled_high = scaled.astype(jnp.bfloat16)]
    convert_element_type x1 -> x2, other arithmetic: 1.44 us -> 9.27 us  [silu_conv(): return jax.nn.silu(summed).astype(jnp.bfloat16)]
    dot_general x1, matrix products: 12.7 us -> 5.81 us  [per_device(): jnp.einsum('bshp,bsn->bhpn', jnp.concatenate([scaled_high, scaled_low], a...]
    unnamed x70 -> x92, local copies, waits for them, and re-layouts: 23.5 us -> 23.2 us
  transfers between devices with their start and end apart: 12 -> 12, of which waited for: 7 -> 7; matrix products, arithmetic and copies ran while one was open for 27% -> 25% of each run, Pallas kernels for 0% -> 0%
where the time goes in v5:
time: 497 us; the launch traced here: 491 us
  waiting for transfers between devices  178 us (36%)
  local copies, waits for them, and re-layouts  103 us (21%)
  other arithmetic  73.4 us (15%)
  starting transfers between devices  66.5 us (13%)
  matrix products  55.7 us (11%)
  between operations  14.5 us (3%)
    all_to_all x1, waiting for transfers between devices, per_device(): lax.all_to_all(partial, 'head', split_axis=0, concat_axis=1, tiled=True)  76.4 us
    ppermute x6, starting transfers between devices, from_behind(): return lax.ppermute(value, axis, pairs)  47.4 us
    ppermute x6, waiting for transfers between devices, from_behind(): return lax.ppermute(value, axis, pairs)  44.1 us
    all_gather x1, waiting for transfers between devices, per_device(): state_whole = lax.all_gather(state_inputs, 'head', axis=0, tiled=True)  28.1 us
    all_to_all x1, waiting for transfers between devices, per_device(): lax.all_to_all(inner_tokens, 'head', split_axis=1, concat_axis=0, tiled=T...  27.9 us
    unnamed x92, local copies, waits for them, and re-layouts  23.2 us
    dot_general x1, matrix products, per_device(): jnp.einsum('bhts,bshp->bthp', mixing, u_blocks, preferred_element_type=jn...  19.3 us
    dot_general x1, matrix products, per_device(): jnp.einsum('tn,kn->tk', c_tokens, incoming_all.reshape(-1, state_width),...  17.1 us
  transfers between devices with their start and end apart: 12, of which 7 were waited for; matrix products, arithmetic and copies ran while one was open for 25% of the time, Pallas kernels for 0%

profile of v5, /device:TPU:98, one launch (start us, length us, event | category | flops | bytes accessed | tf_op | source)
XLA Modules:
  0.0 490.7 jit_solution(17849396719470873063)
XLA Ops:
  6.5 1.6 all_to_all.50
  8.1 4.5 all-to-all-start.1
  12.6 5.2 %copy.111 = bf16[64,4,8,1280]{3,2,0,1:T(8,128)(2,1)} copy(bf16[64,4,8,1280]{3,2,1,0:T(8,128)(2,1)} %bitcast.172) | data formatting | bytes 10485760 | tf_op jit(solution)/shard_map/all_to_all | solution.py:60
  18.4 5.2 %all-to-all-start = ((bf16[512,4,1280]{2,0,1:T(8,128)(2,1)}), bf16[512,4,1280]{2,0,1:T(8,128)(2,1)}, u32[]{:S(2)}, u32[]{:S(2)}) async-start(bf16[512,4,1280]{2,0,1:T(8,128)(2,1)} %bitcast.151), calls=%async_computation | async-start | bytes 10485760 | tf_op jit(solution)/shard_map/all_to_all | solution.py:60
  24.9 4.6 reduce-window.6
  33.4 28.1 %all-gather.3.cloned.1.call-done = bf16[2048,256]{1,0:T(8,128)(2,1)} async-done(((bf16[512,256]{1,0:T(8,128)(2,1)}), bf16[2048,256]{1,0:T(8,128)(2,1)}) %all-gather.3.cloned.1.call-update) | async-done | bytes 1048592 | tf_op jit(solution)/shard_map/all_gather | solution.py:68
  62.2 1.4 convert_element_type.94
  63.6 27.9 %all-to-all-done = bf16[512,4,1280]{2,0,1:T(8,128)(2,1)} async-done(((bf16[512,4,1280]{2,0,1:T(8,128)(2,1)}), bf16[512,4,1280]{2,0,1:T(8,128)(2,1)}, u32[]{:S(2)}, u32[]{:S(2)}) %all-to-all-start) | async-done | bytes 5242912 | tf_op jit(solution)/shard_map/all_to_all | solution.py:60
  92.3 5.0 %collective-permute-start = (bf16[3,1536]{1,0:T(4,128)(2,1)S(1)}, bf16[3,1536]{1,0:T(4,128)(2,1)S(1)}, u32[]{:S(2)}, u32[]{:S(2)}) collective-permute-start(bf16[3,1536]{1,0:T(4,128)(2,1)S(1)} %pad_maximum_fusion.2), channel_id=1, source_target_pairs={{0,4},{4,8},{8,12},{12,16},{16,20},{20,24},{24,28},{28,32},{32,36}... | collective-permute-start | bytes 27656 | tf_op jit(solution)/shard_map/ppermute | solution.py:14
  97.3 3.3 bitcast_convert_fusion
  100.6 7.8 %multiply_convert_fusion.3 = bf16[2048,1280]{1,0:T(8,128)(2,1)} fusion(f32[2048,1280]{1,0:T(8,128)S(1)} %bitcast_convert_fusion, f32[3,1280]{1,0:T(4,128)S(1)} %slice_convert_fusion, f32[1280]{0:T(1024)S(1)} %get-tuple-element.8, f32[1280]{0:T(1024)S(1)} %get-tuple-element.9, f32[1280]{0:T(1024)S(1)} %get-tuple-element.6, f32[1280]{0:T(1024)S(1)} %get-tuple-element.7, ...), kind=kLoop, calls=%fused_computation.32 | loop fusion | flops 41943040 | bytes 15769600 | tf_op jit(solution)/shard_map/convert_element_type | solution.py:26
  108.4 8.7 %copy.70 = f32[2048,1280]{0,1:T(8,128)} copy(bf16[2048,1280]{1,0:T(8,128)(2,1)} %multiply_convert_fusion.3) | data formatting | bytes 15728640 | tf_op jit(solution)/shard_map/convert_element_type | solution.py:82
  117.2 13.2 %copy.98 = f32[160,8,8,256]{3,2,1,0:T(8,128)} copy(f32[160,8,8,256]{3,1,2,0:T(8,128)} %bitcast.149) | data formatting | bytes 20971520
  130.4 12.7 %fusion.22 = (bf16[8,256,20,64]{1,3,2,0:T(8,128)(2,1)}, bf16[8,256,20,64]{1,3,2,0:T(8,128)(2,1)}) fusion(f32[8,256,20]{1,2,0:T(8,128)S(1)} %copy.83, f32[8,256,20]{1,2,0:T(8,128)S(1)} %copy.72, f32[8,256,20,64]{1,0,3,2:T(8,128)} %bitcast.147), kind=kLoop, calls=%fused_computation.30 | loop fusion | flops 13107200 | bytes 21299200 | tf_op jit(solution)/shard_map/convert_element_type | solution.py:93
  143.0 7.0 %subtract_convert_fusion = bf16[8,256,20,64]{1,3,2,0:T(8,128)(2,1)} fusion(bf16[8,256,20,64]{1,3,2,0:T(8,128)(2,1)} %get-tuple-element.29, f32[8,256,20]{1,2,0:T(8,128)S(1)} %copy.83), kind=kLoop, calls=%fused_computation.28 | loop fusion | flops 15728640 | bytes 10649600 | tf_op jit(solution)/shard_map/convert_element_type | solution.py:94
  150.1 1.4 multiply_convert_fusion.6
  152.4 5.8 %fusion.15 = f32[8,20,64,128]{3,2,1,0:T(8,128)S(1)} fusion(bf16[8,256,20,64]{1,3,2,0:T(8,128)(2,1)} %subtract_convert_fusion, bf16[8,256,20,64]{1,3,2,0:T(8,128)(2,1)} %get-tuple-element.28, bf16[8,256,128]{2,1,0:T(8,128)(2,1)S(1)} %bitcast.193), kind=kOutput, calls=%fused_computation.19 | convolution fusion | flops 1365245952 | bytes 16252928 | tf_op jit(solution)/shard_map/bshp,bsn->bhpn/dot_general | solution.py:95
  158.4 3.3 multiply_add_fusion.4
  164.5 3.4 collective-permute-start.1
  170.3 1.0 mul.690
  171.4 1.0 mul.692
  172.5 1.0 mul.694
  173.6 1.0 mul.696
  174.8 1.0 mul.698
  175.9 1.0 mul.700
  176.9 1.0 mul.687
  177.9 2.1 mul.688
  180.0 1.0 mul.684
  181.0 2.1 mul.685
  183.2 1.0 mul.701
  184.2 2.1 mul.702
  187.0 1.7 copy.78
  188.7 1.0 all_to_all.54
  190.4 4.0 all-to-all-start.3
  194.4 2.0 constant_dynamic-update-slice_fusion.6
  197.1 5.0 %add_add_fusion.1 = (f32[163840]{0:T(1024)S(1)}, f32[163840]{0:T(1024)}) fusion(f32[163840]{0:T(1024)} %bitcast.167, f32[163840]{0:T(1024)} %mul.688, f32[163840]{0:T(1024)} %bitcast.169, f32[163840]{0:T(1024)} %mul.690, f32[163840]{0:T(1024)} %bitcast.165, f32[163840]{0:T(1024)} %mul.692, f32[163840]{0:T(1024)S(1)} %bitcast.163, f32[163840]{0:T(1024)} %mul.694, ...), kind=kLoop, calls=%fused_computation.61 | loop fusion | flops 2785280 | bytes 13107200 | tf_op jit(solution)/shard_map/add | solution.py:44
  203.9 3.0 collective-permute-start.2
  209.6 1.0 mul.713
  210.6 24.6 %collective-permute-done.2 = f32[163968]{0:T(1024)} collective-permute-done((f32[163968]{0:T(1024)}, f32[163968]{0:T(1024)}, u32[]{:S(2)}, u32[]{:S(2)}) %collective-permute-start.2) | collective-permute-done | bytes 655904 | tf_op jit(solution)/shard_map/ppermute | solution.py:14
  235.9 2.2 multiply_add_fusion.2
  239.0 4.0 collective-permute-start.3
  243.0 2.0 constant_dynamic-update-slice_fusion.2
  245.8 2.8 fusion.49
  248.8 1.0 mul.718
  249.7 16.8 %collective-permute-done.3 = f32[163968]{0:T(1024)} collective-permute-done((f32[163968]{0:T(1024)}, f32[163968]{0:T(1024)}, u32[]{:S(2)}, u32[]{:S(2)}) %collective-permute-start.3) | collective-permute-done | bytes 655904 | tf_op jit(solution)/shard_map/ppermute | solution.py:14
  267.2 2.2 multiply_add_fusion.1
  269.5 0.9 select_maximum_fusion.1
  270.4 3.2 collective-permute-start.4
  274.5 10.6 %fusion.50 = f32[8,256,1280]{1,2,0:T(8,128)} fusion(bf16[8,256,128]{2,1,0:T(8,128)(2,1)S(1)} %bitcast.171, f32[8,1280,128]{2,1,0:T(8,128)} %constant_dynamic-update-slice_fusion), kind=kOutput, calls=%fused_computation.137 | convolution fusion | flops 4026531840 | bytes 16252928 | tf_op jit(solution)/shard_map/btn,bkn->btk/dot_general | solution.py:126
  285.4 2.7 collective-permute-done.4
  288.7 2.1 multiply_add_fusion
  290.9 28.8 %collective-permute-start.5 = (f32[163968]{0:T(1024)S(1)}, f32[163968]{0:T(1024)S(1)}, u32[]{:S(2)}, u32[]{:S(2)}) collective-permute-start(f32[163968]{0:T(1024)S(1)} %select_maximum_fusion), channel_id=1, source_target_pairs={{0,64},{4,68},{8,72},{12,76},{16,80},{20,84},{24,88},{28,92},{32,9... | collective-permute-start | bytes 1967624 | tf_op jit(solution)/shard_map/ppermute | solution.py:14
  319.7 19.3 %fusion.20 = bf16[8,256,20,64]{1,3,2,0:T(8,128)(2,1)S(1)} fusion(f32[8,256,20,64]{1,3,2,0:T(8,128)} %bitcast.153, f32[8,256,20,64]{1,0,3,2:T(8,128)} %bitcast.148, f32[20]{0:T(128)S(1)} %copy-done.41, f32[8,256,20]{1,2,0:T(8,128)S(1)} %copy-done.23, bf16[8,256,20,64]{1,3,2,0:T(8,128)(2,1)} %get-tuple-element.29, f32[8,20,256]{2,1,0:T(8,128)S(1)} %copy-done.24, ...), kind=kOutput, calls=%fused_computation.25 | convolution fusion | flops 1397227520 | bytes 33947728 | tf_op jit(solution)/shard_map/bhts,bshp->bthp/dot_general | solution.py:121
  339.0 6.0 %copy.86 = bf16[8,256,20,64]{1,0,3,2:T(8,128)(2,1)} copy(bf16[8,256,20,64]{1,3,2,0:T(8,128)(2,1)S(1)} %fusion.20) | data formatting | bytes 10485760 | tf_op jit(solution)/shard_map/convert_element_type | solution.py:136
  345.1 9.2 %all_to_all.52 = bf16[4,512,1280]{1,0,2:T(4,128)(2,1)} reshape(bf16[8,256,20,64]{1,0,3,2:T(8,128)(2,1)} %copy.86) | data formatting | bytes 10485760 | tf_op jit(solution)/shard_map/all_to_all | solution.py:138
  354.3 5.9 %copy.87 = bf16[4,512,1280]{1,2,0:T(8,128)(2,1)} copy(bf16[4,512,1280]{1,0,2:T(4,128)(2,1)} %all_to_all.52) | data formatting | bytes 10485760 | tf_op jit(solution)/shard_map/all_to_all | solution.py:138
  360.3 5.2 %all-to-all-start.2 = ((bf16[4,512,1280]{1,2,0:T(8,128)(2,1)}), bf16[4,512,1280]{1,2,0:T(8,128)(2,1)}, u32[]{:S(2)}, u32[]{:S(2)}) async-start(bf16[4,512,1280]{1,2,0:T(8,128)(2,1)} %copy.87), calls=%async_computation.2 | async-start | bytes 10485760 | tf_op jit(solution)/shard_map/all_to_all | solution.py:138
  365.7 2.2 add_add_fusion
  368.0 0.9 mul.650
  368.9 76.4 %all-to-all-done.2 = bf16[4,512,1280]{1,2,0:T(8,128)(2,1)} async-done(((bf16[4,512,1280]{1,2,0:T(8,128)(2,1)}), bf16[4,512,1280]{1,2,0:T(8,128)(2,1)}, u32[]{:S(2)}, u32[]{:S(2)}) %all-to-all-start.2) | async-done | bytes 5242912 | tf_op jit(solution)/shard_map/all_to_all | solution.py:138
  445.3 8.0 %convert_element_type.110 = f32[4,512,1280]{1,2,0:T(8,128)} convert(bf16[4,512,1280]{1,2,0:T(8,128)(2,1)} %all-to-all-done.2) | non-fusion elementwise | flops 2621440 | bytes 15728640 | tf_op jit(solution)/shard_map/convert_element_type | solution.py:151
  453.3 17.1 %fusion.21 = bf16[512,80,64]{0,1,2:T(8,128)(2,1)S(1)} fusion(f32[512,80,64]{0,2,1:T(8,128)} %bitcast.150, f32[512,80]{0,1:T(8,128)S(1)} %mul.650, f32[80,64,128]{2,1,0:T(8,128)} %all-gather.5.cloned.1.call-done, bf16[2048,128]{1,0:T(8,128)(2,1)S(1)} %copy-done.11, s32[]{:T(128)S(6)} %select_n.18), kind=kOutput, calls=%fused_computation.27 | convolution fusion | flops 4034396160 | bytes 18644996 | tf_op jit(solution)/shard_map/tn,kn->tk/dot_general | solution.py:145
  470.4 5.3 %copy.92 = bf16[512,80,64]{0,2,1:T(8,128)(2,1)} copy(bf16[512,80,64]{0,1,2:T(8,128)(2,1)S(1)} %fusion.21) | data formatting | bytes 10485760 | tf_op jit(solution)/shard_map/convert_element_type | solution.py:154
  475.8 7.9 %copy.93 = bf16[512,5120]{1,0:T(8,128)(2,1)} copy(bf16[512,5120]{0,1:T(8,128)(2,1)} %bitcast.152) | data formatting | bytes 10485760 | tf_op jit(solution)/shard_map/reshape | solution.py:154
  (166 shorter events, 25.7 us)
Async XLA Ops:
  8.1 10.3 %all-to-all-start.1 = ((bf16[512,4,20]{0,2,1:T(8,128)(2,1)}), bf16[512,4,20]{0,2,1:T(8,128)(2,1)S(1)}, u32[]{:S(2)}, u32[]{:S(2)}) async-start(bf16[512,4,20]{0,2,1:T(8,128)(2,1)} %all_to_all.50), calls=%async_computation.1 | async-start | bytes 196608 | tf_op jit(solution)/shard_map/all_to_all | solution.py:61
  18.4 6.0 %copy-start.26 = (f32[5,1280]{1,0:T(8,128)S(1)}, f32[5,1280]{1,0:T(8,128)}, u32[]{:S(2)}) copy-start(f32[5,1280]{1,0:T(8,128)} %param.10) | copy-start | bytes 76804
  18.4 6.1 %copy-start.40 = (f32[2,20]{1,0:T(2,128)S(1)}, f32[2,20]{1,0:T(2,128)}, u32[]{:S(2)}) copy-start(f32[2,20]{1,0:T(2,128)} %param.12) | copy-start | bytes 484
  18.4 6.1 %copy-start.39 = (f32[5,256]{1,0:T(8,128)S(1)}, f32[5,256]{1,0:T(8,128)}, u32[]{:S(2)}) copy-start(f32[5,256]{1,0:T(8,128)} %param.11) | copy-start | bytes 15364
  18.4 73.1 %all-to-all-start = ((bf16[512,4,1280]{2,0,1:T(8,128)(2,1)}), bf16[512,4,1280]{2,0,1:T(8,128)(2,1)}, u32[]{:S(2)}, u32[]{:S(2)}) async-start(bf16[512,4,1280]{2,0,1:T(8,128)(2,1)} %bitcast.151), calls=%async_computation | async-start | bytes 10485760 | tf_op jit(solution)/shard_map/all_to_all | solution.py:60
  23.6 37.9 %all-gather.3.cloned.1.call-start = ((), (), s32[]{:S(2)}) async-start(), calls=%async_computation.4 | async-start | bytes 1310720 | tf_op jit(solution)/shard_map/all_gather | solution.py:68
  30.1 0.7 copy-start.21
  92.3 8.3 %collective-permute-start = (bf16[3,1536]{1,0:T(4,128)(2,1)S(1)}, bf16[3,1536]{1,0:T(4,128)(2,1)S(1)}, u32[]{:S(2)}, u32[]{:S(2)}) collective-permute-start(bf16[3,1536]{1,0:T(4,128)(2,1)S(1)} %pad_maximum_fusion.2), channel_id=1, source_target_pairs={{0,4},{4,8},{8,12},{12,16},{16,20},{20,24},{24,28},{28,32},{32,36}... | collective-permute-start | bytes 27656 | tf_op jit(solution)/shard_map/ppermute | solution.py:14
  152.4 5.8 %copy-start.20 = (bf16[2048,128]{1,0:T(8,128)(2,1)}, bf16[2048,128]{1,0:T(8,128)(2,1)S(1)}, u32[]{:S(2)}) copy-start(bf16[2048,128]{1,0:T(8,128)(2,1)S(1)} %get-tuple-element.40) | copy-start | bytes 1572868
  158.4 4.4 copy-start.8
  158.4 4.4 copy-start.9
  158.4 4.4 copy-start.10
  158.4 3.4 copy-start.33
  158.4 3.5 copy-start.31
  158.4 3.6 copy-start.29
  158.4 3.7 copy-start.27
  158.4 4.1 copy-start.37
  158.4 4.2 copy-start.34
  161.8 1.8 copy-start
  161.8 1.8 copy-start.2
  161.8 1.8 copy-start.4
  162.8 0.8 copy-start.36
  162.8 6.7 %copy-start.22 = (f32[8,20,2,128]{3,1,2,0:T(8,128)S(1)}, f32[8,20,2,128]{3,1,2,0:T(8,128)}, u32[]{:S(2)}) copy-start(f32[8,20,2,128]{3,1,2,0:T(8,128)} %copy-done.21) | copy-start | bytes 491524
  162.8 8.5 %copy-start.32 = (f32[20]{0:T(128)S(1)}, f32[20]{0:T(128)}, u32[]{:S(2)}) copy-start(f32[20]{0:T(128)} %get-tuple-element.68) | copy-start | bytes 244
  163.6 8.9 %copy-start.30 = (f32[20]{0:T(128)S(1)}, f32[20]{0:T(128)}, u32[]{:S(2)}) copy-start(f32[20]{0:T(128)} %get-tuple-element.67) | copy-start | bytes 244
  163.6 9.9 %copy-start.28 = (f32[20]{0:T(128)S(1)}, f32[20]{0:T(128)}, u32[]{:S(2)}) copy-start(f32[20]{0:T(128)} %get-tuple-element.66) | copy-start | bytes 244
  164.5 31.9 %collective-permute-start.1 = (f32[163968]{0:T(1024)}, f32[163968]{0:T(1024)}, u32[]{:S(2)}, u32[]{:S(2)}) collective-permute-start(f32[163968]{0:T(1024)} %select_maximum_fusion.4), channel_id=1, source_target_pairs={{0,4},{4,8},{8,12},{12,16},{16,20},{20,24},{24,28},{28,32},{32,36}... | collective-permute-start | bytes 1967624 | tf_op jit(solution)/shard_map/ppermute | solution.py:14
  171.4 5.5 %copy-start.38 = (f32[20]{0:T(128)S(1)}, f32[20]{0:T(128)}, u32[]{:S(2)}) copy-start(f32[20]{0:T(128)} %get-tuple-element.59) | copy-start | bytes 244
  173.6 9.5 %copy-start.35 = (f32[20]{0:T(128)S(1)}, f32[20]{0:T(128)}, u32[]{:S(2)}) copy-start(f32[20]{0:T(128)} %get-tuple-element.61) | copy-start | bytes 244
  176.9 20.2 %copy-start.1 = (f32[1,20,64,128]{3,2,1,0:T(8,128)S(1)}, f32[1,20,64,128]{3,2,1,0:T(8,128)}, u32[]{:S(2)}) copy-start(f32[1,20,64,128]{3,2,1,0:T(8,128)} %copy-done) | copy-start | bytes 1966084
  176.9 20.2 %copy-start.3 = (f32[1,20,64,128]{3,2,1,0:T(8,128)S(1)}, f32[1,20,64,128]{3,2,1,0:T(8,128)}, u32[]{:S(2)}) copy-start(f32[1,20,64,128]{3,2,1,0:T(8,128)} %copy-done.2) | copy-start | bytes 1966084
  176.9 20.2 %copy-start.5 = (f32[1,20,64,128]{3,2,1,0:T(8,128)S(1)}, f32[1,20,64,128]{3,2,1,0:T(8,128)}, u32[]{:S(2)}) copy-start(f32[1,20,64,128]{3,2,1,0:T(8,128)} %copy-done.4) | copy-start | bytes 1966084
  190.4 169.9 %all-to-all-start.3 = ((f32[4,512,20]{1,2,0:T(8,128)}), f32[4,512,20]{1,2,0:T(8,128)}, u32[]{:S(2)}, u32[]{:S(2)}) async-start(f32[4,512,20]{1,2,0:T(8,128)} %copy.89), calls=%async_computation.3 | async-start | bytes 393216 | tf_op jit(solution)/shard_map/all_to_all | solution.py:139
  197.1 9.8 %copy-start.17 = (f32[1,20,64,128]{3,2,1,0:T(8,128)S(1)}, f32[1,20,64,128]{3,2,1,0:T(8,128)}, u32[]{:S(2)}) copy-start(f32[1,20,64,128]{3,2,1,0:T(8,128)} %get-tuple-element.26) | copy-start | bytes 1966084
  197.1 10.7 %copy-start.16 = (f32[1,20,64,128]{3,2,1,0:T(8,128)S(1)}, f32[1,20,64,128]{3,2,1,0:T(8,128)}, u32[]{:S(2)}) copy-start(f32[1,20,64,128]{3,2,1,0:T(8,128)} %get-tuple-element.25) | copy-start | bytes 1966084
  197.1 11.5 %copy-start.15 = (f32[1,20,64,128]{3,2,1,0:T(8,128)S(1)}, f32[1,20,64,128]{3,2,1,0:T(8,128)}, u32[]{:S(2)}) copy-start(f32[1,20,64,128]{3,2,1,0:T(8,128)} %get-tuple-element.24) | copy-start | bytes 1966084
  202.1 0.8 copy-start.6
  203.9 32.0 %copy-start.7 = (f32[163840]{0:T(1024)S(1)}, f32[163840]{0:T(1024)}, u32[]{:S(2)}) copy-start(f32[163840]{0:T(1024)} %copy-done.6) | copy-start | bytes 1966084
  203.9 31.3 %collective-permute-start.2 = (f32[163968]{0:T(1024)}, f32[163968]{0:T(1024)}, u32[]{:S(2)}, u32[]{:S(2)}) collective-permute-start(f32[163968]{0:T(1024)} %select_maximum_fusion.3), channel_id=1, source_target_pairs={{0,8},{4,12},{8,16},{12,20},{16,24},{20,28},{24,32},{28,36},{32,40... | collective-permute-start | bytes 1967624 | tf_op jit(solution)/shard_map/ppermute | solution.py:14
  207.7 37.2 %copy-start.14 = (f32[1,20,64,128]{3,2,1,0:T(8,128)S(1)}, f32[1,20,64,128]{3,2,1,0:T(8,128)}, u32[]{:S(2)}) copy-start(f32[1,20,64,128]{3,2,1,0:T(8,128)} %get-tuple-element.22) | copy-start | bytes 1966084
  208.6 37.2 %copy-start.11 = (bf16[2048,128]{1,0:T(8,128)(2,1)S(1)}, bf16[2048,128]{1,0:T(8,128)(2,1)}, u32[]{:S(2)}) copy-start(bf16[2048,128]{1,0:T(8,128)(2,1)} %get-tuple-element.41) | copy-start | bytes 1572868
  239.0 27.6 %collective-permute-start.3 = (f32[163968]{0:T(1024)}, f32[163968]{0:T(1024)}, u32[]{:S(2)}, u32[]{:S(2)}) collective-permute-start(f32[163968]{0:T(1024)} %select_maximum_fusion.2), channel_id=1, source_target_pairs={{0,16},{4,20},{8,24},{12,28},{16,32},{20,36},{24,40},{28,44},{32,4... | collective-permute-start | bytes 1967624 | tf_op jit(solution)/shard_map/ppermute | solution.py:14
  245.8 27.8 %copy-start.13 = (f32[1,20,64,128]{3,2,1,0:T(8,128)S(1)}, f32[1,20,64,128]{3,2,1,0:T(8,128)}, u32[]{:S(2)}) copy-start(f32[1,20,64,128]{3,2,1,0:T(8,128)} %get-tuple-element.21) | copy-start | bytes 1966084
  270.4 17.6 %collective-permute-start.4 = (f32[163968]{0:T(1024)}, f32[163968]{0:T(1024)}, u32[]{:S(2)}, u32[]{:S(2)}) collective-permute-start(f32[163968]{0:T(1024)} %select_maximum_fusion.1), channel_id=1, source_target_pairs={{0,32},{4,36},{8,40},{12,44},{16,48},{20,52},{24,56},{28,60},{32,6... | collective-permute-start | bytes 1967624 | tf_op jit(solution)/shard_map/ppermute | solution.py:14
  285.1 34.5 %copy-start.23 = (f32[8,256,20]{1,2,0:T(8,128)S(1)}, f32[8,256,20]{1,2,0:T(8,128)}, u32[]{:S(2)}) copy-start(f32[8,256,20]{1,2,0:T(8,128)} %copy.80) | copy-start | bytes 491524
  285.1 34.5 %copy-start.24 = (f32[8,20,256]{2,1,0:T(8,128)S(1)}, f32[8,20,256]{2,1,0:T(8,128)}, u32[]{:S(2)}) copy-start(f32[8,20,256]{2,1,0:T(8,128)} %copy.78) | copy-start | bytes 491524
  285.1 34.5 %copy-start.25 = (pred[256,256]{1,0:T(8,128)(4,1)S(1)}, pred[256,256]{1,0:T(8,128)(4,1)}, u32[]{:S(2)}) copy-start(pred[256,256]{1,0:T(8,128)(4,1)} %iota_compare_fusion.1) | copy-start | bytes 196612
  285.1 34.5 %copy-start.41 = (f32[20]{0:T(128)S(1)}, f32[20]{0:T(128)}, u32[]{:S(2)}) copy-start(f32[20]{0:T(128)} %param.13) | copy-start | bytes 244
  290.9 69.3 %collective-permute-start.5 = (f32[163968]{0:T(1024)S(1)}, f32[163968]{0:T(1024)S(1)}, u32[]{:S(2)}, u32[]{:S(2)}) collective-permute-start(f32[163968]{0:T(1024)S(1)} %select_maximum_fusion), channel_id=1, source_target_pairs={{0,64},{4,68},{8,72},{12,76},{16,80},{20,84},{24,88},{28,92},{32,9... | collective-permute-start | bytes 1967624 | tf_op jit(solution)/shard_map/ppermute | solution.py:14
  360.2 5.5 %copy-start.12 = (f32[163840]{0:T(1024)S(1)}, f32[163840]{0:T(1024)}, u32[]{:S(2)}) copy-start(f32[163840]{0:T(1024)} %get-tuple-element.51) | copy-start | bytes 1966084
  360.2 5.5 %copy-start.18 = (f32[163840]{0:T(1024)S(1)}, f32[163840]{0:T(1024)}, u32[]{:S(2)}) copy-start(f32[163840]{0:T(1024)} %get-tuple-element.49) | copy-start | bytes 1966084
  360.2 5.5 %copy-start.19 = (f32[163840]{0:T(1024)S(1)}, f32[163840]{0:T(1024)}, u32[]{:S(2)}) copy-start(f32[163840]{0:T(1024)} %get-tuple-element.47) | copy-start | bytes 1966084
  360.3 85.0 %all-to-all-start.2 = ((bf16[4,512,1280]{1,2,0:T(8,128)(2,1)}), bf16[4,512,1280]{1,2,0:T(8,128)(2,1)}, u32[]{:S(2)}, u32[]{:S(2)}) async-start(bf16[4,512,1280]{1,2,0:T(8,128)(2,1)} %copy.87), calls=%async_computation.2 | async-start | bytes 10485760 | tf_op jit(solution)/shard_map/all_to_all | solution.py:138
  365.5 87.8 %all-gather.5.cloned.1.call-start = ((), (), s32[]{:S(2)}) async-start(), calls=%async_computation.5 | async-start | bytes 3276800 | tf_op jit(solution)/shard_map/all_gather | solution.py:144
Sparse Core Ops, SparseCore 0:
  26.2 35.2 all-gather.2
  368.1 56.5 all-gather.4

commit v6 on v4

--- a/solution.py
+++ b/solution.py
@@ -65,7 +65,9 @@
     heads_local = head_rates.shape[1]
     head_width = channels // heads_local
     margin_rows = KERNEL - 1
-    state_whole = lax.all_gather(state_inputs, "head", axis=0, tiled=True)
+    state_whole = lax.all_to_all(
+        jnp.tile(state_inputs, (lax.axis_size("head"), 1)), "head", split_axis=0, concat_axis=0, tiled=True
+    )
     edge_rows = jnp.concatenate(
         [x_local[context - margin_rows :], state_whole[context - margin_rows :]], axis=1
     )
@@ -136,7 +138,10 @@
     tokens = inner_tokens.shape[0]
     group = lax.axis_index("head")
     c_tokens = lax.dynamic_slice_in_dim(c_rows, group * tokens, tokens, axis=0).astype(jnp.float32)
-    incoming_all = lax.all_gather(incoming, "head", axis=0, tiled=True)
+    groups = lax.axis_size("head")
+    incoming_all = lax.all_to_all(
+        jnp.tile(incoming, (groups, 1, 1)), "head", split_axis=0, concat_axis=0, tiled=True
+    )
     carried_in = jnp.einsum(
         "tn,kn->tk",
         c_tokens,

time: 510 us -> 445 us (0.87)
  the two profiles are of different devices: /device:TPU:98 before, /device:TPU:6 now
where the time goes in v6:
time: 445 us; the launch traced here: 438 us
  waiting for transfers between devices  178 us (40%)
  local copies, waits for them, and re-layouts  95.3 us (21%)
  matrix products  60.2 us (14%)
  other arithmetic  53.8 us (12%)
  starting transfers between devices  38.9 us (9%)
  blocking collectives  10.1 us (2%)
    ppermute x6, waiting for transfers between devices, from_behind(): return lax.ppermute(value, axis, pairs)  72 us
    all_to_all x1, waiting for transfers between devices, per_device(): lax.all_to_all(partial, 'head', split_axis=0, concat_axis=1, tiled=True)  37.9 us
    all_to_all x1, waiting for transfers between devices, per_device(): lax.all_to_all(inner_tokens, 'head', split_axis=1, concat_axis=0, tiled=T...  36.2 us
    all_to_all x1, waiting for transfers between devices, per_device(): lax.all_to_all(jnp.tile(incoming, (groups, 1, 1)), 'head', split_axis=0,...  23.5 us
    dot_general x1, matrix products, per_device(): jnp.einsum('bhts,bshp->bthp', mixing, u_blocks, preferred_element_type=jn...  20.8 us
    unnamed x96, local copies, waits for them, and re-layouts  19.4 us
    ppermute x6, starting transfers between devices, from_behind(): return lax.ppermute(value, axis, pairs)  17.8 us
    all_to_all x2, local copies, waits for them, and re-layouts, per_device(): lax.all_to_all(partial, 'head', split_axis=0, concat_axis=1, tiled=True)  15.1 us
  transfers between devices with their start and end apart: 11, of which 9 were waited for; matrix products, arithmetic and copies ran while one was open for 38% of the time, Pallas kernels for 0%

profile of v6, /device:TPU:6, one launch (start us, length us, event | category | flops | bytes accessed | tf_op | source)
XLA Modules:
  0.0 437.8 jit_solution(6037491749890303663)
XLA Ops:
  0.0 0.9 all_to_all.61
  0.9 10.1 %all_to_all.75 = bf16[512,4,20]{0,2,1:T(8,128)(2,1)S(1)} all-to-all(bf16[512,4,20]{0,2,1:T(8,128)(2,1)S(1)} %all_to_all.61), channel_id=1, replica_groups=mesh['run'=2,'ctx'=32,'head'=4] {'head'}, dimensions={1} | all-to-all | bytes 163840 | tf_op jit(solution)/shard_map/all_to_all | solution.py:61
  11.0 2.0 tile.6
  13.0 3.5 all-to-all-start.1
  16.5 5.2 %copy.106 = bf16[64,4,8,1280]{3,2,0,1:T(8,128)(2,1)} copy(bf16[64,4,8,1280]{3,2,1,0:T(8,128)(2,1)} %bitcast.176) | data formatting | bytes 10485760 | tf_op jit(solution)/shard_map/all_to_all | solution.py:60
  21.7 8.7 %all-to-all-done.1 = bf16[4,512,256]{2,1,0:T(8,128)(2,1)S(1)} async-done(((bf16[4,512,256]{2,1,0:T(8,128)(2,1)}), bf16[4,512,256]{2,1,0:T(8,128)(2,1)S(1)}, u32[]{:S(2)}, u32[]{:S(2)}) %all-to-all-start.1) | async-done | bytes 1048608 | tf_op jit(solution)/shard_map/all_to_all | solution.py:68
  30.4 5.2 %all-to-all-start = ((bf16[512,4,1280]{2,0,1:T(8,128)(2,1)}), bf16[512,4,1280]{2,0,1:T(8,128)(2,1)}, u32[]{:S(2)}, u32[]{:S(2)}) async-start(bf16[512,4,1280]{2,0,1:T(8,128)(2,1)} %bitcast.153), calls=%async_computation | async-start | bytes 10485760 | tf_op jit(solution)/shard_map/all_to_all | solution.py:60
  37.0 0.9 broadcast_dynamic-update-slice_fusion
  39.0 4.6 %reduce-window.6 = f32[8,20,2,128]{3,1,2,0:T(8,128)S(1)} reduce-window(f32[8,20,2,128]{3,1,2,0:T(8,128)S(1)} %copy.62, f32[]{:T(128)} %constant.8.clone.1), window={size=1x1x1x128 pad=0_0x0_0x0_0x127_0}, to_apply=%region_0.1 | reduce-window | flops 5201920 | bytes 327684 | tf_op jit(solution)/shard_map/reduce-window
  45.0 1.0 mul.702
  46.1 1.0 mul.704
  47.2 1.0 mul.706
  48.3 1.0 mul.708
  49.4 1.0 mul.710
  50.6 1.0 mul.712
  51.7 1.0 mul.700
  52.8 1.0 mul.697
  53.9 1.0 mul.714
  57.5 36.2 %all-to-all-done = bf16[512,4,1280]{2,0,1:T(8,128)(2,1)} async-done(((bf16[512,4,1280]{2,0,1:T(8,128)(2,1)}), bf16[512,4,1280]{2,0,1:T(8,128)(2,1)}, u32[]{:S(2)}, u32[]{:S(2)}) %all-to-all-start) | async-done | bytes 5242912 | tf_op jit(solution)/shard_map/all_to_all | solution.py:60
  93.7 3.4 all-to-all-start.4
  97.8 4.0 collective-permute-start
  101.8 3.3 bitcast_convert_fusion
  105.1 2.4 collective-permute-done
  107.5 8.1 %fusion.23 = f32[2048,1280]{1,0:T(8,128)} fusion(f32[2048,1280]{1,0:T(8,128)S(1)} %bitcast_convert_fusion, f32[1280]{0:T(1024)S(1)} %get-tuple-element.8, f32[3,1280]{1,0:T(4,128)S(1)} %slice_convert_fusion, f32[1280]{0:T(1024)S(1)} %get-tuple-element.9, f32[1280]{0:T(1024)S(1)} %get-tuple-element.6, f32[1280]{0:T(1024)S(1)} %get-tuple-element.7, ...), kind=kLoop, calls=%fused_computation.32 | loop fusion | flops 44564480 | bytes 21012480 | tf_op jit(solution)/shard_map/convert_element_type | solution.py:84
  115.6 11.3 %copy.60 = f32[2048,1280]{0,1:T(8,128)} copy(f32[2048,1280]{1,0:T(8,128)} %fusion.23) | data formatting | bytes 20971520 | tf_op jit(solution)/shard_map/convert_element_type | solution.py:84
  127.0 13.0 %copy.87 = f32[160,8,8,256]{3,2,1,0:T(8,128)} copy(f32[160,8,8,256]{3,1,2,0:T(8,128)} %bitcast.151) | data formatting | bytes 20971520
  140.1 1.5 multiply_convert_fusion.6
  141.6 11.7 %convert_multiply_fusion = (f32[8,256,20,64]{1,0,3,2:T(8,128)}, bf16[8,256,20,64]{1,0,3,2:T(8,128)(2,1)}) fusion(f32[8,256,20]{1,0,2:T(8,128)S(1)} %get-tuple-element.53, f32[8,256,20,64]{1,0,3,2:T(8,128)} %bitcast.149, f32[8,256,20]{1,0,2:T(8,128)S(1)} %copy-done.14), kind=kLoop, calls=%fused_computation.27 | loop fusion | flops 10485760 | bytes 26542080 | tf_op jit(solution)/shard_map/mul | solution.py:94
  153.3 12.7 %fusion.18 = f32[8,20,64,128]{3,2,1,0:T(8,128)S(1)} fusion(bf16[8,256,128,1]{2,1,3,0:T(8,128)(2,1)S(1)} %bitcast.174, f32[8,256,20,64]{1,0,3,2:T(8,128)} %get-tuple-element.28), kind=kOutput, calls=%fused_computation.25 | convolution fusion | flops 4026531840 | bytes 16252928 | tf_op jit(solution)/shard_map/bshp,bsn->bhpn/dot_general | solution.py:95
  166.1 1.5 multiply_add_fusion.4
  169.6 2.3 collective-permute-start.1
  175.5 11.1 %collective-permute-done.1 = f32[163968]{0:T(1024)S(1)} collective-permute-done((f32[163968]{0:T(1024)S(1)}, f32[163968]{0:T(1024)S(1)}, u32[]{:S(2)}, u32[]{:S(2)}) %collective-permute-start.1) | collective-permute-done | bytes 655904 | tf_op jit(solution)/shard_map/ppermute | solution.py:14
  186.7 1.5 add_add_fusion.1
  188.2 0.9 select_maximum_fusion.3
  189.1 1.9 collective-permute-start.2
  192.8 1.8 fusion.47
  194.7 1.0 mul.725
  195.7 23.8 %collective-permute-done.2 = f32[163968]{0:T(1024)} collective-permute-done((f32[163968]{0:T(1024)}, f32[163968]{0:T(1024)}, u32[]{:S(2)}, u32[]{:S(2)}) %collective-permute-start.2) | collective-permute-done | bytes 655904 | tf_op jit(solution)/shard_map/ppermute | solution.py:14
  220.2 2.2 multiply_add_fusion.2
  222.4 0.9 select_maximum_fusion.2
  223.3 7.0 %collective-permute-start.3 = (f32[163968]{0:T(1024)}, f32[163968]{0:T(1024)}, u32[]{:S(2)}, u32[]{:S(2)}) collective-permute-start(f32[163968]{0:T(1024)} %select_maximum_fusion.2), channel_id=1, source_target_pairs={{0,16},{4,20},{8,24},{12,28},{16,32},{20,36},{24,40},{28,44},{32,4... | collective-permute-start | bytes 1967624 | tf_op jit(solution)/shard_map/ppermute | solution.py:14
  230.4 0.9 constant_dynamic-update-slice_fusion
  231.3 10.6 %fusion.48 = f32[8,256,1280]{1,2,0:T(8,128)} fusion(bf16[8,256,128]{2,1,0:T(8,128)(2,1)S(1)} %bitcast.173, f32[8,1280,128]{2,1,0:T(8,128)} %constant_dynamic-update-slice_fusion), kind=kOutput, calls=%fused_computation.133 | convolution fusion | flops 4026531840 | bytes 16252928 | tf_op jit(solution)/shard_map/btn,bkn->btk/dot_general | solution.py:123
  242.0 1.0 mul.730
  243.0 15.9 %collective-permute-done.3 = f32[163968]{0:T(1024)} collective-permute-done((f32[163968]{0:T(1024)}, f32[163968]{0:T(1024)}, u32[]{:S(2)}, u32[]{:S(2)}) %collective-permute-start.3) | collective-permute-done | bytes 655904 | tf_op jit(solution)/shard_map/ppermute | solution.py:14
  259.6 2.2 multiply_add_fusion.1
  262.7 1.3 collective-permute-start.4
  264.0 20.8 %fusion.16 = bf16[8,256,20,64]{1,3,2,0:T(8,128)(2,1)S(1)} fusion(f32[8,256,20,64]{1,0,3,2:T(8,128)} %bitcast.150, f32[8,256,20,64]{1,3,2,0:T(8,128)} %bitcast.155, f32[8,20,256]{2,1,0:T(8,128)S(1)} %copy-done.17, f32[8,256,256]{2,1,0:T(8,128)} %fusion.47, pred[256,256]{1,0:T(8,128)(4,1)S(1)} %copy-done.18, bf16[8,256,20,64]{1,0,3,2:T(8,128)(2,1)} %get-tuple-element.29, ...), kind=kOutput, calls=%fused_computation.21 | convolution fusion | flops 1397227520 | bytes 33947728 | tf_op jit(solution)/shard_map/bhts,bshp->bthp/dot_general | solution.py:118
  284.9 6.0 %copy.75 = bf16[8,256,20,64]{1,0,3,2:T(8,128)(2,1)} copy(bf16[8,256,20,64]{1,3,2,0:T(8,128)(2,1)S(1)} %fusion.16) | data formatting | bytes 10485760 | tf_op jit(solution)/shard_map/convert_element_type | solution.py:133
  290.9 9.2 %all_to_all.63 = bf16[4,512,1280]{1,0,2:T(4,128)(2,1)} reshape(bf16[8,256,20,64]{1,0,3,2:T(8,128)(2,1)} %copy.75) | data formatting | bytes 10485760 | tf_op jit(solution)/shard_map/all_to_all | solution.py:135
  300.1 5.9 %copy.76 = bf16[4,512,1280]{1,2,0:T(8,128)(2,1)} copy(bf16[4,512,1280]{1,0,2:T(4,128)(2,1)} %all_to_all.63) | data formatting | bytes 10485760 | tf_op jit(solution)/shard_map/all_to_all | solution.py:135
  306.1 1.1 mul.736
  307.2 5.2 %all-to-all-start.3 = ((bf16[4,512,1280]{1,2,0:T(8,128)(2,1)}), bf16[4,512,1280]{1,2,0:T(8,128)(2,1)}, u32[]{:S(2)}, u32[]{:S(2)}) async-start(bf16[4,512,1280]{1,2,0:T(8,128)(2,1)} %copy.76), calls=%async_computation.3 | async-start | bytes 10485760 | tf_op jit(solution)/shard_map/all_to_all | solution.py:135
  312.4 1.3 multiply_add_fusion
  314.5 1.3 collective-permute-start.5
  315.8 18.8 %collective-permute-done.5 = f32[163968]{0:T(1024)S(1)} collective-permute-done((f32[163968]{0:T(1024)S(1)}, f32[163968]{0:T(1024)S(1)}, u32[]{:S(2)}, u32[]{:S(2)}) %collective-permute-start.5) | collective-permute-done | bytes 655904 | tf_op jit(solution)/shard_map/ppermute | solution.py:14
  335.1 37.9 %all-to-all-done.3 = bf16[4,512,1280]{1,2,0:T(8,128)(2,1)} async-done(((bf16[4,512,1280]{1,2,0:T(8,128)(2,1)}), bf16[4,512,1280]{1,2,0:T(8,128)(2,1)}, u32[]{:S(2)}, u32[]{:S(2)}) %all-to-all-start.3) | async-done | bytes 5242912 | tf_op jit(solution)/shard_map/all_to_all | solution.py:135
  372.9 1.8 tile.7
  374.8 3.8 all-to-all-start.5
  378.6 7.9 %convert_element_type.99 = f32[4,512,1280]{1,2,0:T(8,128)} convert(bf16[4,512,1280]{1,2,0:T(8,128)(2,1)} %all-to-all-done.3) | non-fusion elementwise | flops 2621440 | bytes 15728640 | tf_op jit(solution)/shard_map/convert_element_type | solution.py:151
  386.6 23.5 %all-to-all-done.5 = f32[80,64,128]{2,1,0:T(8,128)S(1)} async-done(((f32[80,64,128]{2,1,0:T(8,128)}), f32[80,64,128]{2,1,0:T(8,128)S(1)}, u32[]{:S(2)}, u32[]{:S(2)}) %all-to-all-start.5) | async-done | bytes 2621472 | tf_op jit(solution)/shard_map/all_to_all | solution.py:142
  410.1 14.3 %fusion.17 = bf16[512,80,64]{0,1,2:T(8,128)(2,1)S(1)} fusion(f32[512,80,64]{0,2,1:T(8,128)} %bitcast.152, f32[512,80]{0,1:T(8,128)S(1)} %mul.662, f32[80,64,128]{2,1,0:T(8,128)S(1)} %all-to-all-done.5, bf16[2048,128]{1,0:T(8,128)(2,1)S(1)} %get-tuple-element.41, s32[]{:T(128)S(6)} %select_n.18), kind=kOutput, calls=%fused_computation.23 | convolution fusion | flops 4034396160 | bytes 18644996 | tf_op jit(solution)/shard_map/tn,kn->tk/dot_general | solution.py:145
  424.4 5.3 %copy.81 = bf16[512,80,64]{0,2,1:T(8,128)(2,1)} copy(bf16[512,80,64]{0,1,2:T(8,128)(2,1)S(1)} %fusion.17) | data formatting | bytes 10485760 | tf_op jit(solution)/shard_map/convert_element_type | solution.py:154
  429.7 7.9 %copy.82 = bf16[512,5120]{1,0:T(8,128)(2,1)} copy(bf16[512,5120]{0,1:T(8,128)(2,1)} %bitcast.154) | data formatting | bytes 10485760 | tf_op jit(solution)/shard_map/reshape | solution.py:154
  (166 shorter events, 19.2 us)
Async XLA Ops:
  13.0 17.4 %all-to-all-start.1 = ((bf16[4,512,256]{2,1,0:T(8,128)(2,1)}), bf16[4,512,256]{2,1,0:T(8,128)(2,1)S(1)}, u32[]{:S(2)}, u32[]{:S(2)}) async-start(bf16[4,512,256]{2,1,0:T(8,128)(2,1)} %tile.6), calls=%async_computation.1 | async-start | bytes 2097152 | tf_op jit(solution)/shard_map/all_to_all | solution.py:68
  30.4 5.9 %copy-start.19 = (f32[5,1280]{1,0:T(8,128)S(1)}, f32[5,1280]{1,0:T(8,128)}, u32[]{:S(2)}) copy-start(f32[5,1280]{1,0:T(8,128)} %param.10) | copy-start | bytes 76804
  30.4 5.9 %copy-start.42 = (f32[2,20]{1,0:T(2,128)S(1)}, f32[2,20]{1,0:T(2,128)}, u32[]{:S(2)}) copy-start(f32[2,20]{1,0:T(2,128)} %param.12) | copy-start | bytes 484
  30.4 5.9 %copy-start.41 = (f32[5,256]{1,0:T(8,128)S(1)}, f32[5,256]{1,0:T(8,128)}, u32[]{:S(2)}) copy-start(f32[5,256]{1,0:T(8,128)} %param.11) | copy-start | bytes 15364
  30.4 63.3 %all-to-all-start = ((bf16[512,4,1280]{2,0,1:T(8,128)(2,1)}), bf16[512,4,1280]{2,0,1:T(8,128)(2,1)}, u32[]{:S(2)}, u32[]{:S(2)}) async-start(bf16[512,4,1280]{2,0,1:T(8,128)(2,1)} %bitcast.153), calls=%async_computation | async-start | bytes 10485760 | tf_op jit(solution)/shard_map/all_to_all | solution.py:60
  44.7 5.7 %copy-start.20 = (f32[20]{0:T(128)}, f32[20]{0:T(128)S(1)}, u32[]{:S(2)}) copy-start(f32[20]{0:T(128)S(1)} %get-tuple-element.65) | copy-start | bytes 244
  44.7 5.7 %copy-start.22 = (f32[20]{0:T(128)}, f32[20]{0:T(128)S(1)}, u32[]{:S(2)}) copy-start(f32[20]{0:T(128)S(1)} %get-tuple-element.66) | copy-start | bytes 244
  44.7 5.7 %copy-start.24 = (f32[20]{0:T(128)}, f32[20]{0:T(128)S(1)}, u32[]{:S(2)}) copy-start(f32[20]{0:T(128)S(1)} %get-tuple-element.67) | copy-start | bytes 244
  44.8 5.7 %copy-start.26 = (f32[20]{0:T(128)}, f32[20]{0:T(128)S(1)}, u32[]{:S(2)}) copy-start(f32[20]{0:T(128)S(1)} %get-tuple-element.68) | copy-start | bytes 244
  44.8 5.7 %copy-start.28 = (f32[20]{0:T(128)}, f32[20]{0:T(128)S(1)}, u32[]{:S(2)}) copy-start(f32[20]{0:T(128)S(1)} %get-tuple-element.62) | copy-start | bytes 244
  44.8 6.8 %copy-start.34 = (f32[20]{0:T(128)}, f32[20]{0:T(128)S(1)}, u32[]{:S(2)}) copy-start(f32[20]{0:T(128)S(1)} %get-tuple-element.59) | copy-start | bytes 244
  52.7 3.7 copy-start.32
  52.7 4.6 %copy-start.30 = (f32[20]{0:T(128)}, f32[20]{0:T(128)S(1)}, u32[]{:S(2)}) copy-start(f32[20]{0:T(128)S(1)} %get-tuple-element.61) | copy-start | bytes 244
  93.7 213.5 %all-to-all-start.4 = ((f32[4,512,20]{1,2,0:T(8,128)}), f32[4,512,20]{1,2,0:T(8,128)S(1)}, u32[]{:S(2)}, u32[]{:S(2)}) async-start(f32[4,512,20]{1,2,0:T(8,128)} %copy.78), calls=%async_computation.4 | async-start | bytes 393216 | tf_op jit(solution)/shard_map/all_to_all | solution.py:136
  97.8 9.7 %collective-permute-start = (bf16[3,1536]{1,0:T(4,128)(2,1)S(1)}, bf16[3,1536]{1,0:T(4,128)(2,1)S(1)}, u32[]{:S(2)}, u32[]{:S(2)}) collective-permute-start(bf16[3,1536]{1,0:T(4,128)(2,1)S(1)} %pad_maximum_fusion.2), channel_id=1, source_target_pairs={{0,4},{4,8},{8,12},{12,16},{16,20},{20,24},{24,28},{28,32},{32,36}... | collective-permute-start | bytes 27656 | tf_op jit(solution)/shard_map/ppermute | solution.py:14
  127.0 13.1 %copy-start.36 = (f32[1,256]{1,0:T(1,128)S(1)}, f32[1,256]{1,0:T(1,128)}, u32[]{:S(2)}) copy-start(f32[1,256]{1,0:T(1,128)} %get-tuple-element.54) | copy-start | bytes 3076
  127.0 13.1 %copy-start.37 = (f32[1,256]{1,0:T(1,128)S(1)}, f32[1,256]{1,0:T(1,128)}, u32[]{:S(2)}) copy-start(f32[1,256]{1,0:T(1,128)} %get-tuple-element.55) | copy-start | bytes 3076
  127.0 13.1 %copy-start.38 = (f32[1,256]{1,0:T(1,128)S(1)}, f32[1,256]{1,0:T(1,128)}, u32[]{:S(2)}) copy-start(f32[1,256]{1,0:T(1,128)} %get-tuple-element.56) | copy-start | bytes 3076
  127.0 13.1 %copy-start.39 = (f32[1,256]{1,0:T(1,128)S(1)}, f32[1,256]{1,0:T(1,128)}, u32[]{:S(2)}) copy-start(f32[1,256]{1,0:T(1,128)} %get-tuple-element.57) | copy-start | bytes 3076
  127.0 13.1 %copy-start.40 = (f32[1,256]{1,0:T(1,128)S(1)}, f32[1,256]{1,0:T(1,128)}, u32[]{:S(2)}) copy-start(f32[1,256]{1,0:T(1,128)} %get-tuple-element.58) | copy-start | bytes 3076
  140.0 1.6 copy-start.14
  153.3 12.7 %copy-start.21 = (f32[20]{0:T(128)S(1)}, f32[20]{0:T(128)}, u32[]{:S(2)}) copy-start(f32[20]{0:T(128)} %copy-done.20) | copy-start | bytes 244
  153.3 12.7 %copy-start.23 = (f32[20]{0:T(128)S(1)}, f32[20]{0:T(128)}, u32[]{:S(2)}) copy-start(f32[20]{0:T(128)} %copy-done.22) | copy-start | bytes 244
  153.3 12.7 %copy-start.25 = (f32[20]{0:T(128)S(1)}, f32[20]{0:T(128)}, u32[]{:S(2)}) copy-start(f32[20]{0:T(128)} %copy-done.24) | copy-start | bytes 244
  153.3 12.7 %copy-start.27 = (f32[20]{0:T(128)S(1)}, f32[20]{0:T(128)}, u32[]{:S(2)}) copy-start(f32[20]{0:T(128)} %copy-done.26) | copy-start | bytes 244
  153.3 12.7 %copy-start.29 = (f32[20]{0:T(128)S(1)}, f32[20]{0:T(128)}, u32[]{:S(2)}) copy-start(f32[20]{0:T(128)} %copy-done.28) | copy-start | bytes 244
  153.3 12.7 %copy-start.31 = (f32[20]{0:T(128)S(1)}, f32[20]{0:T(128)}, u32[]{:S(2)}) copy-start(f32[20]{0:T(128)} %copy-done.30) | copy-start | bytes 244
  167.5 0.9 copy-start.35
  168.7 0.8 copy-start.33
  169.5 17.1 %copy-start.1 = (f32[163840]{0:T(1024)S(1)}, f32[163840]{0:T(1024)}, u32[]{:S(2)}) copy-start(f32[163840]{0:T(1024)} %mul.702) | copy-start | bytes 1966084
  169.5 17.1 %copy-start.2 = (f32[163840]{0:T(1024)S(1)}, f32[163840]{0:T(1024)}, u32[]{:S(2)}) copy-start(f32[163840]{0:T(1024)} %mul.704) | copy-start | bytes 1966084
  169.5 17.1 %copy-start.3 = (f32[163840]{0:T(1024)S(1)}, f32[163840]{0:T(1024)}, u32[]{:S(2)}) copy-start(f32[163840]{0:T(1024)} %mul.706) | copy-start | bytes 1966084
  169.5 17.1 %copy-start.4 = (f32[163840]{0:T(1024)S(1)}, f32[163840]{0:T(1024)}, u32[]{:S(2)}) copy-start(f32[163840]{0:T(1024)} %mul.708) | copy-start | bytes 1966084
  169.5 17.1 %copy-start.5 = (f32[163840]{0:T(1024)S(1)}, f32[163840]{0:T(1024)}, u32[]{:S(2)}) copy-start(f32[163840]{0:T(1024)} %mul.710) | copy-start | bytes 1966084
  169.5 17.1 %copy-start.6 = (f32[163840]{0:T(1024)S(1)}, f32[163840]{0:T(1024)}, u32[]{:S(2)}) copy-start(f32[163840]{0:T(1024)} %mul.712) | copy-start | bytes 1966084
  169.5 17.1 %copy-start.7 = (f32[163840]{0:T(1024)S(1)}, f32[163840]{0:T(1024)}, u32[]{:S(2)}) copy-start(f32[163840]{0:T(1024)} %mul.700) | copy-start | bytes 1966084
  169.5 17.1 %copy-start.8 = (f32[163840]{0:T(1024)S(1)}, f32[163840]{0:T(1024)}, u32[]{:S(2)}) copy-start(f32[163840]{0:T(1024)} %mul.697) | copy-start | bytes 1966084
  169.5 17.1 %copy-start.9 = (f32[163840]{0:T(1024)S(1)}, f32[163840]{0:T(1024)}, u32[]{:S(2)}) copy-start(f32[163840]{0:T(1024)} %mul.714) | copy-start | bytes 1966084
  169.6 17.0 %collective-permute-start.1 = (f32[163968]{0:T(1024)S(1)}, f32[163968]{0:T(1024)S(1)}, u32[]{:S(2)}, u32[]{:S(2)}) collective-permute-start(f32[163968]{0:T(1024)S(1)} %select_maximum_fusion.4), channel_id=1, source_target_pairs={{0,4},{4,8},{8,12},{12,16},{16,20},{20,24},{24,28},{28,32},{32,36}... | collective-permute-start | bytes 1967624 | tf_op jit(solution)/shard_map/ppermute | solution.py:14
  186.6 1.6 copy-start.15
  189.1 30.4 %collective-permute-start.2 = (f32[163968]{0:T(1024)}, f32[163968]{0:T(1024)}, u32[]{:S(2)}, u32[]{:S(2)}) collective-permute-start(f32[163968]{0:T(1024)} %select_maximum_fusion.3), channel_id=1, source_target_pairs={{0,8},{4,12},{8,16},{12,20},{16,24},{20,28},{24,32},{28,36},{32,40... | collective-permute-start | bytes 1967624 | tf_op jit(solution)/shard_map/ppermute | solution.py:14
  192.8 37.6 %copy-start.10 = (f32[1,20,64,128]{3,2,1,0:T(8,128)S(1)}, f32[1,20,64,128]{3,2,1,0:T(8,128)}, u32[]{:S(2)}) copy-start(f32[1,20,64,128]{3,2,1,0:T(8,128)} %get-tuple-element.21) | copy-start | bytes 1966084
  223.3 35.6 %collective-permute-start.3 = (f32[163968]{0:T(1024)}, f32[163968]{0:T(1024)}, u32[]{:S(2)}, u32[]{:S(2)}) collective-permute-start(f32[163968]{0:T(1024)} %select_maximum_fusion.2), channel_id=1, source_target_pairs={{0,16},{4,20},{8,24},{12,28},{16,32},{20,36},{24,40},{28,44},{32,4... | collective-permute-start | bytes 1967624 | tf_op jit(solution)/shard_map/ppermute | solution.py:14
  241.9 22.1 %copy-start.16 = (f32[8,256,20]{1,2,0:T(8,128)S(1)}, f32[8,256,20]{1,2,0:T(8,128)}, u32[]{:S(2)}) copy-start(f32[8,256,20]{1,2,0:T(8,128)} %copy.69) | copy-start | bytes 491524
  241.9 22.1 %copy-start.17 = (f32[8,20,256]{2,1,0:T(8,128)S(1)}, f32[8,20,256]{2,1,0:T(8,128)}, u32[]{:S(2)}) copy-start(f32[8,20,256]{2,1,0:T(8,128)} %copy.66) | copy-start | bytes 491524
  241.9 22.1 %copy-start.18 = (pred[256,256]{1,0:T(8,128)(4,1)S(1)}, pred[256,256]{1,0:T(8,128)(4,1)}, u32[]{:S(2)}) copy-start(pred[256,256]{1,0:T(8,128)(4,1)} %iota_compare_fusion.1) | copy-start | bytes 196612
  241.9 22.1 %copy-start.43 = (f32[20]{0:T(128)S(1)}, f32[20]{0:T(128)}, u32[]{:S(2)}) copy-start(f32[20]{0:T(128)} %param.13) | copy-start | bytes 244
  262.7 49.7 %collective-permute-start.4 = (f32[163968]{0:T(1024)}, f32[163968]{0:T(1024)}, u32[]{:S(2)}, u32[]{:S(2)}) collective-permute-start(f32[163968]{0:T(1024)} %select_maximum_fusion.1), channel_id=1, source_target_pairs={{0,32},{4,36},{8,40},{12,44},{16,48},{20,52},{24,56},{28,60},{32,6... | collective-permute-start | bytes 1967624 | tf_op jit(solution)/shard_map/ppermute | solution.py:14
  307.2 5.2 %copy-start.13 = (f32[163840]{0:T(1024)S(1)}, f32[163840]{0:T(1024)}, u32[]{:S(2)}) copy-start(f32[163840]{0:T(1024)} %mul.736) | copy-start | bytes 1966084
  307.2 65.7 %all-to-all-start.3 = ((bf16[4,512,1280]{1,2,0:T(8,128)(2,1)}), bf16[4,512,1280]{1,2,0:T(8,128)(2,1)}, u32[]{:S(2)}, u32[]{:S(2)}) async-start(bf16[4,512,1280]{1,2,0:T(8,128)(2,1)} %copy.76), calls=%async_computation.3 | async-start | bytes 10485760 | tf_op jit(solution)/shard_map/all_to_all | solution.py:135
  312.4 22.4 %copy-start = (f32[163840]{0:T(1024)S(1)}, f32[163840]{0:T(1024)}, u32[]{:S(2)}) copy-start(f32[163840]{0:T(1024)} %get-tuple-element.51) | copy-start | bytes 1966084
  312.4 22.4 %copy-start.11 = (f32[163840]{0:T(1024)S(1)}, f32[163840]{0:T(1024)}, u32[]{:S(2)}) copy-start(f32[163840]{0:T(1024)} %get-tuple-element.49) | copy-start | bytes 1966084
  312.4 22.4 %copy-start.12 = (f32[163840]{0:T(1024)S(1)}, f32[163840]{0:T(1024)}, u32[]{:S(2)}) copy-start(f32[163840]{0:T(1024)} %get-tuple-element.47) | copy-start | bytes 1966084
  314.5 20.1 %collective-permute-start.5 = (f32[163968]{0:T(1024)S(1)}, f32[163968]{0:T(1024)S(1)}, u32[]{:S(2)}, u32[]{:S(2)}) collective-permute-start(f32[163968]{0:T(1024)S(1)} %select_maximum_fusion), channel_id=1, source_target_pairs={{0,64},{4,68},{8,72},{12,76},{16,80},{20,84},{24,88},{28,92},{32,9... | collective-permute-start | bytes 1967624 | tf_op jit(solution)/shard_map/ppermute | solution.py:14
  374.8 35.3 %all-to-all-start.5 = ((f32[80,64,128]{2,1,0:T(8,128)}), f32[80,64,128]{2,1,0:T(8,128)S(1)}, u32[]{:S(2)}, u32[]{:S(2)}) async-start(f32[80,64,128]{2,1,0:T(8,128)} %bitcast.66), calls=%async_computation.5 | async-start | bytes 5242880 | tf_op jit(solution)/shard_map/all_to_all | solution.py:142

commit v7 on v6

--- a/solution.py
+++ b/solution.py
@@ -56,18 +56,21 @@
 
 
 def per_device(inner_tokens, state_inputs, step_raw, conv_inner, conv_state, head_rates, skip_gain):
-    x_local, step_local = (
-        lax.all_to_all(inner_tokens, "head", split_axis=1, concat_axis=0, tiled=True),
-        lax.all_to_all(step_raw, "head", split_axis=1, concat_axis=0, tiled=True),
+    x_local = lax.all_to_all(inner_tokens, "head", split_axis=1, concat_axis=0, tiled=True)
+    groups = lax.axis_size("head")
+    rows = inner_tokens.shape[0]
+    step_chunks = step_raw.reshape(rows, groups, -1).transpose(1, 0, 2).reshape(groups * rows, -1)
+    shared = lax.all_to_all(
+        jnp.concatenate([jnp.tile(state_inputs, (groups, 1)), step_chunks], axis=1),
+        "head", split_axis=0, concat_axis=0, tiled=True,
     )
+    state_whole = shared[:, : state_inputs.shape[1]]
+    step_local = shared[:, state_inputs.shape[1] :]
     context = x_local.shape[0]
     channels = x_local.shape[1]
     heads_local = head_rates.shape[1]
     head_width = channels // heads_local
     margin_rows = KERNEL - 1
-    state_whole = lax.all_to_all(
-        jnp.tile(state_inputs, (lax.axis_size("head"), 1)), "head", split_axis=0, concat_axis=0, tiled=True
-    )
     edge_rows = jnp.concatenate(
         [x_local[context - margin_rows :], state_whole[context - margin_rows :]], axis=1
     )
@@ -138,7 +141,6 @@
     tokens = inner_tokens.shape[0]
     group = lax.axis_index("head")
     c_tokens = lax.dynamic_slice_in_dim(c_rows, group * tokens, tokens, axis=0).astype(jnp.float32)
-    groups = lax.axis_size("head")
     incoming_all = lax.all_to_all(
         jnp.tile(incoming, (groups, 1, 1)), "head", split_axis=0, concat_axis=0, tiled=True
     )

time: 445 us -> 468 us (1.052)
  other arithmetic: 53.8 us -> 70.2 us
  local copies, waits for them, and re-layouts: 95.3 us -> 111 us
  blocking collectives: 10.1 us -> 0 us
    unnamed x96 -> x100, local copies, waits for them, and re-layouts: 19.4 us -> 31 us
    convert_element_type x1, other arithmetic: 8.09 us -> 19 us  [per_device(): x_heads.astype(jnp.float32) * step_size[:, :, None]]
    all_to_all x1 -> x0, blocking collectives: 10.1 us -> none  [per_device(): lax.all_to_all(step_raw, 'head', split_axis=1, concat_axis=0, tiled=True)]
  transfers between devices with their start and end apart: 11 -> 11, of which waited for: 9 -> 9; matrix products, arithmetic and copies ran while one was open for 38% -> 43% of each run, Pallas kernels for 0% -> 0%
where the time goes in v7:
time: 468 us; the launch traced here: 459 us
  waiting for transfers between devices  179 us (38%)
  local copies, waits for them, and re-layouts  111 us (24%)
  other arithmetic  70.2 us (15%)
  matrix products  60.2 us (13%)
  starting transfers between devices  38 us (8%)
    ppermute x6, waiting for transfers between devices, from_behind(): return lax.ppermute(value, axis, pairs)  74.1 us
    all_to_all x1, waiting for transfers between devices, per_device(): lax.all_to_all(partial, 'head', split_axis=0, concat_axis=1, tiled=True)  37.9 us
    all_to_all x1, waiting for transfers between devices, per_device(): lax.all_to_all(inner_tokens, 'head', split_axis=1, concat_axis=0, tiled=T...  35.2 us
    unnamed x100, local copies, waits for them, and re-layouts  31 us
    all_to_all x1, waiting for transfers between devices, per_device(): lax.all_to_all(jnp.tile(incoming, (groups, 1, 1)), 'head', split_axis=0,...  23.5 us
    dot_general x1, matrix products, per_device(): jnp.einsum('bhts,bshp->bthp', mixing, u_blocks, preferred_element_type=jn...  20.8 us
    convert_element_type x1, other arithmetic, per_device(): x_heads.astype(jnp.float32) * step_size[:, :, None]  19 us
    ppermute x6, starting transfers between devices, from_behind(): return lax.ppermute(value, axis, pairs)  15.9 us
  transfers between devices with their start and end apart: 11, of which 9 were waited for; matrix products, arithmetic and copies ran while one was open for 43% of the time, Pallas kernels for 0%

profile of v7, /device:TPU:6, one launch (start us, length us, event | category | flops | bytes accessed | tf_op | source)
XLA Modules:
  0.0 459.4 jit_solution(5760375679582992649)
XLA Ops:
  0.0 1.1 copy.191
  1.1 0.9 reshape.342
  2.1 1.1 pad_maximum_fusion.2
  3.2 4.5 all-to-all-start.1
  7.7 7.9 %copy.188 = bf16[512,5120]{0,1:T(8,128)(2,1)} copy(bf16[512,5120]{1,0:T(8,128)(2,1)} %param.7) | data formatting | bytes 10485760 | tf_op args[0]
  15.6 8.2 %all-to-all-done.1 = bf16[4,512,276]{1,2,0:T(8,128)(2,1)S(1)} async-done(((bf16[4,512,276]{1,2,0:T(8,128)(2,1)}), bf16[4,512,276]{1,2,0:T(8,128)(2,1)S(1)}, u32[]{:S(2)}, u32[]{:S(2)}) %all-to-all-start.1) | async-done | bytes 1130528 | tf_op jit(solution)/shard_map/all_to_all | solution.py:63
  23.8 5.2 %all-to-all-start = ((bf16[512,4,1280]{0,2,1:T(8,128)(2,1)}), bf16[512,4,1280]{0,2,1:T(8,128)(2,1)}, u32[]{:S(2)}, u32[]{:S(2)}) async-start(bf16[512,4,1280]{0,2,1:T(8,128)(2,1)} %bitcast.168), calls=%async_computation | async-start | bytes 10485760 | tf_op jit(solution)/shard_map/all_to_all | solution.py:59
  33.0 4.6 %reduce-window.6 = f32[8,20,2,128]{3,1,2,0:T(8,128)S(1)} reduce-window(f32[8,20,2,128]{3,1,2,0:T(8,128)S(1)} %copy.197, f32[]{:T(128)} %constant.8.clone.1), window={size=1x1x1x128 pad=0_0x0_0x0_0x127_0}, to_apply=%region_0.1 | reduce-window | flops 5201920 | bytes 327684 | tf_op jit(solution)/shard_map/reduce-window
  39.9 1.0 mul.704
  41.0 1.0 mul.706
  42.1 1.0 mul.708
  43.2 1.0 mul.710
  44.3 1.0 mul.712
  45.5 1.0 mul.714
  46.6 1.0 mul.702
  47.7 1.0 mul.699
  48.9 1.0 mul.716
  53.1 35.2 %all-to-all-done = bf16[512,4,1280]{0,2,1:T(8,128)(2,1)} async-done(((bf16[512,4,1280]{0,2,1:T(8,128)(2,1)}), bf16[512,4,1280]{0,2,1:T(8,128)(2,1)}, u32[]{:S(2)}, u32[]{:S(2)}) %all-to-all-start) | async-done | bytes 5242912 | tf_op jit(solution)/shard_map/all_to_all | solution.py:59
  88.3 3.4 all-to-all-start.3
  91.7 7.9 %copy.189 = bf16[512,4,1280]{2,0,1:T(8,128)(2,1)} copy(bf16[512,4,1280]{0,2,1:T(8,128)(2,1)} %all-to-all-done) | data formatting | bytes 10485760 | tf_op jit(solution)/shard_map/all_to_all | solution.py:59
  100.7 4.0 collective-permute-start
  104.7 7.2 %bitcast_convert_fusion = f32[2048,1280]{1,0:T(8,128)} fusion(bf16[512,4,1280]{2,0,1:T(8,128)(2,1)} %copy.189), kind=kLoop, calls=%fused_computation.132 | loop fusion | flops 2621440 | bytes 15728640 | tf_op jit(solution)/shard_map/convert_element_type | solution.py:21
  111.9 4.0 collective-permute-done
  116.0 19.0 %fusion.23 = f32[2048,1280]{1,0:T(8,128)} fusion(f32[2048,1280]{1,0:T(8,128)} %bitcast_convert_fusion, f32[1280]{0:T(1024)S(1)} %get-tuple-element.8, f32[3,1280]{1,0:T(4,128)S(1)} %convert_element_type.65, f32[1280]{0:T(1024)S(1)} %get-tuple-element.9, f32[1280]{0:T(1024)S(1)} %get-tuple-element.6, f32[1280]{0:T(1024)S(1)} %get-tuple-element.7, ...), kind=kLoop, calls=%fused_computation.31 | loop fusion | flops 44564480 | bytes 21012480 | tf_op jit(solution)/shard_map/convert_element_type | solution.py:87
  135.0 11.3 %copy.194 = f32[2048,1280]{0,1:T(8,128)} copy(f32[2048,1280]{1,0:T(8,128)} %fusion.23) | data formatting | bytes 20971520 | tf_op jit(solution)/shard_map/convert_element_type | solution.py:87
  146.3 13.2 %copy.233 = f32[160,8,8,256]{3,2,1,0:T(8,128)} copy(f32[160,8,8,256]{3,1,2,0:T(8,128)} %bitcast.165) | data formatting | bytes 20971520
  159.6 2.2 multiply_convert_fusion.6
  162.0 11.7 %convert_multiply_fusion = (f32[8,256,20,64]{1,0,3,2:T(8,128)}, bf16[8,256,20,64]{1,0,3,2:T(8,128)(2,1)}) fusion(f32[8,256,20]{1,0,2:T(8,128)S(1)} %get-tuple-element.53, f32[8,256,20,64]{1,0,3,2:T(8,128)} %bitcast.163, f32[8,256,20]{1,0,2:T(8,128)S(1)} %copy-done.13), kind=kLoop, calls=%fused_computation.27 | loop fusion | flops 10485760 | bytes 26542080 | tf_op jit(solution)/shard_map/mul | solution.py:97
  173.7 12.8 %fusion.18 = f32[8,20,64,128]{3,2,1,0:T(8,128)S(1)} fusion(f32[8,256,20,64]{1,0,3,2:T(8,128)} %get-tuple-element.28, bf16[8,256,128,1]{1,0,2,3:T(8,128)(2,1)S(1)} %bitcast.196), kind=kOutput, calls=%fused_computation.25 | convolution fusion | flops 4026531840 | bytes 16252928 | tf_op jit(solution)/shard_map/bshp,bsn->bhpn/dot_general | solution.py:98
  186.6 1.7 multiply_add_fusion.4
  190.4 2.3 collective-permute-start.1
  196.2 12.4 %collective-permute-done.1 = f32[163968]{0:T(1024)S(1)} collective-permute-done((f32[163968]{0:T(1024)S(1)}, f32[163968]{0:T(1024)S(1)}, u32[]{:S(2)}, u32[]{:S(2)}) %collective-permute-start.1) | collective-permute-done | bytes 655904 | tf_op jit(solution)/shard_map/ppermute | solution.py:14
  208.7 1.5 add_add_fusion.1
  211.1 1.9 collective-permute-start.2
  213.1 0.9 constant_dynamic-update-slice_fusion.2
  214.3 2.0 constant_dynamic-update-slice_fusion.1
  216.3 1.7 fusion.34
  218.1 1.0 mul.727
  219.1 22.8 %collective-permute-done.2 = f32[163968]{0:T(1024)} collective-permute-done((f32[163968]{0:T(1024)}, f32[163968]{0:T(1024)}, u32[]{:S(2)}, u32[]{:S(2)}) %collective-permute-start.2) | collective-permute-done | bytes 655904 | tf_op jit(solution)/shard_map/ppermute | solution.py:14
  242.6 2.2 multiply_add_fusion.2
  245.7 5.1 %collective-permute-start.3 = (f32[163968]{0:T(1024)}, f32[163968]{0:T(1024)}, u32[]{:S(2)}, u32[]{:S(2)}) collective-permute-start(f32[163968]{0:T(1024)} %select_maximum_fusion.2), channel_id=1, source_target_pairs={{0,16},{4,20},{8,24},{12,28},{16,32},{20,36},{24,40},{28,44},{32,4... | collective-permute-start | bytes 1967624 | tf_op jit(solution)/shard_map/ppermute | solution.py:14
  250.8 2.0 constant_dynamic-update-slice_fusion
  252.8 10.6 %fusion.51 = f32[8,256,1280]{1,2,0:T(8,128)} fusion(bf16[8,256,128]{2,1,0:T(8,128)(2,1)S(1)} %bitcast.191, f32[8,1280,128]{2,1,0:T(8,128)} %constant_dynamic-update-slice_fusion), kind=kOutput, calls=%fused_computation.139 | convolution fusion | flops 4026531840 | bytes 16252928 | tf_op jit(solution)/shard_map/btn,bkn->btk/dot_general | solution.py:126
  263.5 1.0 mul.732
  264.5 16.2 %collective-permute-done.3 = f32[163968]{0:T(1024)} collective-permute-done((f32[163968]{0:T(1024)}, f32[163968]{0:T(1024)}, u32[]{:S(2)}, u32[]{:S(2)}) %collective-permute-start.3) | collective-permute-done | bytes 655904 | tf_op jit(solution)/shard_map/ppermute | solution.py:14
  281.3 2.2 multiply_add_fusion.1
  284.5 1.3 collective-permute-start.4
  285.8 20.8 %fusion.16 = bf16[8,256,20,64]{1,3,2,0:T(8,128)(2,1)S(1)} fusion(f32[8,256,20,64]{1,0,3,2:T(8,128)} %bitcast.164, f32[8,256,20,64]{1,3,2,0:T(8,128)} %bitcast.170, f32[8,20,256]{2,1,0:T(8,128)S(1)} %copy-done.17, f32[8,256,256]{2,1,0:T(8,128)} %fusion.34, pred[256,256]{1,0:T(8,128)(4,1)S(1)} %copy-done.18, bf16[8,256,20,64]{1,0,3,2:T(8,128)(2,1)} %get-tuple-element.29, ...), kind=kOutput, calls=%fused_computation.21 | convolution fusion | flops 1397227520 | bytes 33947728 | tf_op jit(solution)/shard_map/bhts,bshp->bthp/dot_general | solution.py:121
  306.6 6.0 %copy.212 = bf16[8,256,20,64]{1,0,3,2:T(8,128)(2,1)} copy(bf16[8,256,20,64]{1,3,2,0:T(8,128)(2,1)S(1)} %fusion.16) | data formatting | bytes 10485760 | tf_op jit(solution)/shard_map/convert_element_type | solution.py:136
  312.7 9.2 %all_to_all.51 = bf16[4,512,1280]{1,0,2:T(4,128)(2,1)} reshape(bf16[8,256,20,64]{1,0,3,2:T(8,128)(2,1)} %copy.212) | data formatting | bytes 10485760 | tf_op jit(solution)/shard_map/all_to_all | solution.py:138
  321.9 5.9 %copy.213 = bf16[4,512,1280]{1,2,0:T(8,128)(2,1)} copy(bf16[4,512,1280]{1,0,2:T(4,128)(2,1)} %all_to_all.51) | data formatting | bytes 10485760 | tf_op jit(solution)/shard_map/all_to_all | solution.py:138
  327.9 1.0 mul.738
  328.9 5.2 %all-to-all-start.2 = ((bf16[4,512,1280]{1,2,0:T(8,128)(2,1)}), bf16[4,512,1280]{1,2,0:T(8,128)(2,1)}, u32[]{:S(2)}, u32[]{:S(2)}) async-start(bf16[4,512,1280]{1,2,0:T(8,128)(2,1)} %copy.213), calls=%async_computation.2 | async-start | bytes 10485760 | tf_op jit(solution)/shard_map/all_to_all | solution.py:138
  334.1 1.3 multiply_add_fusion
  336.2 1.3 collective-permute-start.5
  337.5 18.8 %collective-permute-done.5 = f32[163968]{0:T(1024)S(1)} collective-permute-done((f32[163968]{0:T(1024)S(1)}, f32[163968]{0:T(1024)S(1)}, u32[]{:S(2)}, u32[]{:S(2)}) %collective-permute-start.5) | collective-permute-done | bytes 655904 | tf_op jit(solution)/shard_map/ppermute | solution.py:14
  356.7 37.9 %all-to-all-done.2 = bf16[4,512,1280]{1,2,0:T(8,128)(2,1)} async-done(((bf16[4,512,1280]{1,2,0:T(8,128)(2,1)}), bf16[4,512,1280]{1,2,0:T(8,128)(2,1)}, u32[]{:S(2)}, u32[]{:S(2)}) %all-to-all-start.2) | async-done | bytes 5242912 | tf_op jit(solution)/shard_map/all_to_all | solution.py:138
  394.6 1.8 tile.7
  396.5 3.8 all-to-all-start.4
  400.3 8.0 %convert_element_type.84 = f32[4,512,1280]{1,2,0:T(8,128)} convert(bf16[4,512,1280]{1,2,0:T(8,128)(2,1)} %all-to-all-done.2) | non-fusion elementwise | flops 2621440 | bytes 15728640 | tf_op jit(solution)/shard_map/convert_element_type | solution.py:153
  408.3 23.5 %all-to-all-done.4 = f32[80,64,128]{2,1,0:T(8,128)S(1)} async-done(((f32[80,64,128]{2,1,0:T(8,128)}), f32[80,64,128]{2,1,0:T(8,128)S(1)}, u32[]{:S(2)}, u32[]{:S(2)}) %all-to-all-start.4) | async-done | bytes 2621472 | tf_op jit(solution)/shard_map/all_to_all | solution.py:144
  431.8 14.2 %fusion.17 = bf16[512,80,64]{0,1,2:T(8,128)(2,1)S(1)} fusion(f32[512,80,64]{0,2,1:T(8,128)} %bitcast.166, f32[512,80]{0,1:T(8,128)S(1)} %mul.664, f32[80,64,128]{2,1,0:T(8,128)S(1)} %all-to-all-done.4, bf16[2048,128]{0,1:T(8,128)(2,1)S(1)} %get-tuple-element.41, s32[]{:T(128)S(6)} %select_n.13), kind=kOutput, calls=%fused_computation.23 | convolution fusion | flops 4034396160 | bytes 18644996 | tf_op jit(solution)/shard_map/tn,kn->tk/dot_general | solution.py:147
  446.0 5.3 %copy.219 = bf16[512,80,64]{0,2,1:T(8,128)(2,1)} copy(bf16[512,80,64]{0,1,2:T(8,128)(2,1)S(1)} %fusion.17) | data formatting | bytes 10485760 | tf_op jit(solution)/shard_map/convert_element_type | solution.py:156
  451.3 7.9 %copy.220 = bf16[512,5120]{1,0:T(8,128)(2,1)} copy(bf16[512,5120]{0,1:T(8,128)(2,1)} %bitcast.169) | data formatting | bytes 10485760 | tf_op jit(solution)/shard_map/reshape | solution.py:156
  (173 shorter events, 23.1 us)
Async XLA Ops:
  3.2 20.6 %all-to-all-start.1 = ((bf16[4,512,276]{1,2,0:T(8,128)(2,1)}), bf16[4,512,276]{1,2,0:T(8,128)(2,1)S(1)}, u32[]{:S(2)}, u32[]{:S(2)}) async-start(bf16[4,512,276]{1,2,0:T(8,128)(2,1)} %pad_maximum_fusion.2), calls=%async_computation.1 | async-start | bytes 2293760 | tf_op jit(solution)/shard_map/all_to_all | solution.py:63
  23.8 5.9 %copy-start.19 = (f32[5,1280]{1,0:T(8,128)S(1)}, f32[5,1280]{1,0:T(8,128)}, u32[]{:S(2)}) copy-start(f32[5,1280]{1,0:T(8,128)} %param.10) | copy-start | bytes 76804
  23.8 6.0 %copy-start.40 = (f32[2,20]{1,0:T(2,128)S(1)}, f32[2,20]{1,0:T(2,128)}, u32[]{:S(2)}) copy-start(f32[2,20]{1,0:T(2,128)} %param.12) | copy-start | bytes 484
  23.8 6.0 %copy-start.39 = (f32[5,256]{1,0:T(8,128)S(1)}, f32[5,256]{1,0:T(8,128)}, u32[]{:S(2)}) copy-start(f32[5,256]{1,0:T(8,128)} %param.11) | copy-start | bytes 15364
  23.8 64.5 %all-to-all-start = ((bf16[512,4,1280]{0,2,1:T(8,128)(2,1)}), bf16[512,4,1280]{0,2,1:T(8,128)(2,1)}, u32[]{:S(2)}, u32[]{:S(2)}) async-start(bf16[512,4,1280]{0,2,1:T(8,128)(2,1)} %bitcast.168), calls=%async_computation | async-start | bytes 10485760 | tf_op jit(solution)/shard_map/all_to_all | solution.py:59
  39.5 5.8 %copy-start.20 = (f32[20]{0:T(128)}, f32[20]{0:T(128)S(1)}, u32[]{:S(2)}) copy-start(f32[20]{0:T(128)S(1)} %get-tuple-element.66) | copy-start | bytes 244
  39.5 5.8 %copy-start.22 = (f32[20]{0:T(128)}, f32[20]{0:T(128)S(1)}, u32[]{:S(2)}) copy-start(f32[20]{0:T(128)S(1)} %get-tuple-element.67) | copy-start | bytes 244
  39.5 5.8 %copy-start.24 = (f32[20]{0:T(128)}, f32[20]{0:T(128)S(1)}, u32[]{:S(2)}) copy-start(f32[20]{0:T(128)S(1)} %get-tuple-element.68) | copy-start | bytes 244
  39.5 5.8 %copy-start.26 = (f32[20]{0:T(128)}, f32[20]{0:T(128)S(1)}, u32[]{:S(2)}) copy-start(f32[20]{0:T(128)S(1)} %get-tuple-element.62) | copy-start | bytes 244
  39.5 6.9 %copy-start.32 = (f32[20]{0:T(128)}, f32[20]{0:T(128)S(1)}, u32[]{:S(2)}) copy-start(f32[20]{0:T(128)S(1)} %get-tuple-element.59) | copy-start | bytes 244
  47.6 40.7 %copy-start.28 = (f32[20]{0:T(128)}, f32[20]{0:T(128)S(1)}, u32[]{:S(2)}) copy-start(f32[20]{0:T(128)S(1)} %get-tuple-element.61) | copy-start | bytes 244
  47.6 40.7 %copy-start.30 = (f32[20]{0:T(128)}, f32[20]{0:T(128)S(1)}, u32[]{:S(2)}) copy-start(f32[20]{0:T(128)S(1)} %get-tuple-element.60) | copy-start | bytes 244
  88.3 240.6 %all-to-all-start.3 = ((f32[4,512,20]{1,2,0:T(8,128)}), f32[4,512,20]{1,2,0:T(8,128)S(1)}, u32[]{:S(2)}, u32[]{:S(2)}) async-start(f32[4,512,20]{1,2,0:T(8,128)} %copy.215), calls=%async_computation.3 | async-start | bytes 393216 | tf_op jit(solution)/shard_map/all_to_all | solution.py:139
  91.7 8.9 %copy-start.15 = (bf16[3,256]{0,1:T(8,128)(2,1)S(1)}, bf16[3,256]{0,1:T(8,128)(2,1)}, u32[]{:S(2)}) copy-start(bf16[3,256]{0,1:T(8,128)(2,1)} %slice.226) | copy-start | bytes 4612
  100.7 15.1 %collective-permute-start = (bf16[3,1536]{0,1:T(8,128)(2,1)S(1)}, bf16[3,1536]{0,1:T(8,128)(2,1)S(1)}, u32[]{:S(2)}, u32[]{:S(2)}) collective-permute-start(bf16[3,1536]{0,1:T(8,128)(2,1)S(1)} %pad_maximum_fusion.3), channel_id=1, source_target_pairs={{0,4},{4,8},{8,12},{12,16},{16,20},{20,24},{24,28},{28,32},{32,36}... | collective-permute-start | bytes 27656 | tf_op jit(solution)/shard_map/ppermute | solution.py:14
  146.3 13.2 %copy-start.34 = (f32[1,256]{1,0:T(1,128)S(1)}, f32[1,256]{1,0:T(1,128)}, u32[]{:S(2)}) copy-start(f32[1,256]{1,0:T(1,128)} %get-tuple-element.54) | copy-start | bytes 3076
  146.3 13.2 %copy-start.35 = (f32[1,256]{1,0:T(1,128)S(1)}, f32[1,256]{1,0:T(1,128)}, u32[]{:S(2)}) copy-start(f32[1,256]{1,0:T(1,128)} %get-tuple-element.55) | copy-start | bytes 3076
  146.3 13.2 %copy-start.36 = (f32[1,256]{1,0:T(1,128)S(1)}, f32[1,256]{1,0:T(1,128)}, u32[]{:S(2)}) copy-start(f32[1,256]{1,0:T(1,128)} %get-tuple-element.56) | copy-start | bytes 3076
  146.3 13.3 %copy-start.37 = (f32[1,256]{1,0:T(1,128)S(1)}, f32[1,256]{1,0:T(1,128)}, u32[]{:S(2)}) copy-start(f32[1,256]{1,0:T(1,128)} %get-tuple-element.57) | copy-start | bytes 3076
  146.3 13.3 %copy-start.38 = (f32[1,256]{1,0:T(1,128)S(1)}, f32[1,256]{1,0:T(1,128)}, u32[]{:S(2)}) copy-start(f32[1,256]{1,0:T(1,128)} %get-tuple-element.58) | copy-start | bytes 3076
  159.5 2.5 copy-start.13
  173.7 12.8 %copy-start.21 = (f32[20]{0:T(128)S(1)}, f32[20]{0:T(128)}, u32[]{:S(2)}) copy-start(f32[20]{0:T(128)} %copy-done.20) | copy-start | bytes 244
  173.7 12.8 %copy-start.23 = (f32[20]{0:T(128)S(1)}, f32[20]{0:T(128)}, u32[]{:S(2)}) copy-start(f32[20]{0:T(128)} %copy-done.22) | copy-start | bytes 244
  173.7 12.8 %copy-start.25 = (f32[20]{0:T(128)S(1)}, f32[20]{0:T(128)}, u32[]{:S(2)}) copy-start(f32[20]{0:T(128)} %copy-done.24) | copy-start | bytes 244
  173.7 12.9 %copy-start.27 = (f32[20]{0:T(128)S(1)}, f32[20]{0:T(128)}, u32[]{:S(2)}) copy-start(f32[20]{0:T(128)} %copy-done.26) | copy-start | bytes 244
  173.7 12.9 %copy-start.29 = (f32[20]{0:T(128)S(1)}, f32[20]{0:T(128)}, u32[]{:S(2)}) copy-start(f32[20]{0:T(128)} %copy-done.28) | copy-start | bytes 244
  188.3 0.9 copy-start.33
  189.4 0.8 copy-start.31
  190.2 18.4 %copy-start.1 = (f32[163840]{0:T(1024)S(1)}, f32[163840]{0:T(1024)}, u32[]{:S(2)}) copy-start(f32[163840]{0:T(1024)} %mul.704) | copy-start | bytes 1966084
  190.2 18.4 %copy-start.2 = (f32[163840]{0:T(1024)S(1)}, f32[163840]{0:T(1024)}, u32[]{:S(2)}) copy-start(f32[163840]{0:T(1024)} %mul.706) | copy-start | bytes 1966084
  190.2 18.4 %copy-start.3 = (f32[163840]{0:T(1024)S(1)}, f32[163840]{0:T(1024)}, u32[]{:S(2)}) copy-start(f32[163840]{0:T(1024)} %mul.708) | copy-start | bytes 1966084
  190.2 18.4 %copy-start.4 = (f32[163840]{0:T(1024)S(1)}, f32[163840]{0:T(1024)}, u32[]{:S(2)}) copy-start(f32[163840]{0:T(1024)} %mul.710) | copy-start | bytes 1966084
  190.3 18.4 %copy-start.5 = (f32[163840]{0:T(1024)S(1)}, f32[163840]{0:T(1024)}, u32[]{:S(2)}) copy-start(f32[163840]{0:T(1024)} %mul.712) | copy-start | bytes 1966084
  190.3 18.4 %copy-start.6 = (f32[163840]{0:T(1024)S(1)}, f32[163840]{0:T(1024)}, u32[]{:S(2)}) copy-start(f32[163840]{0:T(1024)} %mul.714) | copy-start | bytes 1966084
  190.3 18.4 %copy-start.7 = (f32[163840]{0:T(1024)S(1)}, f32[163840]{0:T(1024)}, u32[]{:S(2)}) copy-start(f32[163840]{0:T(1024)} %mul.702) | copy-start | bytes 1966084
  190.3 18.4 %copy-start.8 = (f32[163840]{0:T(1024)S(1)}, f32[163840]{0:T(1024)}, u32[]{:S(2)}) copy-start(f32[163840]{0:T(1024)} %mul.699) | copy-start | bytes 1966084
  190.3 18.4 %copy-start.9 = (f32[163840]{0:T(1024)S(1)}, f32[163840]{0:T(1024)}, u32[]{:S(2)}) copy-start(f32[163840]{0:T(1024)} %mul.716) | copy-start | bytes 1966084
  190.4 18.3 %collective-permute-start.1 = (f32[163968]{0:T(1024)S(1)}, f32[163968]{0:T(1024)S(1)}, u32[]{:S(2)}, u32[]{:S(2)}) collective-permute-start(f32[163968]{0:T(1024)S(1)} %select_maximum_fusion.4), channel_id=1, source_target_pairs={{0,4},{4,8},{8,12},{12,16},{16,20},{20,24},{24,28},{28,32},{32,36}... | collective-permute-start | bytes 1967624 | tf_op jit(solution)/shard_map/ppermute | solution.py:14
  208.6 1.6 copy-start.14
  211.1 30.8 %collective-permute-start.2 = (f32[163968]{0:T(1024)}, f32[163968]{0:T(1024)}, u32[]{:S(2)}, u32[]{:S(2)}) collective-permute-start(f32[163968]{0:T(1024)} %select_maximum_fusion.3), channel_id=1, source_target_pairs={{0,8},{4,12},{8,16},{12,20},{16,24},{20,28},{24,32},{28,36},{32,40... | collective-permute-start | bytes 1967624 | tf_op jit(solution)/shard_map/ppermute | solution.py:14
  245.7 34.9 %collective-permute-start.3 = (f32[163968]{0:T(1024)}, f32[163968]{0:T(1024)}, u32[]{:S(2)}, u32[]{:S(2)}) collective-permute-start(f32[163968]{0:T(1024)} %select_maximum_fusion.2), channel_id=1, source_target_pairs={{0,16},{4,20},{8,24},{12,28},{16,32},{20,36},{24,40},{28,44},{32,4... | collective-permute-start | bytes 1967624 | tf_op jit(solution)/shard_map/ppermute | solution.py:14
  263.4 22.4 %copy-start.16 = (f32[8,256,20]{1,2,0:T(8,128)S(1)}, f32[8,256,20]{1,2,0:T(8,128)}, u32[]{:S(2)}) copy-start(f32[8,256,20]{1,2,0:T(8,128)} %copy.204) | copy-start | bytes 491524
  263.4 22.4 %copy-start.17 = (f32[8,20,256]{2,1,0:T(8,128)S(1)}, f32[8,20,256]{2,1,0:T(8,128)}, u32[]{:S(2)}) copy-start(f32[8,20,256]{2,1,0:T(8,128)} %copy.201) | copy-start | bytes 491524
  263.4 22.4 %copy-start.18 = (pred[256,256]{1,0:T(8,128)(4,1)S(1)}, pred[256,256]{1,0:T(8,128)(4,1)}, u32[]{:S(2)}) copy-start(pred[256,256]{1,0:T(8,128)(4,1)} %iota_compare_fusion.1) | copy-start | bytes 196612
  263.4 22.4 %copy-start.41 = (f32[20]{0:T(128)S(1)}, f32[20]{0:T(128)}, u32[]{:S(2)}) copy-start(f32[20]{0:T(128)} %param.13) | copy-start | bytes 244
  284.5 49.7 %collective-permute-start.4 = (f32[163968]{0:T(1024)}, f32[163968]{0:T(1024)}, u32[]{:S(2)}, u32[]{:S(2)}) collective-permute-start(f32[163968]{0:T(1024)} %select_maximum_fusion.1), channel_id=1, source_target_pairs={{0,32},{4,36},{8,40},{12,44},{16,48},{20,52},{24,56},{28,60},{32,6... | collective-permute-start | bytes 1967624 | tf_op jit(solution)/shard_map/ppermute | solution.py:14
  328.9 5.3 %copy-start.12 = (f32[163840]{0:T(1024)S(1)}, f32[163840]{0:T(1024)}, u32[]{:S(2)}) copy-start(f32[163840]{0:T(1024)} %mul.738) | copy-start | bytes 1966084
  328.9 65.8 %all-to-all-start.2 = ((bf16[4,512,1280]{1,2,0:T(8,128)(2,1)}), bf16[4,512,1280]{1,2,0:T(8,128)(2,1)}, u32[]{:S(2)}, u32[]{:S(2)}) async-start(bf16[4,512,1280]{1,2,0:T(8,128)(2,1)} %copy.213), calls=%async_computation.2 | async-start | bytes 10485760 | tf_op jit(solution)/shard_map/all_to_all | solution.py:138
  334.1 22.3 %copy-start = (f32[163840]{0:T(1024)S(1)}, f32[163840]{0:T(1024)}, u32[]{:S(2)}) copy-start(f32[163840]{0:T(1024)} %get-tuple-element.51) | copy-start | bytes 1966084
  334.1 22.3 %copy-start.10 = (f32[163840]{0:T(1024)S(1)}, f32[163840]{0:T(1024)}, u32[]{:S(2)}) copy-start(f32[163840]{0:T(1024)} %get-tuple-element.49) | copy-start | bytes 1966084
  334.1 22.3 %copy-start.11 = (f32[163840]{0:T(1024)S(1)}, f32[163840]{0:T(1024)}, u32[]{:S(2)}) copy-start(f32[163840]{0:T(1024)} %get-tuple-element.47) | copy-start | bytes 1966084
  336.2 20.1 %collective-permute-start.5 = (f32[163968]{0:T(1024)S(1)}, f32[163968]{0:T(1024)S(1)}, u32[]{:S(2)}, u32[]{:S(2)}) collective-permute-start(f32[163968]{0:T(1024)S(1)} %select_maximum_fusion), channel_id=1, source_target_pairs={{0,64},{4,68},{8,72},{12,76},{16,80},{20,84},{24,88},{28,92},{32,9... | collective-permute-start | bytes 1967624 | tf_op jit(solution)/shard_map/ppermute | solution.py:14
  396.5 35.3 %all-to-all-start.4 = ((f32[80,64,128]{2,1,0:T(8,128)}), f32[80,64,128]{2,1,0:T(8,128)S(1)}, u32[]{:S(2)}, u32[]{:S(2)}) async-start(f32[80,64,128]{2,1,0:T(8,128)} %bitcast.63), calls=%async_computation.4 | async-start | bytes 5242880 | tf_op jit(solution)/shard_map/all_to_all | solution.py:144
